TPU v7x, 128 devices: a whole 4x4x4 slice. The times are simulated.
128 devices in a mesh: leaf: 128 (over z, x, y, core).
Axes of the slice: x: 4, y: 4, z: 4, core: 2. Of those that a mesh axis runs over, the one named last changes fastest.
Arguments:
- charges: bfloat16 [8192, 16, 128], P('leaf'), may hold values from -6 to 6
- leaf_basis: bfloat16 [8192, 64, 128], P('leaf'), may hold values from -0.5 to 0.5
- leaf_up: float32 [8192, 64, 64], P('leaf'), may hold values from -0.75 to 0.75
- top_up: float32 [7, 2, 64, 64], replicated, may hold values from -0.5 to 0.5
- top_coupling: float32 [7, 2, 64, 64], replicated, may hold values from -0.75 to 0.75
- near_blocks: bfloat16 [8192, 8, 128, 128], P('leaf'), may hold values from -0.5 to 0.5
- near_list: int32 [8192, 8], P('leaf'), may hold values from 0 to 8191, as said below
- coupling_blocks: bfloat16 [131072, 64, 64], P('leaf'), may hold values from -0.75 to 0.75
- coup_source: int32 [131072], P('leaf'), may hold values from 0 to 63
- coup_device: int32 [131072, 1], P('leaf'), may hold values from 0 to 127; in each aligned block of 1024 rows (0 to 1023, 1024 to 2047, ...) at most 12 rows name the same one
- coup_box: int32 [131072], P('leaf'), may hold values from 0 to 63
Outputs:
- potential: float32 [8192, 16, 128], P('leaf')
Inputs may be any that keep to these rules, and one draw needn't show every extreme that they name: near_list[b, 0] = b, and every entry lies within 64 of b. `coup_device`: the interactions held by one device name each target device at most 12 times.
All inputs are finite; a program needn't handle non-finite values.
Results may differ from a plain program's by a relative error of at most 0.003.
Values may be sent and summed in bfloat16 or wider, within the bound.
No kernel may reach another device: no remote copies, remote signals or barrier semaphores. Data moves between devices by JAX's collectives and lax.ppermute only.
A program may use at most 192 MiB of HBM per device.

v0:
```python
import jax
import jax.numpy as jnp
from jax import lax
from jax.sharding import PartitionSpec as P


def padded_2(value, sides, width):
    for axis, dim in sides:
        peers, length = (lax.axis_size(axis), value.shape[dim])
        up = [(i, (i + 1) % peers) for i in range(peers - 1)]
        down = [(j, i) for i, j in up]
        last = lax.slice_in_dim(value, length - width, length, axis=dim)
        initial = lax.slice_in_dim(value, 0, width, axis=dim)
        before = lax.ppermute(last, axis, up)
        after = lax.ppermute(initial, axis, down)
        value = jnp.concatenate([before, value, after], axis=dim)
    return value


def partner_2(value, axis, stride):
    return lax.ppermute(value, axis, [(i, i ^ 1 << stride) for i in range(lax.axis_size(axis))])


def body(
    charges,
    leaf_basis,
    leaf_up,
    top_up,
    top_coupling,
    near_blocks,
    near_list,
    coupling_blocks,
    coup_source,
    coup_device,
    coup_box,
):
    highest = lax.Precision.HIGHEST
    device_pos = lax.axis_index("leaf")
    devices = lax.axis_size("leaf")
    levels = devices.bit_length() - 1
    leaf_count = charges.shape[0]
    ranks = leaf_basis.shape[1]
    sides_rhs = charges.shape[1]
    panels = charges.shape[2]
    near_count = near_list.shape[1]
    entries = coup_source.shape[0]
    capacity = entries // devices + entries // (2 * devices)
    flat_width = sides_rhs * ranks
    skeleton = jnp.einsum("bkp,brp->brk", leaf_basis, charges, preferred_element_type=jnp.float32)
    skeleton_low = skeleton.astype(jnp.bfloat16)
    own_box = jnp.einsum("brj,bjk->brk", skeleton, leaf_up, precision=highest).sum(axis=0)
    target_dev = coup_device[:, 0]
    onehot_dev = (target_dev[:, None] == jnp.arange(devices, dtype=jnp.int32)[None, :]).astype(
        jnp.int32
    )
    slot_pos = jnp.sum((jnp.cumsum(onehot_dev, axis=0) - onehot_dev) * onehot_dev, axis=1)
    slot_flat = target_dev * capacity + slot_pos
    box_buffer = jnp.full((devices, capacity), -1, jnp.int32).at[target_dev, slot_pos].set(coup_box)
    slot_table = (
        jnp.arange(devices * capacity, dtype=jnp.int32)[:, None] == slot_flat[None, :]
    ).astype(jnp.bfloat16)
    picked = skeleton_low[coup_source].reshape(entries, flat_width)
    products = jnp.einsum(
        "crj,cjk->crk",
        picked.reshape(entries, sides_rhs, ranks),
        coupling_blocks,
        preferred_element_type=jnp.float32,
    ).astype(jnp.bfloat16)
    send_values = jnp.dot(
        slot_table, products.reshape(entries, flat_width), preferred_element_type=jnp.float32
    ).astype(jnp.bfloat16)
    send_values = send_values.reshape(devices, capacity, flat_width)
    received, recv_boxes = (
        lax.all_to_all(send_values, "leaf", split_axis=0, concat_axis=0, tiled=True),
        lax.all_to_all(box_buffer, "leaf", split_axis=0, concat_axis=0, tiled=True),
    )
    scatter_table = (
        recv_boxes.reshape(1, devices * capacity)
        == jnp.arange(leaf_count, dtype=jnp.int32)[:, None]
    ).astype(jnp.bfloat16)
    far = jnp.dot(
        scatter_table,
        received.reshape(devices * capacity, flat_width),
        preferred_element_type=jnp.float32,
    )
    far = far.reshape(leaf_count, sides_rhs, ranks)
    padded = padded_2(charges, (("leaf", 0),), leaf_count)
    local_rows = near_list - (device_pos * leaf_count - leaf_count)
    gathered = padded[local_rows]
    gathered = jnp.transpose(gathered, (0, 2, 1, 3)).reshape(
        leaf_count, sides_rhs, near_count * panels
    )
    nearfield = jnp.einsum(
        "brm,bmp->brp",
        gathered,
        near_blocks.reshape(leaf_count, near_count * panels, panels),
        preferred_element_type=jnp.float32,
    )
    upward = own_box
    stored = []
    for level in range(levels):
        partner = partner_2(upward, "leaf", level)
        node_side = device_pos >> level & 1
        stored.append(jnp.dot(partner, top_coupling[level][node_side], precision=highest))
        left_node = jnp.where(node_side == 0, upward, partner)
        right_node = jnp.where(node_side == 0, partner, upward)
        upward = jnp.dot(left_node, top_up[level, 0], precision=highest) + jnp.dot(
            right_node, top_up[level, 1], precision=highest
        )
    local_exp = jnp.zeros_like(upward)
    for level in reversed(range(levels)):
        node_side = device_pos >> level & 1
        local_exp = (
            jnp.dot(local_exp, top_up[level][node_side].T, precision=highest) + stored[level]
        )
    leaf_local = (jnp.einsum("rk,bjk->brj", local_exp, leaf_up, precision=highest) + far).astype(
        jnp.bfloat16
    )
    farfield = jnp.einsum(
        "brk,bkp->brp", leaf_local, leaf_basis, preferred_element_type=jnp.float32
    )
    return farfield + nearfield


def solution(mesh):
    return jax.shard_map(
        body,
        mesh=mesh,
        in_specs=(
            P("leaf", None, None),
            P("leaf", None, None),
            P("leaf", None, None),
            P(),
            P(),
            P("leaf", None, None, None),
            P("leaf", None),
            P("leaf", None, None),
            P("leaf"),
            P("leaf", None),
            P("leaf"),
        ),
        out_specs=P("leaf", None, None),
        check_vma=False,
    )
```

profile of v0, /device:TPU:28, one launch (start us, length us, event | category | flops | bytes accessed | tf_op | source)
XLA Modules:
  0.0 212.1 jit_solution(4208158184005081645)
XLA Ops:
  0.0 2.2 %collective-permute-start.8 = (bf16[64,16,128]{2,1,0:T(8,128)(2,1)}, bf16[64,16,128]{2,1,0:T(8,128)(2,1)S(1)}, u32[]{:S(2)}, u32[]{:S(2)}) collective-permute-start(bf16[64,16,128]{2,1,0:T(8,128)(2,1)} %param.11), channel_id=1, source_target_pairs={{1,0},{2,1},{3,2},{4,3},{5,4},{6,5},{7,6},{8,7},{9,8},{10,9},{11,1... | collective-permute-start | bytes 786440 | tf_op jit(solution)/shard_map/ppermute | solution.py:15
  2.2 2.2 %collective-permute-start.7 = (bf16[64,16,128]{2,1,0:T(8,128)(2,1)}, bf16[64,16,128]{2,1,0:T(8,128)(2,1)}, u32[]{:S(2)}, u32[]{:S(2)}) collective-permute-start(bf16[64,16,128]{2,1,0:T(8,128)(2,1)} %param.11), channel_id=1, source_target_pairs={{0,1},{1,2},{2,3},{3,4},{4,5},{5,6},{6,7},{7,8},{8,9},{9,10},{10,1... | collective-permute-start | bytes 786440 | tf_op jit(solution)/shard_map/ppermute | solution.py:14
  4.5 2.0 fusion.131
  6.5 1.2 convolution_bitcast_fusion.1
  7.7 3.3 %collective-permute-start = (f32[16,64]{1,0:T(8,128)S(1)}, f32[16,64]{1,0:T(8,128)S(1)}, u32[]{:S(2)}, u32[]{:S(2)}) collective-permute-start(f32[16,64]{1,0:T(8,128)S(1)} %convolution_bitcast_fusion.1), channel_id=1, source_target_pairs={{0,1},{1,0},{2,3},{3,2},{4,5},{5,4},{6,7},{7,6},{8,9},{9,8},{10,11... | collective-permute-start | bytes 12296 | tf_op jit(solution)/shard_map/ppermute | solution.py:21
  12.0 4.5 %scatter_custom_fusion = s32[1536]{0:T(1024)S(1)} fusion(s32[1024]{0:T(1024)S(1)} %broadcast_select_fusion, s32[1024]{0:T(1024)} %param.21, s32[]{:T(128)} %constant.48.clone.1), kind=kCustom, calls=%fused_computation.131 | custom fusion | bytes 6656
  17.3 11.7 %all-to-all-start = ((s32[128,1,12]{2,1,0:T(1,128)}), s32[128,1,12]{2,1,0:T(1,128)S(1)}, u32[]{:S(2)}, u32[]{:S(2)}) async-start(s32[128,1,12]{2,1,0:T(1,128)} %copy.37), calls=%async_computation | async-start | bytes 131072 | tf_op jit(solution)/shard_map/all_to_all | solution.py:75
  29.0 24.0 %copy.38 = bf16[1024,64,64]{2,1,0:T(8,128)(2,1)} copy(bf16[1024,64,64]{0,2,1:T(8,128)(2,1)} %param.18) | data formatting | bytes 16777216 | tf_op args[7]
  53.0 8.4 %gather_fusion = bf16[1024,16,64]{2,1,0:T(8,128)(2,1)} fusion(bf16[64,16,64]{2,1,0:T(8,128)(2,1)S(1)} %get-tuple-element.19, s32[1024]{0:T(1024)S(1)} %fusion.98), kind=kCustom, calls=%fused_computation | custom fusion | bytes 4198400 | tf_op jit(solution)/shard_map/gather | solution.py:62
  61.4 10.6 %convolution_convert_fusion = bf16[1024,16,64]{2,1,0:T(8,128)(2,1)} fusion(bf16[1024,16,64]{2,1,0:T(8,128)(2,1)} %gather_fusion, bf16[1024,64,64]{2,1,0:T(8,128)(2,1)} %copy.38), kind=kOutput, calls=%fused_computation.7 | convolution fusion | flops 135266304 | bytes 12582912 | tf_op jit(solution)/shard_map/crj,cjk->crk/dot_general | solution.py:63
  72.1 5.6 %copy.39 = bf16[1024,16,64]{0,2,1:T(8,128)(2,1)} copy(bf16[1024,16,64]{2,1,0:T(8,128)(2,1)} %convolution_convert_fusion) | data formatting | bytes 4194304 | tf_op jit(solution)/shard_map/convert_element_type | solution.py:68
  78.7 6.5 %fusion.1 = bf16[1536,1024]{1,0:T(8,128)(2,1)} fusion(bf16[1024,1024]{0,1:T(8,128)(2,1)} %bitcast.152, s32[1024]{0:T(1024)S(1)} %multiply_add_fusion), kind=kOutput, calls=%fused_computation.5 | convolution fusion | flops 3224371200 | bytes 5246976 | tf_op jit(solution)/shard_map/dot_general | solution.py:69
  85.5 1.2 collective-permute-start.2
  87.4 3.3 %collective-permute-done.2 = f32[16,64]{1,0:T(8,128)S(1)} collective-permute-done((f32[16,64]{1,0:T(8,128)S(1)}, f32[16,64]{1,0:T(8,128)S(1)}, u32[]{:S(2)}, u32[]{:S(2)}) %collective-permute-start.2) | collective-permute-done | bytes 4128 | tf_op jit(solution)/shard_map/ppermute | solution.py:21
  91.3 1.2 collective-permute-start.3
  93.3 1.6 collective-permute-done.3
  95.9 4.6 %collective-permute-done.4 = f32[16,64]{1,0:T(8,128)S(1)} collective-permute-done((f32[16,64]{1,0:T(8,128)S(1)}, f32[16,64]{1,0:T(8,128)S(1)}, u32[]{:S(2)}, u32[]{:S(2)}) %collective-permute-start.4) | collective-permute-done | bytes 4128 | tf_op jit(solution)/shard_map/ppermute | solution.py:21
  100.8 1.8 collective-permute-start.5
  103.4 6.0 %reshape.89 = bf16[128,12,1024]{2,1,0:T(8,128)(2,1)} reshape(bf16[1536,1024]{1,0:T(8,128)(2,1)} %fusion.1) | data formatting | bytes 6291456 | tf_op jit(solution)/shard_map/reshape | solution.py:72
  111.0 10.4 %all-to-all-start.1 = ((bf16[128,12,1024]{2,1,0:T(8,128)(2,1)}), bf16[128,12,1024]{2,1,0:T(8,128)(2,1)}, u32[]{:S(2)}, u32[]{:S(2)}) async-start(bf16[128,12,1024]{2,1,0:T(8,128)(2,1)} %reshape.89), calls=%async_computation.1 | async-start | bytes 8388608 | tf_op jit(solution)/shard_map/all_to_all | solution.py:74
  121.4 1.5 convolution_add_fusion.7
  122.9 3.5 %collective-permute-start.6 = (f32[16,64]{1,0:T(8,128)}, f32[16,64]{1,0:T(8,128)S(1)}, u32[]{:S(2)}, u32[]{:S(2)}) collective-permute-start(f32[16,64]{1,0:T(8,128)} %convolution_add_fusion.7), channel_id=1, source_target_pairs={{0,64},{1,65},{2,66},{3,67},{4,68},{5,69},{6,70},{7,71},{8,72},{9,... | collective-permute-start | bytes 12296 | tf_op jit(solution)/shard_map/ppermute | solution.py:21
  127.8 41.9 %collective-permute-done.6 = f32[16,64]{1,0:T(8,128)S(1)} collective-permute-done((f32[16,64]{1,0:T(8,128)}, f32[16,64]{1,0:T(8,128)S(1)}, u32[]{:S(2)}, u32[]{:S(2)}) %collective-permute-start.6) | collective-permute-done | bytes 4128 | tf_op jit(solution)/shard_map/ppermute | solution.py:21
  170.6 0.9 fusion.37
  172.4 0.9 fusion.34
  180.6 1.0 pad_maximum_fusion
  181.6 2.8 %gather_fusion.1 = bf16[512,16,128]{2,1,0:T(8,128)(2,1)} fusion(bf16[192,16,128]{2,1,0:T(8,128)(2,1)S(1)} %pad_maximum_fusion, s32[1024]{0:T(1024)S(1)} %pad_clamp_fusion), kind=kCustom, calls=%fused_computation.1 | custom fusion | bytes 4196352 | tf_op jit(solution)/shard_map/gather | solution.py:89
  184.4 6.1 %reshape.90 = bf16[1536,1024]{1,0:T(8,128)(2,1)} reshape(bf16[128,12,1024]{2,1,0:T(8,128)(2,1)} %all-to-all-done.1) | data formatting | bytes 6291456 | tf_op jit(solution)/shard_map/reshape | solution.py:83
  190.6 4.7 %copy.40 = bf16[1024,1536]{1,0:T(8,128)(2,1)} copy(bf16[1024,1536]{0,1:T(8,128)(2,1)} %bitcast.150) | data formatting | bytes 6291456 | tf_op jit(solution)/shard_map/dot_general | solution.py:81
  195.3 3.6 %fusion.17 = f32[64,16,64]{2,0,1:T(8,128)S(1)} fusion(bf16[16,64,1536]{2,1,0:T(8,128)(2,1)} %bitcast.151, s32[1536]{0:T(1024)S(1)} %eq.91), kind=kOutput, calls=%fused_computation.40 | convolution fusion | flops 201424896 | bytes 3414016 | tf_op jit(solution)/shard_map/dot_general | solution.py:81
  198.8 5.0 %fusion.10 = bf16[64,16,64]{2,1,0:T(8,128)(2,1)S(1)} fusion(f32[16,64,1]{1,0,2:T(8,128)S(1)} %fusion.11, f32[64,64,64]{2,1,0:T(8,128)S(1)} %copy-done, f32[64,16,64]{2,0,1:T(8,128)S(1)} %fusion.17), kind=kOutput, calls=%fused_computation.14 | convolution fusion | flops 50462720 | bytes 1445888 | tf_op jit(solution)/shard_map/rk,bjk->brj/dot_general | solution.py:116
  204.2 7.8 %fusion.7 = f32[64,16,128]{2,1,0:T(8,128)} fusion(f32[64,16,128]{2,1,0:T(8,128)S(1)} %fusion.132, bf16[64,1024,128]{2,1,0:T(8,128)(2,1)} %bitcast.148, bf16[64,8,2,8,128]{4,3,2,1,0:T(8,128)(2,1)S(1)} %bitcast.149), kind=kOutput, calls=%fused_computation.13 | convolution fusion | flops 268566528 | bytes 19922944 | tf_op jit(solution)/shard_map/brm,bmp->brp/dot_general | solution.py:93
  (102 shorter events, 19.8 us)
Async XLA Ops:
  0.0 6.5 %copy-start = (f32[64,64,64]{2,1,0:T(8,128)S(1)}, f32[64,64,64]{2,1,0:T(8,128)}, u32[]{:S(2)}) copy-start(f32[64,64,64]{2,1,0:T(8,128)} %param.13) | copy-start | bytes 3145732
  0.0 10.9 %copy-start.17 = (s32[1024,1]{0,1:T(1,128)S(1)}, s32[1024,1]{0,1:T(1,128)}, u32[]{:S(2)}) copy-start(s32[1024,1]{0,1:T(1,128)} %param.20) | copy-start | bytes 12292
  0.0 180.6 %collective-permute-start.8 = (bf16[64,16,128]{2,1,0:T(8,128)(2,1)}, bf16[64,16,128]{2,1,0:T(8,128)(2,1)S(1)}, u32[]{:S(2)}, u32[]{:S(2)}) collective-permute-start(bf16[64,16,128]{2,1,0:T(8,128)(2,1)} %param.11), channel_id=1, source_target_pairs={{1,0},{2,1},{3,2},{4,3},{5,4},{6,5},{7,6},{8,7},{9,8},{10,9},{11,1... | collective-permute-start | bytes 786440 | tf_op jit(solution)/shard_map/ppermute | solution.py:15
  2.2 178.3 %collective-permute-start.7 = (bf16[64,16,128]{2,1,0:T(8,128)(2,1)}, bf16[64,16,128]{2,1,0:T(8,128)(2,1)}, u32[]{:S(2)}, u32[]{:S(2)}) collective-permute-start(bf16[64,16,128]{2,1,0:T(8,128)(2,1)} %param.11), channel_id=1, source_target_pairs={{0,1},{1,2},{2,3},{3,4},{4,5},{5,6},{6,7},{7,8},{8,9},{9,10},{10,1... | collective-permute-start | bytes 786440 | tf_op jit(solution)/shard_map/ppermute | solution.py:14
  6.4 5.4 %copy-start.21 = (s32[2]{0:T(128)S(1)}, s32[2]{0:T(128)}, u32[]{:S(2)}) copy-start(s32[2]{0:T(128)} %constant.62) | copy-start | bytes 28
  6.4 5.5 %copy-start.20 = (s32[2]{0:T(128)S(1)}, s32[2]{0:T(128)}, u32[]{:S(2)}) copy-start(s32[2]{0:T(128)} %constant.59) | copy-start | bytes 28
  6.4 22.6 %copy-start.18 = (s32[1024]{0:T(1024)S(1)}, s32[1024]{0:T(1024)}, u32[]{:S(2)}) copy-start(s32[1024]{0:T(1024)} %param.19) | copy-start | bytes 12292
  7.7 70.0 %collective-permute-start = (f32[16,64]{1,0:T(8,128)S(1)}, f32[16,64]{1,0:T(8,128)S(1)}, u32[]{:S(2)}, u32[]{:S(2)}) collective-permute-start(f32[16,64]{1,0:T(8,128)S(1)} %convolution_bitcast_fusion.1), channel_id=1, source_target_pairs={{0,1},{1,0},{2,3},{3,2},{4,5},{5,4},{6,7},{7,6},{8,9},{9,8},{10,11... | collective-permute-start | bytes 12296 | tf_op jit(solution)/shard_map/ppermute | solution.py:21
  17.3 93.8 %all-to-all-start = ((s32[128,1,12]{2,1,0:T(1,128)}), s32[128,1,12]{2,1,0:T(1,128)S(1)}, u32[]{:S(2)}, u32[]{:S(2)}) async-start(s32[128,1,12]{2,1,0:T(1,128)} %copy.37), calls=%async_computation | async-start | bytes 131072 | tf_op jit(solution)/shard_map/all_to_all | solution.py:75
  72.1 5.6 %copy-start.3 = (f32[7,2,64,64]{3,2,1,0:T(8,128)S(1)}, f32[7,2,64,64]{3,2,1,0:T(8,128)}, u32[]{:S(2)}) copy-start(f32[7,2,64,64]{3,2,1,0:T(8,128)} %param.14) | copy-start | bytes 688132
  77.9 7.3 %collective-permute-start.1 = (f32[16,64]{1,0:T(8,128)S(1)}, f32[16,64]{1,0:T(8,128)S(1)}, u32[]{:S(2)}, u32[]{:S(2)}) collective-permute-start(f32[16,64]{1,0:T(8,128)S(1)} %convolution_add_fusion.12), channel_id=1, source_target_pairs={{0,2},{1,3},{2,0},{3,1},{4,6},{5,7},{6,4},{7,5},{8,10},{9,11},{10,... | collective-permute-start | bytes 12296 | tf_op jit(solution)/shard_map/ppermute | solution.py:21
  78.7 13.7 %copy-start.5 = (f32[7,2,64,64]{3,2,1,0:T(8,128)S(1)}, f32[7,2,64,64]{3,2,1,0:T(8,128)}, u32[]{:S(2)}) copy-start(f32[7,2,64,64]{3,2,1,0:T(8,128)} %param.15) | copy-start | bytes 688132
  78.7 17.2 %copy-start.19 = (s32[64,8]{0,1:T(8,128)S(1)}, s32[64,8]{0,1:T(8,128)}, u32[]{:S(2)}) copy-start(s32[64,8]{0,1:T(8,128)} %param.17) | copy-start | bytes 6148
  85.2 5.7 %copy-start.11 = (f32[16,64]{1,0:T(8,128)}, f32[16,64]{1,0:T(8,128)S(1)}, u32[]{:S(2)}) copy-start(f32[16,64]{1,0:T(8,128)S(1)} %collective-permute-done.1) | copy-start | bytes 12292
  85.5 5.2 %collective-permute-start.2 = (f32[16,64]{1,0:T(8,128)S(1)}, f32[16,64]{1,0:T(8,128)S(1)}, u32[]{:S(2)}, u32[]{:S(2)}) collective-permute-start(f32[16,64]{1,0:T(8,128)S(1)} %convolution_add_fusion.11), channel_id=1, source_target_pairs={{0,4},{1,5},{2,6},{3,7},{4,0},{5,1},{6,2},{7,3},{8,12},{9,13},{10,... | collective-permute-start | bytes 12296 | tf_op jit(solution)/shard_map/ppermute | solution.py:21
  91.3 3.7 %collective-permute-start.3 = (f32[16,64]{1,0:T(8,128)S(1)}, f32[16,64]{1,0:T(8,128)S(1)}, u32[]{:S(2)}, u32[]{:S(2)}) collective-permute-start(f32[16,64]{1,0:T(8,128)S(1)} %convolution_add_fusion.10), channel_id=1, source_target_pairs={{0,8},{1,9},{2,10},{3,11},{4,12},{5,13},{6,14},{7,15},{8,0},{9,1},... | collective-permute-start | bytes 12296 | tf_op jit(solution)/shard_map/ppermute | solution.py:21
  94.9 14.6 %copy-start.13 = (f32[16,64]{1,0:T(8,128)}, f32[16,64]{1,0:T(8,128)S(1)}, u32[]{:S(2)}) copy-start(f32[16,64]{1,0:T(8,128)S(1)} %collective-permute-done.3) | copy-start | bytes 12292
  95.2 5.3 %collective-permute-start.4 = (f32[16,64]{1,0:T(8,128)S(1)}, f32[16,64]{1,0:T(8,128)S(1)}, u32[]{:S(2)}, u32[]{:S(2)}) collective-permute-start(f32[16,64]{1,0:T(8,128)S(1)} %convolution_add_fusion.9), channel_id=1, source_target_pairs={{0,16},{1,17},{2,18},{3,19},{4,20},{5,21},{6,22},{7,23},{8,24},{9,... | collective-permute-start | bytes 12296 | tf_op jit(solution)/shard_map/ppermute | solution.py:21
  100.5 8.9 %copy-start.14 = (f32[16,64]{1,0:T(8,128)}, f32[16,64]{1,0:T(8,128)S(1)}, u32[]{:S(2)}) copy-start(f32[16,64]{1,0:T(8,128)S(1)} %collective-permute-done.4) | copy-start | bytes 12292
  100.8 8.8 %copy-start.16 = (f32[16,64]{1,0:T(8,128)}, f32[16,64]{1,0:T(8,128)S(1)}, u32[]{:S(2)}) copy-start(f32[16,64]{1,0:T(8,128)S(1)} %convolution_add_fusion.8) | copy-start | bytes 12292
  100.8 8.8 %collective-permute-start.5 = (f32[16,64]{1,0:T(8,128)S(1)}, f32[16,64]{1,0:T(8,128)S(1)}, u32[]{:S(2)}, u32[]{:S(2)}) collective-permute-start(f32[16,64]{1,0:T(8,128)S(1)} %convolution_add_fusion.8), channel_id=1, source_target_pairs={{0,32},{1,33},{2,34},{3,35},{4,36},{5,37},{6,38},{7,39},{8,40},{9,... | collective-permute-start | bytes 12296 | tf_op jit(solution)/shard_map/ppermute | solution.py:21
  109.7 0.6 copy-start.15
  111.0 60.5 %copy-start.10 = (f32[1,2,64,64]{3,2,1,0:T(8,128)S(1)}, f32[1,2,64,64]{3,2,1,0:T(8,128)}, u32[]{:S(2)}) copy-start(f32[1,2,64,64]{3,2,1,0:T(8,128)} %get-tuple-element.9) | copy-start | bytes 98308
  111.0 62.3 %copy-start.9 = (f32[1,2,64,64]{3,2,1,0:T(8,128)S(1)}, f32[1,2,64,64]{3,2,1,0:T(8,128)}, u32[]{:S(2)}) copy-start(f32[1,2,64,64]{3,2,1,0:T(8,128)} %get-tuple-element.8) | copy-start | bytes 98308
  111.0 64.1 %copy-start.8 = (f32[1,2,64,64]{3,2,1,0:T(8,128)S(1)}, f32[1,2,64,64]{3,2,1,0:T(8,128)}, u32[]{:S(2)}) copy-start(f32[1,2,64,64]{3,2,1,0:T(8,128)} %get-tuple-element.7) | copy-start | bytes 98308
  111.0 65.8 %copy-start.7 = (f32[1,2,64,64]{3,2,1,0:T(8,128)S(1)}, f32[1,2,64,64]{3,2,1,0:T(8,128)}, u32[]{:S(2)}) copy-start(f32[1,2,64,64]{3,2,1,0:T(8,128)} %get-tuple-element.6) | copy-start | bytes 98308
  111.0 67.6 %copy-start.6 = (f32[1,2,64,64]{3,2,1,0:T(8,128)S(1)}, f32[1,2,64,64]{3,2,1,0:T(8,128)}, u32[]{:S(2)}) copy-start(f32[1,2,64,64]{3,2,1,0:T(8,128)} %get-tuple-element.11) | copy-start | bytes 98308
  111.0 69.6 %copy-start.4 = (bf16[64,16,128]{2,1,0:T(8,128)(2,1)S(1)}, bf16[64,16,128]{2,1,0:T(8,128)(2,1)}, u32[]{:S(2)}) copy-start(bf16[64,16,128]{2,1,0:T(8,128)(2,1)} %param.11) | copy-start | bytes 786436
  111.0 73.4 %all-to-all-start.1 = ((bf16[128,12,1024]{2,1,0:T(8,128)(2,1)}), bf16[128,12,1024]{2,1,0:T(8,128)(2,1)}, u32[]{:S(2)}, u32[]{:S(2)}) async-start(bf16[128,12,1024]{2,1,0:T(8,128)(2,1)} %reshape.89), calls=%async_computation.1 | async-start | bytes 8388608 | tf_op jit(solution)/shard_map/all_to_all | solution.py:74
  122.9 46.8 %collective-permute-start.6 = (f32[16,64]{1,0:T(8,128)}, f32[16,64]{1,0:T(8,128)S(1)}, u32[]{:S(2)}, u32[]{:S(2)}) collective-permute-start(f32[16,64]{1,0:T(8,128)} %convolution_add_fusion.7), channel_id=1, source_target_pairs={{0,64},{1,65},{2,66},{3,67},{4,68},{5,69},{6,70},{7,71},{8,72},{9,... | collective-permute-start | bytes 12296 | tf_op jit(solution)/shard_map/ppermute | solution.py:21
  195.3 8.6 %copy-start.2 = (bf16[64,64,128]{2,1,0:T(8,128)(2,1)S(1)}, bf16[64,64,128]{2,1,0:T(8,128)(2,1)}, u32[]{:S(2)}) copy-start(bf16[64,64,128]{2,1,0:T(8,128)(2,1)} %param.12) | copy-start | bytes 3145732
  198.8 5.4 %copy-start.1 = (bf16[512,16,128]{2,1,0:T(8,128)(2,1)S(1)}, bf16[512,16,128]{2,1,0:T(8,128)(2,1)}, u32[]{:S(2)}) copy-start(bf16[512,16,128]{2,1,0:T(8,128)(2,1)} %gather_fusion.1) | copy-start | bytes 6291460
  (1 other events, 0.6 us)
where the time goes:
time: 214 us; the launch traced here: 212 us
  local copies, waits for them, and re-layouts  66.4 us (31%)
  matrix products  52.2 us (24%)
  waiting for transfers between devices  51.4 us (24%)
  starting transfers between devices  39 us (18%)
  other arithmetic  2.66 us (1%)
    ppermute x7, waiting for transfers between devices, partner_2(): lax.ppermute(value, axis, [(i, i ^ 1 << stride) for i in range(lax.axis_s...  51.4 us
    unnamed x46, local copies, waits for them, and re-layouts  29.5 us
    ppermute x7, starting transfers between devices, partner_2(): lax.ppermute(value, axis, [(i, i ^ 1 << stride) for i in range(lax.axis_s...  12.5 us
    all_to_all x1, starting transfers between devices, body(): lax.all_to_all(box_buffer, 'leaf', split_axis=0, concat_axis=0, tiled=True)  11.7 us
    dot_general x1, matrix products, body(): jnp.einsum('crj,cjk->crk', picked.reshape(entries, sides_rhs, ranks), cou...  10.6 us
    all_to_all x1, starting transfers between devices, body(): lax.all_to_all(send_values, 'leaf', split_axis=0, concat_axis=0, tiled=True)  10.4 us
    gather x1, local copies, waits for them, and re-layouts, body(): picked = skeleton_low[coup_source].reshape(entries, flat_width)  8.42 us
    dot_general x1, matrix products, body(): jnp.einsum('brm,bmp->brp', gathered, near_blocks.reshape(leaf_count, near...  7.84 us
  transfers between devices with their start and end apart: 11, of which 4 were waited for; matrix products, arithmetic and copies ran while one was open for 44% of the time, Pallas kernels for 0%

commit v1 on v0

v1 whole, which is shorter than its diff:
```python
import jax
import jax.numpy as jnp
from jax import lax
from jax.sharding import PartitionSpec as P


def padded_2(value, sides, width):
    for axis, dim in sides:
        peers, length = (lax.axis_size(axis), value.shape[dim])
        up = [(i, (i + 1) % peers) for i in range(peers - 1)]
        down = [(j, i) for i, j in up]
        last = lax.slice_in_dim(value, length - width, length, axis=dim)
        initial = lax.slice_in_dim(value, 0, width, axis=dim)
        before = lax.ppermute(last, axis, up)
        after = lax.ppermute(initial, axis, down)
        value = jnp.concatenate([before, value, after], axis=dim)
    return value


def body(
    charges,
    leaf_basis,
    leaf_up,
    top_up,
    top_coupling,
    near_blocks,
    near_list,
    coupling_blocks,
    coup_source,
    coup_device,
    coup_box,
):
    highest = lax.Precision.HIGHEST
    device_pos = lax.axis_index("leaf")
    devices = lax.axis_size("leaf")
    levels = devices.bit_length() - 1
    leaf_count = charges.shape[0]
    ranks = leaf_basis.shape[1]
    sides_rhs = charges.shape[1]
    panels = charges.shape[2]
    near_count = near_list.shape[1]
    entries = coup_source.shape[0]
    capacity = entries // devices + entries // (2 * devices)
    capacity = -(-capacity // 8) * 8
    slots = devices * capacity
    flat_width = sides_rhs * ranks

    target_dev = coup_device[:, 0]
    onehot_dev = (target_dev[:, None] == jnp.arange(devices, dtype=jnp.int32)[None, :]).astype(
        jnp.int32
    )
    slot_pos = jnp.sum((jnp.cumsum(onehot_dev, axis=0) - onehot_dev) * onehot_dev, axis=1)
    slot_flat = target_dev * capacity + slot_pos
    slot_table = (
        jnp.arange(slots, dtype=jnp.int32)[:, None] == slot_flat[None, :]
    ).astype(jnp.bfloat16)
    box_plus = (coup_box + 1).astype(jnp.bfloat16)
    box_buffer = (
        jnp.dot(slot_table, box_plus, preferred_element_type=jnp.float32).astype(jnp.int32) - 1
    )
    recv_boxes = lax.all_to_all(
        box_buffer.reshape(devices, 1, capacity), "leaf", split_axis=0, concat_axis=0, tiled=True
    )

    skeleton = jnp.einsum("bkp,brp->brk", leaf_basis, charges, preferred_element_type=jnp.float32)
    skeleton_low = skeleton.astype(jnp.bfloat16)
    own_box = jnp.einsum("brj,bjk->rk", skeleton, leaf_up, precision=highest)

    picked = skeleton_low[coup_source]
    products = jnp.einsum(
        "crj,cjk->crk", picked, coupling_blocks, preferred_element_type=jnp.float32
    ).astype(jnp.bfloat16)
    send_values = jnp.dot(
        slot_table, products.reshape(entries, flat_width), preferred_element_type=jnp.float32
    ).astype(jnp.bfloat16)
    received = lax.all_to_all(
        send_values.reshape(devices, capacity, flat_width),
        "leaf",
        split_axis=0,
        concat_axis=0,
        tiled=True,
    )

    boxes_all = lax.all_gather(own_box, "leaf", axis=0, tiled=False)
    upward = boxes_all
    ups = []
    for level in range(levels):
        ups.append(upward)
        if level + 1 < levels:
            count = upward.shape[0]
            paired = upward.reshape(count // 2, 2, sides_rhs, ranks)
            upward = jnp.einsum("nsrj,sjk->nrk", paired, top_up[level], precision=highest)
    local_exp = jnp.zeros((sides_rhs, ranks), jnp.float32)
    for level in reversed(range(levels)):
        node = device_pos >> level
        node_side = node & 1
        sibling = lax.dynamic_index_in_dim(ups[level], node ^ 1, 0, keepdims=False)
        coupled = jnp.dot(
            sibling,
            lax.dynamic_index_in_dim(top_coupling[level], node_side, 0, keepdims=False),
            precision=highest,
        )
        local_exp = (
            jnp.dot(
                local_exp,
                lax.dynamic_index_in_dim(top_up[level], node_side, 0, keepdims=False).T,
                precision=highest,
            )
            + coupled
        )

    padded = padded_2(charges, (("leaf", 0),), leaf_count)
    local_rows = near_list - (device_pos * leaf_count - leaf_count)
    gathered = padded[local_rows]
    gathered = jnp.transpose(gathered, (0, 2, 1, 3)).reshape(
        leaf_count, sides_rhs, near_count * panels
    )
    nearfield = jnp.einsum(
        "brm,bmp->brp",
        gathered,
        near_blocks.reshape(leaf_count, near_count * panels, panels),
        preferred_element_type=jnp.float32,
    )

    scatter_table = (
        recv_boxes.reshape(1, slots) == jnp.arange(leaf_count, dtype=jnp.int32)[:, None]
    ).astype(jnp.bfloat16)
    far = jnp.dot(
        scatter_table,
        received.reshape(slots, flat_width),
        preferred_element_type=jnp.float32,
    )
    far = far.reshape(leaf_count, sides_rhs, ranks)
    leaf_local = (jnp.einsum("rk,bjk->brj", local_exp, leaf_up, precision=highest) + far).astype(
        jnp.bfloat16
    )
    farfield = jnp.einsum(
        "brk,bkp->brp", leaf_local, leaf_basis, preferred_element_type=jnp.float32
    )
    return farfield + nearfield


def solution(mesh):
    return jax.shard_map(
        body,
        mesh=mesh,
        in_specs=(
            P("leaf", None, None),
            P("leaf", None, None),
            P("leaf", None, None),
            P(),
            P(),
            P("leaf", None, None, None),
            P("leaf", None),
            P("leaf", None, None),
            P("leaf"),
            P("leaf", None),
            P("leaf"),
        ),
        out_specs=P("leaf", None, None),
        check_vma=False,
    )
```

time: 214 us -> 221 us (1.033)
  the two profiles are of different devices: /device:TPU:28 before, /device:TPU:1 now
where the time goes in v1:
time: 221 us; the launch traced here: 218 us
  local copies, waits for them, and re-layouts  56.5 us (26%)
  matrix products  55.4 us (25%)
  blocking collectives  38.1 us (17%)
  waiting for transfers between devices  33.7 us (15%)
  starting transfers between devices  27.1 us (12%)
  other arithmetic  7.33 us (3%)
    all_gather x1, blocking collectives, body(): boxes_all = lax.all_gather(own_box, 'leaf', axis=0, tiled=False)  38.1 us
    all_to_all x1, waiting for transfers between devices, body(): lax.all_to_all(send_values.reshape(devices, capacity, flat_width), 'leaf'...  33.7 us
    unnamed x19, local copies, waits for them, and re-layouts  26.3 us
    all_to_all x1, starting transfers between devices, body(): lax.all_to_all(box_buffer.reshape(devices, 1, capacity), 'leaf', split_ax...  14.1 us
    dot_general x1, matrix products, body(): jnp.einsum('crj,cjk->crk', picked, coupling_blocks, preferred_element_typ...  10.6 us
    gather x1, local copies, waits for them, and re-layouts, body(): picked = skeleton_low[coup_source]  8.39 us
    dot_general x6, matrix products, body(): jnp.einsum('nsrj,sjk->nrk', paired, top_up[level], precision=highest)  8.35 us
    dot_general x1, matrix products, body(): jnp.einsum('brm,bmp->brp', gathered, near_blocks.reshape(leaf_count, near...  7.84 us
  transfers between devices with their start and end apart: 4, of which 1 were waited for; matrix products, arithmetic and copies ran while one was open for 42% of the time, Pallas kernels for 0%

profile of v1, /device:TPU:1, one launch (start us, length us, event | category | flops | bytes accessed | tf_op | source)
XLA Modules:
  0.0 218.3 jit_solution(15941930566522681434)
XLA Ops:
  0.0 3.5 %collective-permute-start.1 = (bf16[64,16,128]{2,1,0:T(8,128)(2,1)}, bf16[64,16,128]{2,1,0:T(8,128)(2,1)}, u32[]{:S(2)}, u32[]{:S(2)}) collective-permute-start(bf16[64,16,128]{2,1,0:T(8,128)(2,1)} %param.11), channel_id=1, source_target_pairs={{1,0},{2,1},{3,2},{4,3},{5,4},{6,5},{7,6},{8,7},{9,8},{10,9},{11,1... | collective-permute-start | bytes 786440 | tf_op jit(solution)/shard_map/ppermute | solution.py:15
  3.6 3.2 %collective-permute-start = (bf16[64,16,128]{2,1,0:T(8,128)(2,1)}, bf16[64,16,128]{2,1,0:T(8,128)(2,1)}, u32[]{:S(2)}, u32[]{:S(2)}) collective-permute-start(bf16[64,16,128]{2,1,0:T(8,128)(2,1)} %param.11), channel_id=1, source_target_pairs={{0,1},{1,2},{2,3},{3,4},{4,5},{5,6},{6,7},{7,8},{8,9},{9,10},{10,1... | collective-permute-start | bytes 786440 | tf_op jit(solution)/shard_map/ppermute | solution.py:14
  8.6 1.1 broadcast_add_fusion
  9.8 1.0 fusion.17
  12.2 1.5 fusion.1
  14.4 14.1 %all-to-all-start = ((s32[128,1,16]{2,1,0:T(1,128)}), s32[128,1,16]{2,1,0:T(1,128)}, u32[]{:S(2)}, u32[]{:S(2)}) async-start(s32[128,1,16]{2,1,0:T(1,128)} %bitcast.61), calls=%async_computation | async-start | bytes 131072 | tf_op jit(solution)/shard_map/all_to_all | solution.py:61
  28.5 1.8 fusion.106
  30.3 1.6 fusion.107
  31.9 1.2 convolution_bitcast_fusion.2
  33.2 38.1 %all-gather = f32[2048,64]{1,0:T(8,128)S(1)} all-gather(f32[16,64]{1,0:T(8,128)S(1)} %convolution_bitcast_fusion.2), channel_id=2, replica_groups=mesh['leaf'=128] {'leaf'}, dimensions={0}, use_global_device_ids=true | all-gather | bytes 528384 | tf_op jit(solution)/shard_map/all_gather | solution.py:84
  71.3 2.4 %fusion.14 = f32[64,16,64,1]{2,0,3,1:T(8,128)S(1)} fusion(f32[64,2,16,64]{3,2,1,0:T(8,128)S(1)} %bitcast.179, f32[7,2,64,64]{3,2,1,0:T(8,128)} %param.14), kind=kOutput, calls=%fused_computation.26 | convolution fusion | flops 100663296 | bytes 851968 | tf_op jit(solution)/shard_map/nsrj,sjk->nrk/dot_general | solution.py:92
  74.5 1.4 fusion.18
  76.6 1.3 fusion.25
  77.9 23.9 %copy.45 = bf16[1024,64,64]{2,1,0:T(8,128)(2,1)} copy(bf16[1024,64,64]{0,2,1:T(8,128)(2,1)} %param.18) | data formatting | bytes 16777216 | tf_op args[7]
  101.9 8.4 %gather_fusion = bf16[1024,16,64]{2,1,0:T(8,128)(2,1)} fusion(bf16[64,16,64]{2,1,0:T(8,128)(2,1)S(1)} %get-tuple-element.19, s32[1024]{0:T(1024)S(1)} %fusion.96), kind=kCustom, calls=%fused_computation | custom fusion | bytes 4198400 | tf_op jit(solution)/shard_map/gather | solution.py:69
  110.2 10.6 %convolution_convert_fusion = bf16[1024,16,64]{2,1,0:T(8,128)(2,1)} fusion(bf16[1024,16,64]{2,1,0:T(8,128)(2,1)} %gather_fusion, bf16[1024,64,64]{2,1,0:T(8,128)(2,1)} %copy.45), kind=kOutput, calls=%fused_computation.8 | convolution fusion | flops 135266304 | bytes 12582912 | tf_op jit(solution)/shard_map/crj,cjk->crk/dot_general | solution.py:70
  120.9 5.5 %copy.46 = bf16[1024,16,64]{0,2,1:T(8,128)(2,1)} copy(bf16[1024,16,64]{2,1,0:T(8,128)(2,1)} %convolution_convert_fusion) | data formatting | bytes 4194304 | tf_op jit(solution)/shard_map/convert_element_type | solution.py:72
  126.4 7.7 %fusion.4 = bf16[2048,1024]{1,0:T(8,128)(2,1)} fusion(bf16[1024,1024]{0,1:T(8,128)(2,1)} %bitcast.184, s32[1024]{0:T(1024)S(1)} %multiply_add_fusion), kind=kOutput, calls=%fused_computation.7 | convolution fusion | flops 4299161600 | bytes 6295552 | tf_op jit(solution)/shard_map/dot_general | solution.py:73
  135.1 6.3 %all-to-all-start.1 = ((bf16[128,16,1024]{2,1,0:T(8,128)(2,1)}), bf16[128,16,1024]{2,1,0:T(8,128)(2,1)}, u32[]{:S(2)}, u32[]{:S(2)}) async-start(bf16[128,16,1024]{2,1,0:T(8,128)(2,1)} %bitcast.181), calls=%async_computation.1 | async-start | bytes 8388608 | tf_op jit(solution)/shard_map/all_to_all | solution.py:76
  142.2 1.1 fusion.32
  143.3 1.1 fusion.30
  144.4 1.1 convolution_bitcast_fusion.1
  145.5 1.1 fusion.105
  147.8 0.9 fusion.50
  154.6 1.6 reduce.3
  156.4 1.2 pad_maximum_fusion
  157.6 2.8 %gather_fusion.1 = bf16[512,16,128]{2,1,0:T(8,128)(2,1)} fusion(bf16[192,16,128]{2,1,0:T(8,128)(2,1)S(1)} %pad_maximum_fusion, s32[1024]{0:T(1024)S(1)} %pad_clamp_fusion), kind=kCustom, calls=%fused_computation.1 | custom fusion | bytes 4196352 | tf_op jit(solution)/shard_map/gather | solution.py:114
  160.3 33.7 %all-to-all-done.1 = bf16[128,16,1024]{2,1,0:T(8,128)(2,1)} async-done(((bf16[128,16,1024]{2,1,0:T(8,128)(2,1)}), bf16[128,16,1024]{2,1,0:T(8,128)(2,1)}, u32[]{:S(2)}, u32[]{:S(2)}) %all-to-all-start.1) | async-done | bytes 4194336 | tf_op jit(solution)/shard_map/all_to_all | solution.py:76
  194.1 6.5 %copy.47 = bf16[1024,2048]{1,0:T(8,128)(2,1)} copy(bf16[1024,2048]{0,1:T(8,128)(2,1)} %bitcast.66) | data formatting | bytes 8388608 | tf_op jit(solution)/shard_map/dot_general | solution.py:128
  200.6 4.5 %fusion.23 = f32[64,16,64]{2,0,1:T(8,128)S(1)} fusion(bf16[16,64,2048]{2,1,0:T(8,128)(2,1)} %bitcast.177, s32[2048]{0:T(1024)S(1)} %eq.61), kind=kOutput, calls=%fused_computation.40 | convolution fusion | flops 268566528 | bytes 4464640 | tf_op jit(solution)/shard_map/dot_general | solution.py:128
  205.1 5.0 %fusion.12 = bf16[64,16,64]{2,1,0:T(8,128)(2,1)S(1)} fusion(f32[16,64,1]{1,0,2:T(8,128)S(1)} %fusion.13, f32[64,64,64]{2,1,0:T(8,128)S(1)} %copy-done, f32[64,16,64]{2,0,1:T(8,128)S(1)} %fusion.23), kind=kOutput, calls=%fused_computation.15 | convolution fusion | flops 50462720 | bytes 1445888 | tf_op jit(solution)/shard_map/rk,bjk->brj/dot_general | solution.py:134
  210.5 7.8 %fusion.9 = f32[64,16,128]{2,1,0:T(8,128)} fusion(f32[64,16,128]{2,1,0:T(8,128)S(1)} %fusion.108, bf16[64,1024,128]{2,1,0:T(8,128)(2,1)} %bitcast.176, bf16[64,8,2,8,128]{4,3,2,1,0:T(8,128)(2,1)S(1)} %bitcast.178), kind=kOutput, calls=%fused_computation.14 | convolution fusion | flops 268566528 | bytes 19922944 | tf_op jit(solution)/shard_map/brm,bmp->brp/dot_general | solution.py:118
  (55 shorter events, 15.1 us)
Async XLA Ops:
  0.0 31.9 %copy-start = (f32[64,64,64]{2,1,0:T(8,128)S(1)}, f32[64,64,64]{2,1,0:T(8,128)}, u32[]{:S(2)}) copy-start(f32[64,64,64]{2,1,0:T(8,128)} %param.13) | copy-start | bytes 3145732
  0.0 30.3 %copy-start.2 = (bf16[64,64,128]{2,1,0:T(8,128)(2,1)S(1)}, bf16[64,64,128]{2,1,0:T(8,128)(2,1)}, u32[]{:S(2)}) copy-start(bf16[64,64,128]{2,1,0:T(8,128)(2,1)} %param.12) | copy-start | bytes 3145732
  0.0 156.4 %collective-permute-start.1 = (bf16[64,16,128]{2,1,0:T(8,128)(2,1)}, bf16[64,16,128]{2,1,0:T(8,128)(2,1)}, u32[]{:S(2)}, u32[]{:S(2)}) collective-permute-start(bf16[64,16,128]{2,1,0:T(8,128)(2,1)} %param.11), channel_id=1, source_target_pairs={{1,0},{2,1},{3,2},{4,3},{5,4},{6,5},{7,6},{8,7},{9,8},{10,9},{11,1... | collective-permute-start | bytes 786440 | tf_op jit(solution)/shard_map/ppermute | solution.py:15
  3.6 152.8 %collective-permute-start = (bf16[64,16,128]{2,1,0:T(8,128)(2,1)}, bf16[64,16,128]{2,1,0:T(8,128)(2,1)}, u32[]{:S(2)}, u32[]{:S(2)}) collective-permute-start(bf16[64,16,128]{2,1,0:T(8,128)(2,1)} %param.11), channel_id=1, source_target_pairs={{0,1},{1,2},{2,3},{3,4},{4,5},{5,6},{6,7},{7,8},{8,9},{9,10},{10,1... | collective-permute-start | bytes 786440 | tf_op jit(solution)/shard_map/ppermute | solution.py:14
  7.8 0.8 copy-start.5
  14.4 120.7 %all-to-all-start = ((s32[128,1,16]{2,1,0:T(1,128)}), s32[128,1,16]{2,1,0:T(1,128)}, u32[]{:S(2)}, u32[]{:S(2)}) async-start(s32[128,1,16]{2,1,0:T(1,128)} %bitcast.61), calls=%async_computation | async-start | bytes 131072 | tf_op jit(solution)/shard_map/all_to_all | solution.py:61
  30.3 47.6 %copy-start.8 = (s32[1024]{0:T(1024)S(1)}, s32[1024]{0:T(1024)}, u32[]{:S(2)}) copy-start(s32[1024]{0:T(1024)} %param.19) | copy-start | bytes 12292
  73.7 0.8 copy-start.4
  75.9 0.7 copy-start.6
  126.4 7.7 %copy-start.7 = (f32[1,2,64,64]{3,2,1,0:T(8,128)S(1)}, f32[1,2,64,64]{3,2,1,0:T(8,128)}, u32[]{:S(2)}) copy-start(f32[1,2,64,64]{3,2,1,0:T(8,128)} %get-tuple-element.16) | copy-start | bytes 98308
  135.1 59.0 %all-to-all-start.1 = ((bf16[128,16,1024]{2,1,0:T(8,128)(2,1)}), bf16[128,16,1024]{2,1,0:T(8,128)(2,1)}, u32[]{:S(2)}, u32[]{:S(2)}) async-start(bf16[128,16,1024]{2,1,0:T(8,128)(2,1)} %bitcast.181), calls=%async_computation.1 | async-start | bytes 8388608 | tf_op jit(solution)/shard_map/all_to_all | solution.py:76
  200.6 9.4 %copy-start.3 = (bf16[64,64,128]{2,1,0:T(8,128)(2,1)S(1)}, bf16[64,64,128]{2,1,0:T(8,128)(2,1)}, u32[]{:S(2)}) copy-start(bf16[64,64,128]{2,1,0:T(8,128)(2,1)} %param.12) | copy-start | bytes 3145732
  200.6 9.9 %copy-start.1 = (bf16[512,16,128]{2,1,0:T(8,128)(2,1)S(1)}, bf16[512,16,128]{2,1,0:T(8,128)(2,1)}, u32[]{:S(2)}) copy-start(bf16[512,16,128]{2,1,0:T(8,128)(2,1)} %gather_fusion.1) | copy-start | bytes 6291460

commit v2 on v1

--- a/solution.py
+++ b/solution.py
@@ -41,8 +41,7 @@
     near_count = near_list.shape[1]
     entries = coup_source.shape[0]
     capacity = entries // devices + entries // (2 * devices)
-    capacity = -(-capacity // 8) * 8
-    slots = devices * capacity
+    rows = -(-(capacity + 1) // 8) * 8
     flat_width = sides_rhs * ranks
 
     target_dev = coup_device[:, 0]
@@ -50,38 +49,53 @@
         jnp.int32
     )
     slot_pos = jnp.sum((jnp.cumsum(onehot_dev, axis=0) - onehot_dev) * onehot_dev, axis=1)
-    slot_flat = target_dev * capacity + slot_pos
+    slot_flat = target_dev * rows + slot_pos
     slot_table = (
-        jnp.arange(slots, dtype=jnp.int32)[:, None] == slot_flat[None, :]
+        jnp.arange(devices * rows, dtype=jnp.int32)[:, None] == slot_flat[None, :]
     ).astype(jnp.bfloat16)
     box_plus = (coup_box + 1).astype(jnp.bfloat16)
-    box_buffer = (
-        jnp.dot(slot_table, box_plus, preferred_element_type=jnp.float32).astype(jnp.int32) - 1
+    box_slots = jnp.dot(
+        slot_table.reshape(devices, rows, entries)[:, :capacity, :],
+        box_plus,
+        preferred_element_type=jnp.float32,
     )
-    recv_boxes = lax.all_to_all(
-        box_buffer.reshape(devices, 1, capacity), "leaf", split_axis=0, concat_axis=0, tiled=True
-    )
+    lanes = -(-capacity // 128) * 128
+    box_table = jnp.where(
+        jnp.arange(rows, dtype=jnp.int32)[None, :, None] == capacity,
+        jnp.pad(box_slots, ((0, 0), (0, lanes - capacity)))[:, None, :],
+        0.0,
+    ).astype(jnp.bfloat16).reshape(devices * rows, lanes)
+    lane_place = (
+        jnp.arange(lanes, dtype=jnp.int32)[:, None] == jnp.arange(flat_width, dtype=jnp.int32)[None, :]
+    ).astype(jnp.bfloat16)
 
     skeleton = jnp.einsum("bkp,brp->brk", leaf_basis, charges, preferred_element_type=jnp.float32)
     skeleton_low = skeleton.astype(jnp.bfloat16)
     own_box = jnp.einsum("brj,bjk->rk", skeleton, leaf_up, precision=highest)
 
-    picked = skeleton_low[coup_source]
+    source_table = (
+        coup_source[:, None] == jnp.arange(leaf_count, dtype=jnp.int32)[None, :]
+    ).astype(jnp.bfloat16)
+    picked = jnp.einsum(
+        "es,srj->erj", source_table, skeleton_low, preferred_element_type=jnp.float32
+    ).astype(jnp.bfloat16)
     products = jnp.einsum(
         "crj,cjk->crk", picked, coupling_blocks, preferred_element_type=jnp.float32
     ).astype(jnp.bfloat16)
     send_values = jnp.dot(
         slot_table, products.reshape(entries, flat_width), preferred_element_type=jnp.float32
-    ).astype(jnp.bfloat16)
-    received = lax.all_to_all(
-        send_values.reshape(devices, capacity, flat_width),
-        "leaf",
-        split_axis=0,
-        concat_axis=0,
-        tiled=True,
-    )
+    ) + jnp.dot(box_table, lane_place, preferred_element_type=jnp.float32)
+    send_values = send_values.astype(jnp.bfloat16).reshape(devices, rows, flat_width)
+    received = lax.all_to_all(send_values, "leaf", split_axis=0, concat_axis=0, tiled=True)
+    recv_boxes = jnp.where(
+        jnp.arange(rows, dtype=jnp.int32)[None, :] < capacity,
+        jnp.pad(received[:, capacity, :capacity], ((0, 0), (0, rows - capacity))).astype(jnp.int32),
+        0,
+    ) - 1
 
-    boxes_all = lax.all_gather(own_box, "leaf", axis=0, tiled=False)
+    boxes_all = lax.all_gather(
+        jnp.concatenate([own_box, jnp.zeros_like(own_box)], axis=0), "leaf", axis=0, tiled=False
+    )[:, :sides_rhs]
     upward = boxes_all
     ups = []
     for level in range(levels):
@@ -123,11 +137,11 @@
     )
 
     scatter_table = (
-        recv_boxes.reshape(1, slots) == jnp.arange(leaf_count, dtype=jnp.int32)[:, None]
+        recv_boxes.reshape(1, devices * rows) == jnp.arange(leaf_count, dtype=jnp.int32)[:, None]
     ).astype(jnp.bfloat16)
     far = jnp.dot(
         scatter_table,
-        received.reshape(slots, flat_width),
+        received.reshape(devices * rows, flat_width),
         preferred_element_type=jnp.float32,
     )
     far = far.reshape(leaf_count, sides_rhs, ranks)

time: 221 us -> 186 us (0.84)
  blocking collectives: 38.1 us -> 0 us
  between operations: 0.24 us -> 13.9 us
  starting transfers between devices: 27.1 us -> 20.5 us
  waiting for transfers between devices: 33.7 us -> 39.7 us
  local copies, waits for them, and re-layouts: 56.5 us -> 50.9 us
    all_gather x1 -> x0, blocking collectives: 38.1 us -> none  [body(): boxes_all = lax.all_gather(own_box, 'leaf', axis=0, tiled=False)]
    gather x1 -> x0, local copies, waits for them, and re-layouts: 8.39 us -> none  [body(): picked = skeleton_low[coup_source]]
    dot_general x2 -> x3, matrix products: 5.91 us -> 12.9 us  [the longest x1 6.26 us: body(): jnp.dot(box_table, lane_place, preferred_element_type=jnp.float32)]
    convert_element_type x0 -> x2, local copies, waits for them, and re-layouts: none -> 6.47 us  [the longest x1 6.19 us: body(): picked = jnp.einsum('es,srj->erj', source_table, skeleton_low, preferred_...]
    all_to_all x2 -> x1, starting transfers between devices: 20.3 us -> 13.9 us  [body(): lax.all_to_all(send_values, 'leaf', split_axis=0, concat_axis=0, tiled=True)]
    all_to_all x2 -> x1, waiting for transfers between devices: 33.7 us -> 39.7 us  [body(): lax.all_to_all(send_values, 'leaf', split_axis=0, concat_axis=0, tiled=True)]
    dot_general x6, matrix products: 8.35 us -> 3.32 us  [body(): jnp.einsum('nsrj,sjk->nrk', paired, top_up[level], precision=highest)]
    dot_general x7, matrix products: 5.61 us -> 1.02 us  [body(): jnp.dot(local_exp, lax.dynamic_index_in_dim(top_up[level], node_side, 0,...]
  transfers between devices with their start and end apart: 4 -> 4, of which waited for: 1 -> 1; matrix products, arithmetic and copies ran while one was open for 42% -> 46% of each run, Pallas kernels for 0% -> 0%
where the time goes in v2:
time: 186 us; the launch traced here: 185 us
  matrix products  54.5 us (29%)
  local copies, waits for them, and re-layouts  50.9 us (27%)
  waiting for transfers between devices  39.7 us (21%)
  starting transfers between devices  20.5 us (11%)
  between operations  13.9 us (7%)
  other arithmetic  5.35 us (3%)
    all_to_all x1, waiting for transfers between devices, body(): lax.all_to_all(send_values, 'leaf', split_axis=0, concat_axis=0, tiled=True)  39.7 us
    unnamed x40, local copies, waits for them, and re-layouts  24.1 us
    all_to_all x1, starting transfers between devices, body(): lax.all_to_all(send_values, 'leaf', split_axis=0, concat_axis=0, tiled=True)  13.9 us
    dot_general x1, matrix products, body(): jnp.einsum('crj,cjk->crk', picked, coupling_blocks, preferred_element_typ...  10.7 us
    dot_general x1, matrix products, body(): jnp.dot(slot_table, products.reshape(entries, flat_width), preferred_elem...  8.33 us
    dot_general x1, matrix products, body(): jnp.einsum('brm,bmp->brp', gathered, near_blocks.reshape(leaf_count, near...  7.84 us
    dot_general x1, local copies, waits for them, and re-layouts, body(): jnp.dot(scatter_table, received.reshape(devices * rows, flat_width), pref...  6.55 us
    dot_general x1, matrix products, body(): jnp.dot(box_table, lane_place, preferred_element_type=jnp.float32)  6.26 us
  transfers between devices with their start and end apart: 4, of which 1 were waited for; matrix products, arithmetic and copies ran while one was open for 46% of the time, Pallas kernels for 0%

profile of v2, /device:TPU:1, one launch (start us, length us, event | category | flops | bytes accessed | tf_op | source)
XLA Modules:
  0.0 184.9 jit_solution(7443757082063995882)
XLA Ops:
  6.5 3.4 %collective-permute-start.1 = (bf16[64,16,128]{2,1,0:T(8,128)(2,1)}, bf16[64,16,128]{2,1,0:T(8,128)(2,1)}, u32[]{:S(2)}, u32[]{:S(2)}) collective-permute-start(bf16[64,16,128]{2,1,0:T(8,128)(2,1)} %param.11), channel_id=1, source_target_pairs={{1,0},{2,1},{3,2},{4,3},{5,4},{6,5},{7,6},{8,7},{9,8},{10,9},{11,1... | collective-permute-start | bytes 786440 | tf_op jit(solution)/shard_map/ppermute | solution.py:15
  10.0 3.2 %collective-permute-start = (bf16[64,16,128]{2,1,0:T(8,128)(2,1)}, bf16[64,16,128]{2,1,0:T(8,128)(2,1)}, u32[]{:S(2)}, u32[]{:S(2)}) collective-permute-start(bf16[64,16,128]{2,1,0:T(8,128)(2,1)} %param.11), channel_id=1, source_target_pairs={{0,1},{1,2},{2,3},{3,4},{4,5},{5,6},{6,7},{7,8},{8,9},{9,10},{10,1... | collective-permute-start | bytes 786440 | tf_op jit(solution)/shard_map/ppermute | solution.py:14
  13.2 2.0 %fusion.108 = (bf16[64,16,64]{2,1,0:T(8,128)(2,1)S(1)}, f32[64,16,64]{2,1,0:T(8,128)S(1)}) fusion(bf16[64,16,128]{2,1,0:T(8,128)(2,1)} %param.11, bf16[64,64,128]{2,1,0:T(8,128)(2,1)} %param.12), kind=kOutput, calls=%fused_computation.140 | convolution fusion | flops 16842752 | bytes 1703936 | tf_op jit(solution)/shard_map/bkp,brp->brk/dot_general | solution.py:72
  15.1 1.2 convolution_bitcast_fusion.2
  16.4 0.6 concatenate.6
  17.3 0.7 fusion.29
  18.0 1.7 convert_element_type.43
  19.7 6.2 %copy.50 = bf16[1024,16,64]{2,1,0:T(8,128)(2,1)} copy(bf16[1024,16,64]{0,2,1:T(8,128)(2,1)} %convert_element_type.43) | data formatting | bytes 4194304 | tf_op jit(solution)/shard_map/convert_element_type | solution.py:81
  25.9 23.9 %copy.51 = bf16[1024,64,64]{2,1,0:T(8,128)(2,1)} copy(bf16[1024,64,64]{0,2,1:T(8,128)(2,1)} %param.18) | data formatting | bytes 16777216 | tf_op args[7]
  49.9 10.7 %convolution_convert_fusion = bf16[1024,16,64]{2,1,0:T(8,128)(2,1)} fusion(bf16[1024,16,64]{2,1,0:T(8,128)(2,1)} %copy.50, bf16[1024,64,64]{2,1,0:T(8,128)(2,1)} %copy.51), kind=kOutput, calls=%fused_computation.8 | convolution fusion | flops 135266304 | bytes 12582912 | tf_op jit(solution)/shard_map/crj,cjk->crk/dot_general | solution.py:82
  60.6 5.5 %copy.52 = bf16[1024,16,64]{0,2,1:T(8,128)(2,1)} copy(bf16[1024,16,64]{2,1,0:T(8,128)(2,1)} %convolution_convert_fusion) | data formatting | bytes 4194304 | tf_op jit(solution)/shard_map/convert_element_type | solution.py:84
  66.6 0.4 fusion.17
  67.0 8.3 %fusion = f32[2048,1024]{1,0:T(8,128)} fusion(bf16[1024,1024]{0,1:T(8,128)(2,1)} %bitcast.193, s32[1024]{0:T(1024)S(1)} %multiply_add_fusion.1), kind=kOutput, calls=%fused_computation.3 | convolution fusion | flops 4297064448 | bytes 10489856 | tf_op jit(solution)/shard_map/dot_general | solution.py:85
  75.3 1.3 broadcast_compare_fusion
  76.7 2.2 %fusion.1 = bf16[1,128,12]{1,0,2:T(2,128)(2,1)S(1)} fusion(bf16[1024,1,1]{0,1,2:T(2,128)(2,1)S(1)} %reshape.158, pred[128,12,1024]{2,1,0:T(8,128)(4,1)S(1)} %broadcast_compare_fusion), kind=kOutput, calls=%fused_computation.4 | convolution fusion | flops 3145728 | bytes 1577984 | tf_op jit(solution)/shard_map/dot_general | solution.py:57
  79.5 6.3 %add_convert_fusion = bf16[2048,1024]{1,0:T(8,128)(2,1)} fusion(f32[2048,1024]{1,0:T(8,128)} %fusion, bf16[2048,128]{1,0:T(8,128)(2,1)S(1)} %fusion.13), kind=kOutput, calls=%fused_computation.1 | convolution fusion | flops 541196288 | bytes 13107200 | tf_op jit(solution)/shard_map/dot_general | solution.py:87
  85.7 13.9 %all-to-all-start = ((bf16[128,16,1024]{2,1,0:T(8,128)(2,1)}), bf16[128,16,1024]{2,1,0:T(8,128)(2,1)}, u32[]{:S(2)}, u32[]{:S(2)}) async-start(bf16[128,16,1024]{2,1,0:T(8,128)(2,1)} %bitcast.186), calls=%async_computation | async-start | bytes 8388608 | tf_op jit(solution)/shard_map/all_to_all | solution.py:89
  99.9 0.7 fusion.107
  100.9 0.7 fusion.106
  101.6 1.2 pad_maximum_fusion
  102.8 2.8 %gather_fusion = bf16[512,16,128]{2,1,0:T(8,128)(2,1)} fusion(bf16[192,16,128]{2,1,0:T(8,128)(2,1)S(1)} %pad_maximum_fusion, s32[1024]{0:T(1024)S(1)} %pad_clamp_fusion), kind=kCustom, calls=%fused_computation | custom fusion | bytes 4196352 | tf_op jit(solution)/shard_map/gather | solution.py:128
  105.7 1.5 slice.84
  107.1 1.6 fusion.14
  108.7 0.6 fusion.18
  109.3 0.4 fusion.25
  112.7 39.7 %all-to-all-done = bf16[128,16,1024]{2,1,0:T(8,128)(2,1)} async-done(((bf16[128,16,1024]{2,1,0:T(8,128)(2,1)}), bf16[128,16,1024]{2,1,0:T(8,128)(2,1)}, u32[]{:S(2)}, u32[]{:S(2)}) %all-to-all-start) | async-done | bytes 4194336 | tf_op jit(solution)/shard_map/all_to_all | solution.py:89
  152.4 6.5 %copy.55 = bf16[1024,2048]{1,0:T(8,128)(2,1)} copy(bf16[1024,2048]{0,1:T(8,128)(2,1)} %bitcast.69) | data formatting | bytes 8388608 | tf_op jit(solution)/shard_map/dot_general | solution.py:142
  158.9 1.1 slice.88
  160.4 4.5 %fusion.23 = f32[64,16,64]{2,0,1:T(8,128)S(1)} fusion(bf16[16,64,2048]{2,1,0:T(8,128)(2,1)} %bitcast.188, s32[2048]{0:T(1024)S(1)} %eq.121), kind=kOutput, calls=%fused_computation.43 | convolution fusion | flops 268566528 | bytes 4464640 | tf_op jit(solution)/shard_map/dot_general | solution.py:142
  164.8 5.0 %fusion.11 = bf16[64,16,64]{2,1,0:T(8,128)(2,1)S(1)} fusion(f32[16,64,1]{1,0,2:T(8,128)S(1)} %fusion.12, f32[64,64,64]{2,1,0:T(8,128)S(1)} %copy-done, f32[64,16,64]{2,0,1:T(8,128)S(1)} %fusion.23), kind=kOutput, calls=%fused_computation.15 | convolution fusion | flops 50462720 | bytes 1445888 | tf_op jit(solution)/shard_map/rk,bjk->brj/dot_general | solution.py:148
  169.8 0.4 fusion.109
  170.2 7.8 %fusion.8 = f32[64,16,128]{2,1,0:T(8,128)} fusion(f32[64,16,128]{2,1,0:T(8,128)S(1)} %fusion.109, bf16[64,1024,128]{2,1,0:T(8,128)(2,1)} %bitcast.185, bf16[64,8,2,8,128]{4,3,2,1,0:T(8,128)(2,1)S(1)} %bitcast.189), kind=kOutput, calls=%fused_computation.14 | convolution fusion | flops 268566528 | bytes 19922944 | tf_op jit(solution)/shard_map/brm,bmp->brp/dot_general | solution.py:132
  (89 shorter events, 5.0 us)
Async XLA Ops:
  6.5 8.6 %copy-start = (f32[64,64,64]{2,1,0:T(8,128)S(1)}, f32[64,64,64]{2,1,0:T(8,128)}, u32[]{:S(2)}) copy-start(f32[64,64,64]{2,1,0:T(8,128)} %param.13) | copy-start | bytes 3145732
  6.5 10.8 %copy-start.16 = (s32[1024]{0:T(1024)S(1)}, s32[1024]{0:T(1024)}, u32[]{:S(2)}) copy-start(s32[1024]{0:T(1024)} %param.19) | copy-start | bytes 12292
  6.5 99.1 %all-gather.3.cloned.1.call-start = ((), (), s32[]{:S(2)}) async-start(), calls=%async_computation.1 | async-start | bytes 2113536 | tf_op jit(solution)/shard_map/all_gather | solution.py:96
  6.5 95.1 %collective-permute-start.1 = (bf16[64,16,128]{2,1,0:T(8,128)(2,1)}, bf16[64,16,128]{2,1,0:T(8,128)(2,1)}, u32[]{:S(2)}, u32[]{:S(2)}) collective-permute-start(bf16[64,16,128]{2,1,0:T(8,128)(2,1)} %param.11), channel_id=1, source_target_pairs={{1,0},{2,1},{3,2},{4,3},{5,4},{6,5},{7,6},{8,7},{9,8},{10,9},{11,1... | collective-permute-start | bytes 786440 | tf_op jit(solution)/shard_map/ppermute | solution.py:15
  10.0 91.6 %collective-permute-start = (bf16[64,16,128]{2,1,0:T(8,128)(2,1)}, bf16[64,16,128]{2,1,0:T(8,128)(2,1)}, u32[]{:S(2)}, u32[]{:S(2)}) collective-permute-start(bf16[64,16,128]{2,1,0:T(8,128)(2,1)} %param.11), channel_id=1, source_target_pairs={{0,1},{1,2},{2,3},{3,4},{4,5},{5,6},{6,7},{7,8},{8,9},{9,10},{10,1... | collective-permute-start | bytes 786440 | tf_op jit(solution)/shard_map/ppermute | solution.py:14
  60.6 5.5 %copy-start.15 = (s32[1024,1]{0,1:T(1,128)S(1)}, s32[1024,1]{0,1:T(1,128)}, u32[]{:S(2)}) copy-start(s32[1024,1]{0,1:T(1,128)} %param.20) | copy-start | bytes 12292
  60.6 6.4 %copy-start.17 = (s32[1024]{0:T(1024)S(1)}, s32[1024]{0:T(1024)}, u32[]{:S(2)}) copy-start(s32[1024]{0:T(1024)} %param.21) | copy-start | bytes 12292
  85.7 13.9 %copy-start.18 = (s32[64,8]{0,1:T(8,128)S(1)}, s32[64,8]{0,1:T(8,128)}, u32[]{:S(2)}) copy-start(s32[64,8]{0,1:T(8,128)} %param.17) | copy-start | bytes 6148
  85.7 14.1 %copy-start.3 = (f32[7,2,64,64]{3,2,1,0:T(8,128)S(1)}, f32[7,2,64,64]{3,2,1,0:T(8,128)}, u32[]{:S(2)}) copy-start(f32[7,2,64,64]{3,2,1,0:T(8,128)} %param.14) | copy-start | bytes 688132
  85.7 15.1 %copy-start.4 = (f32[7,2,64,64]{3,2,1,0:T(8,128)S(1)}, f32[7,2,64,64]{3,2,1,0:T(8,128)}, u32[]{:S(2)}) copy-start(f32[7,2,64,64]{3,2,1,0:T(8,128)} %param.15) | copy-start | bytes 688132
  85.7 66.6 %all-to-all-start = ((bf16[128,16,1024]{2,1,0:T(8,128)(2,1)}), bf16[128,16,1024]{2,1,0:T(8,128)(2,1)}, u32[]{:S(2)}, u32[]{:S(2)}) async-start(bf16[128,16,1024]{2,1,0:T(8,128)(2,1)} %bitcast.186), calls=%async_computation | async-start | bytes 8388608 | tf_op jit(solution)/shard_map/all_to_all | solution.py:89
  105.6 5.0 %copy-start.8 = (f32[1,2,64,64]{3,2,1,0:T(8,128)S(1)}, f32[1,2,64,64]{3,2,1,0:T(8,128)}, u32[]{:S(2)}) copy-start(f32[1,2,64,64]{3,2,1,0:T(8,128)} %get-tuple-element.10) | copy-start | bytes 98308
  105.6 5.1 %copy-start.14 = (f32[1,2,64,64]{3,2,1,0:T(8,128)S(1)}, f32[1,2,64,64]{3,2,1,0:T(8,128)}, u32[]{:S(2)}) copy-start(f32[1,2,64,64]{3,2,1,0:T(8,128)} %get-tuple-element.17) | copy-start | bytes 98308
  105.6 5.3 %copy-start.7 = (f32[1,2,64,64]{3,2,1,0:T(8,128)S(1)}, f32[1,2,64,64]{3,2,1,0:T(8,128)}, u32[]{:S(2)}) copy-start(f32[1,2,64,64]{3,2,1,0:T(8,128)} %get-tuple-element.9) | copy-start | bytes 98308
  105.6 5.5 %copy-start.13 = (f32[1,2,64,64]{3,2,1,0:T(8,128)S(1)}, f32[1,2,64,64]{3,2,1,0:T(8,128)}, u32[]{:S(2)}) copy-start(f32[1,2,64,64]{3,2,1,0:T(8,128)} %get-tuple-element.18) | copy-start | bytes 98308
  105.6 5.6 %copy-start.6 = (f32[1,2,64,64]{3,2,1,0:T(8,128)S(1)}, f32[1,2,64,64]{3,2,1,0:T(8,128)}, u32[]{:S(2)}) copy-start(f32[1,2,64,64]{3,2,1,0:T(8,128)} %get-tuple-element.8) | copy-start | bytes 98308
  105.6 5.8 %copy-start.12 = (f32[1,2,64,64]{3,2,1,0:T(8,128)S(1)}, f32[1,2,64,64]{3,2,1,0:T(8,128)}, u32[]{:S(2)}) copy-start(f32[1,2,64,64]{3,2,1,0:T(8,128)} %get-tuple-element.13) | copy-start | bytes 98308
  105.6 5.9 %copy-start.5 = (f32[1,2,64,64]{3,2,1,0:T(8,128)S(1)}, f32[1,2,64,64]{3,2,1,0:T(8,128)}, u32[]{:S(2)}) copy-start(f32[1,2,64,64]{3,2,1,0:T(8,128)} %get-tuple-element.7) | copy-start | bytes 98308
  105.6 6.1 %copy-start.11 = (f32[1,2,64,64]{3,2,1,0:T(8,128)S(1)}, f32[1,2,64,64]{3,2,1,0:T(8,128)}, u32[]{:S(2)}) copy-start(f32[1,2,64,64]{3,2,1,0:T(8,128)} %get-tuple-element.14) | copy-start | bytes 98308
  105.6 6.4 %copy-start.10 = (f32[1,2,64,64]{3,2,1,0:T(8,128)S(1)}, f32[1,2,64,64]{3,2,1,0:T(8,128)}, u32[]{:S(2)}) copy-start(f32[1,2,64,64]{3,2,1,0:T(8,128)} %get-tuple-element.15) | copy-start | bytes 98308
  105.6 6.8 %copy-start.9 = (f32[1,2,64,64]{3,2,1,0:T(8,128)S(1)}, f32[1,2,64,64]{3,2,1,0:T(8,128)}, u32[]{:S(2)}) copy-start(f32[1,2,64,64]{3,2,1,0:T(8,128)} %get-tuple-element.12) | copy-start | bytes 98308
  158.9 10.9 %copy-start.2 = (bf16[64,64,128]{2,1,0:T(8,128)(2,1)S(1)}, bf16[64,64,128]{2,1,0:T(8,128)(2,1)}, u32[]{:S(2)}) copy-start(bf16[64,64,128]{2,1,0:T(8,128)(2,1)} %param.12) | copy-start | bytes 3145732
  160.4 9.9 %copy-start.1 = (bf16[512,16,128]{2,1,0:T(8,128)(2,1)S(1)}, bf16[512,16,128]{2,1,0:T(8,128)(2,1)}, u32[]{:S(2)}) copy-start(bf16[512,16,128]{2,1,0:T(8,128)(2,1)} %gather_fusion) | copy-start | bytes 6291460
Sparse Core Ops, SparseCore 0:
  17.1 71.1 all-gather.2

commit v3 on v2

--- a/solution.py
+++ b/solution.py
@@ -1,6 +1,7 @@
 import jax
 import jax.numpy as jnp
 from jax import lax
+from jax.experimental import pallas as pl
 from jax.sharding import PartitionSpec as P
 
 
@@ -17,7 +18,34 @@
     return value
 
 
-def body(
+def scatter_kernel(boxes_ref, values_ref, out_ref):
+    table = (
+        boxes_ref[...] == lax.broadcasted_iota(jnp.int32, (out_ref.shape[0], boxes_ref.shape[1]), 0)
+    ).astype(values_ref.dtype)
+    out_ref[...] = jnp.dot(table, values_ref[...], preferred_element_type=jnp.float32)
+
+
+def scatter_rows(boxes, values, count):
+    slots, width = values.shape
+    step = 256
+    return pl.pallas_call(
+        scatter_kernel,
+        grid=(width // step,),
+        in_specs=[
+            pl.BlockSpec((1, slots), lambda i: (0, 0)),
+            pl.BlockSpec((slots, step), lambda i: (0, i)),
+        ],
+        out_specs=pl.BlockSpec((count, step), lambda i: (0, i)),
+        out_shape=jax.ShapeDtypeStruct((count, width), jnp.float32),
+        cost_estimate=pl.CostEstimate(
+            flops=2 * count * slots * width,
+            bytes_accessed=slots * width * 2 + count * width * 4 + slots * 4,
+            transcendentals=0,
+        ),
+    )(boxes, values)
+
+
+def body_inner(
     charges,
     leaf_basis,
     leaf_up,
@@ -135,19 +163,16 @@
         near_blocks.reshape(leaf_count, near_count * panels, panels),
         preferred_element_type=jnp.float32,
     )
-
-    scatter_table = (
-        recv_boxes.reshape(1, devices * rows) == jnp.arange(leaf_count, dtype=jnp.int32)[:, None]
-    ).astype(jnp.bfloat16)
-    far = jnp.dot(
-        scatter_table,
+    tree_part = jnp.einsum("rk,bjk->brj", local_exp, leaf_up, precision=highest)
+    nearfield, tree_part = lax.optimization_barrier((nearfield, tree_part))
+
+    far = scatter_rows(
+        recv_boxes.reshape(1, devices * rows),
         received.reshape(devices * rows, flat_width),
-        preferred_element_type=jnp.float32,
+        leaf_count,
     )
     far = far.reshape(leaf_count, sides_rhs, ranks)
-    leaf_local = (jnp.einsum("rk,bjk->brj", local_exp, leaf_up, precision=highest) + far).astype(
-        jnp.bfloat16
-    )
+    leaf_local = (tree_part + far).astype(jnp.bfloat16)
     farfield = jnp.einsum(
         "brk,bkp->brp", leaf_local, leaf_basis, preferred_element_type=jnp.float32
     )
@@ -156,7 +181,7 @@
 
 def solution(mesh):
     return jax.shard_map(
-        body,
+        body_inner,
         mesh=mesh,
         in_specs=(
             P("leaf", None, None),

time: 186 us -> 171 us (0.919)
  waiting for transfers between devices: 39.7 us -> 24.4 us
  Pallas kernels: 0 us -> 4.41 us
  local copies, waits for them, and re-layouts: 50.9 us -> 46.8 us
    all_to_all x1, waiting for transfers between devices: 39.7 us -> 24.3 us  [body_inner(): lax.all_to_all(send_values, 'leaf', split_axis=0, concat_axis=0, tiled=True)]
    dot_general x2 -> x1, local copies, waits for them, and re-layouts: 6.68 us -> 0.14 us  [body_inner(): jnp.dot(slot_table.reshape(devices, rows, entries)[:, :capacity, :], box_...]
    pallas_call x0 -> x1, Pallas kernels: none -> 4.41 us  [scatter_rows(): pl.pallas_call(scatter_kernel, grid=(width // step,), in_specs=[pl.BlockS...]
    reshape x0 -> x2, local copies, waits for them, and re-layouts: none -> 2.58 us  [the longest x1 1.89 us: body_inner(): far = far.reshape(leaf_count, sides_rhs, ranks)]
    dot_general x30 -> x29, matrix products: 53.8 us -> 53.9 us  [the longest x1 10.7 us: body_inner(): jnp.einsum('crj,cjk->crk', picked, coupling_blocks, preferred_element_typ...]
    unnamed x40 -> x38, local copies, waits for them, and re-layouts: 24.1 us -> 24.1 us
  transfers between devices with their start and end apart: 4 -> 4, of which waited for: 1 -> 1; matrix products, arithmetic and copies ran while one was open for 46% -> 59% of each run, Pallas kernels for 0% -> 0%
where the time goes in v3:
time: 171 us; the launch traced here: 170 us
  matrix products  54.6 us (32%)
  local copies, waits for them, and re-layouts  46.8 us (27%)
  waiting for transfers between devices  24.4 us (14%)
  starting transfers between devices  20.5 us (12%)
  between operations  13.9 us (8%)
  other arithmetic  5.35 us (3%)
  Pallas kernels  4.41 us (3%)
    all_to_all x1, waiting for transfers between devices, body_inner(): lax.all_to_all(send_values, 'leaf', split_axis=0, concat_axis=0, tiled=True)  24.3 us
    unnamed x38, local copies, waits for them, and re-layouts  24.1 us
    all_to_all x1, starting transfers between devices, body_inner(): lax.all_to_all(send_values, 'leaf', split_axis=0, concat_axis=0, tiled=True)  13.9 us
    dot_general x1, matrix products, body_inner(): jnp.einsum('crj,cjk->crk', picked, coupling_blocks, preferred_element_typ...  10.7 us
    dot_general x1, matrix products, body_inner(): jnp.einsum('brm,bmp->brp', gathered, near_blocks.reshape(leaf_count, near...  9.51 us
    dot_general x1, matrix products, body_inner(): jnp.dot(slot_table, products.reshape(entries, flat_width), preferred_elem...  8.34 us
    dot_general x1, matrix products, body_inner(): jnp.dot(box_table, lane_place, preferred_element_type=jnp.float32)  6.26 us
    convert_element_type x1, local copies, waits for them, and re-layouts, body_inner(): picked = jnp.einsum('es,srj->erj', source_table, skeleton_low, preferred_...  6.19 us
  transfers between devices with their start and end apart: 4, of which 1 were waited for; matrix products, arithmetic and copies ran while one was open for 59% of the time, Pallas kernels for 0%

profile of v3, /device:TPU:1, one launch (start us, length us, event | category | flops | bytes accessed | tf_op | source)
XLA Modules:
  0.0 170.0 jit_solution(6955290457930622079)
XLA Ops:
  6.5 3.4 %collective-permute-start.1 = (bf16[64,16,128]{2,1,0:T(8,128)(2,1)}, bf16[64,16,128]{2,1,0:T(8,128)(2,1)}, u32[]{:S(2)}, u32[]{:S(2)}) collective-permute-start(bf16[64,16,128]{2,1,0:T(8,128)(2,1)} %param.11), channel_id=1, source_target_pairs={{1,0},{2,1},{3,2},{4,3},{5,4},{6,5},{7,6},{8,7},{9,8},{10,9},{11,1... | collective-permute-start | bytes 786440 | tf_op jit(solution)/shard_map/ppermute | solution.py:16
  10.0 3.2 %collective-permute-start = (bf16[64,16,128]{2,1,0:T(8,128)(2,1)}, bf16[64,16,128]{2,1,0:T(8,128)(2,1)}, u32[]{:S(2)}, u32[]{:S(2)}) collective-permute-start(bf16[64,16,128]{2,1,0:T(8,128)(2,1)} %param.11), channel_id=1, source_target_pairs={{0,1},{1,2},{2,3},{3,4},{4,5},{5,6},{6,7},{7,8},{8,9},{9,10},{10,1... | collective-permute-start | bytes 786440 | tf_op jit(solution)/shard_map/ppermute | solution.py:15
  13.2 2.0 %fusion.99 = (bf16[64,16,64]{2,1,0:T(8,128)(2,1)S(1)}, f32[64,16,64]{2,1,0:T(8,128)S(1)}) fusion(bf16[64,16,128]{2,1,0:T(8,128)(2,1)} %param.11, bf16[64,64,128]{2,1,0:T(8,128)(2,1)} %param.12), kind=kOutput, calls=%fused_computation.135 | convolution fusion | flops 16842752 | bytes 1703936 | tf_op jit(solution)/shard_map/bkp,brp->brk/dot_general | solution.py:100
  15.1 1.2 convolution_bitcast_fusion.2
  16.4 0.6 concatenate.7
  17.3 0.7 fusion.20
  18.0 1.7 convert_element_type.42
  19.7 6.2 %copy.37 = bf16[1024,16,64]{2,1,0:T(8,128)(2,1)} copy(bf16[1024,16,64]{0,2,1:T(8,128)(2,1)} %convert_element_type.42) | data formatting | bytes 4194304 | tf_op jit(solution)/shard_map/convert_element_type | solution.py:109
  25.9 23.9 %copy.38 = bf16[1024,64,64]{2,1,0:T(8,128)(2,1)} copy(bf16[1024,64,64]{0,2,1:T(8,128)(2,1)} %param.18) | data formatting | bytes 16777216 | tf_op args[7]
  49.9 10.7 %convolution_convert_fusion = bf16[1024,16,64]{2,1,0:T(8,128)(2,1)} fusion(bf16[1024,16,64]{2,1,0:T(8,128)(2,1)} %copy.37, bf16[1024,64,64]{2,1,0:T(8,128)(2,1)} %copy.38), kind=kOutput, calls=%fused_computation.8 | convolution fusion | flops 135266304 | bytes 12582912 | tf_op jit(solution)/shard_map/crj,cjk->crk/dot_general | solution.py:110
  60.6 5.5 %copy.39 = bf16[1024,16,64]{0,2,1:T(8,128)(2,1)} copy(bf16[1024,16,64]{2,1,0:T(8,128)(2,1)} %convolution_convert_fusion) | data formatting | bytes 4194304 | tf_op jit(solution)/shard_map/convert_element_type | solution.py:112
  67.0 8.3 %fusion = f32[2048,1024]{1,0:T(8,128)} fusion(bf16[1024,1024]{0,1:T(8,128)(2,1)} %bitcast.178, s32[1024]{0:T(1024)S(1)} %multiply_add_fusion.1), kind=kOutput, calls=%fused_computation.3 | convolution fusion | flops 4297064448 | bytes 10489856 | tf_op jit(solution)/shard_map/dot_general | solution.py:113
  75.3 1.3 broadcast_compare_fusion
  76.7 2.2 %fusion.1 = bf16[1,128,12]{1,0,2:T(2,128)(2,1)S(1)} fusion(bf16[1024,1,1]{0,1,2:T(2,128)(2,1)S(1)} %reshape.162, pred[128,12,1024]{2,1,0:T(8,128)(4,1)S(1)} %broadcast_compare_fusion), kind=kOutput, calls=%fused_computation.4 | convolution fusion | flops 3145728 | bytes 1577984 | tf_op jit(solution)/shard_map/dot_general | solution.py:85
  79.5 6.3 %add_convert_fusion = bf16[2048,1024]{1,0:T(8,128)(2,1)} fusion(f32[2048,1024]{1,0:T(8,128)} %fusion, bf16[2048,128]{1,0:T(8,128)(2,1)S(1)} %fusion.8), kind=kOutput, calls=%fused_computation.1 | convolution fusion | flops 541196288 | bytes 13107200 | tf_op jit(solution)/shard_map/dot_general | solution.py:115
  85.7 13.9 %all-to-all-start = ((bf16[128,16,1024]{2,1,0:T(8,128)(2,1)}), bf16[128,16,1024]{2,1,0:T(8,128)(2,1)}, u32[]{:S(2)}, u32[]{:S(2)}) async-start(bf16[128,16,1024]{2,1,0:T(8,128)(2,1)} %bitcast.172), calls=%async_computation | async-start | bytes 8388608 | tf_op jit(solution)/shard_map/all_to_all | solution.py:117
  99.9 0.8 fusion.98
  100.9 0.7 fusion.97
  101.6 1.2 pad_maximum_fusion
  102.8 2.8 %gather_fusion = bf16[512,16,128]{2,1,0:T(8,128)(2,1)} fusion(bf16[192,16,128]{2,1,0:T(8,128)(2,1)S(1)} %pad_maximum_fusion, s32[1024]{0:T(1024)S(1)} %pad_clamp_fusion), kind=kCustom, calls=%fused_computation | custom fusion | bytes 4196352 | tf_op jit(solution)/shard_map/gather | solution.py:156
  105.6 9.5 %fusion.4 = f32[64,16,128]{2,1,0:T(8,128)} fusion(bf16[64,1024,128]{2,1,0:T(8,128)(2,1)} %bitcast.171, bf16[64,8,2,8,128]{4,3,2,1,0:T(8,128)(2,1)} %bitcast.174), kind=kOutput, calls=%fused_computation.9 | convolution fusion | flops 268435456 | bytes 19398656 | tf_op jit(solution)/shard_map/brm,bmp->brp/dot_general | solution.py:160
  115.2 1.5 slice.84
  116.7 1.6 fusion.9
  118.2 0.6 fusion.13
  118.9 0.4 fusion.17
  122.2 5.8 %convolution_bitcast_fusion = f32[64,16,64]{2,1,0:T(8,128)} fusion(f32[16,64,1]{1,0,2:T(8,128)S(1)} %fusion.7, f32[64,64,64]{2,1,0:T(8,128)S(1)} %copy-done), kind=kOutput, calls=%fused_computation.13 | convolution fusion | flops 50331648 | bytes 1314816 | tf_op jit(solution)/shard_map/rk,bjk->brj/dot_general | solution.py:166
  128.0 24.3 %all-to-all-done = bf16[128,16,1024]{2,1,0:T(8,128)(2,1)} async-done(((bf16[128,16,1024]{2,1,0:T(8,128)(2,1)}), bf16[128,16,1024]{2,1,0:T(8,128)(2,1)}, u32[]{:S(2)}, u32[]{:S(2)}) %all-to-all-start) | async-done | bytes 4194336 | tf_op jit(solution)/shard_map/all_to_all | solution.py:117
  152.4 1.0 slice.88
  153.7 0.7 reshape.132.boxes_ref
  154.3 4.4 %shard_map.109 = f32[64,1024]{1,0:T(8,128)} custom-call(s32[1,2048]{1,0:T(1,128)} %reshape.132.boxes_ref, bf16[2048,1024]{1,0:T(8,128)(2,1)} %bitcast.70.values_ref), custom_call_target="tpu_custom_call" | custom-call | flops 268435456 | bytes 4464640 | tf_op jit(solution)/shard_map/pallas_call | solution.py:31
  158.8 1.9 %reshape.134 = f32[64,16,64]{2,1,0:T(8,128)} reshape(f32[64,1024]{1,0:T(8,128)} %shard_map.109) | data formatting | bytes 524288 | tf_op jit(solution)/shard_map/reshape | solution.py:174
  160.7 2.5 %convolution_add_fusion = f32[64,16,128]{2,1,0:T(8,128)} fusion(f32[64,16,128]{2,1,0:T(8,128)} %fusion.4, bf16[64,64,128]{2,1,0:T(8,128)(2,1)S(1)} %copy-done.1, f32[64,16,64]{2,1,0:T(8,128)} %convolution_bitcast_fusion, f32[64,16,64]{2,1,0:T(8,128)} %reshape.134), kind=kOutput, calls=%fused_computation.12 | convolution fusion | flops 17039360 | bytes 2621440 | tf_op jit(solution)/shard_map/brk,bkp->brp/dot_general | solution.py:176
  (87 shorter events, 5.3 us)
Async XLA Ops:
  6.5 8.6 %copy-start = (f32[64,64,64]{2,1,0:T(8,128)S(1)}, f32[64,64,64]{2,1,0:T(8,128)}, u32[]{:S(2)}) copy-start(f32[64,64,64]{2,1,0:T(8,128)} %param.13) | copy-start | bytes 3145732
  6.5 10.8 %copy-start.15 = (s32[1024]{0:T(1024)S(1)}, s32[1024]{0:T(1024)}, u32[]{:S(2)}) copy-start(s32[1024]{0:T(1024)} %param.19) | copy-start | bytes 12292
  6.5 108.7 %all-gather.3.cloned.1.call-start = ((), (), s32[]{:S(2)}) async-start(), calls=%async_computation.1 | async-start | bytes 2113536 | tf_op jit(solution)/shard_map/all_gather | solution.py:124
  6.5 95.1 %collective-permute-start.1 = (bf16[64,16,128]{2,1,0:T(8,128)(2,1)}, bf16[64,16,128]{2,1,0:T(8,128)(2,1)}, u32[]{:S(2)}, u32[]{:S(2)}) collective-permute-start(bf16[64,16,128]{2,1,0:T(8,128)(2,1)} %param.11), channel_id=1, source_target_pairs={{1,0},{2,1},{3,2},{4,3},{5,4},{6,5},{7,6},{8,7},{9,8},{10,9},{11,1... | collective-permute-start | bytes 786440 | tf_op jit(solution)/shard_map/ppermute | solution.py:16
  10.0 91.7 %collective-permute-start = (bf16[64,16,128]{2,1,0:T(8,128)(2,1)}, bf16[64,16,128]{2,1,0:T(8,128)(2,1)}, u32[]{:S(2)}, u32[]{:S(2)}) collective-permute-start(bf16[64,16,128]{2,1,0:T(8,128)(2,1)} %param.11), channel_id=1, source_target_pairs={{0,1},{1,2},{2,3},{3,4},{4,5},{5,6},{6,7},{7,8},{8,9},{9,10},{10,1... | collective-permute-start | bytes 786440 | tf_op jit(solution)/shard_map/ppermute | solution.py:15
  60.6 5.5 %copy-start.14 = (s32[1024,1]{0,1:T(1,128)S(1)}, s32[1024,1]{0,1:T(1,128)}, u32[]{:S(2)}) copy-start(s32[1024,1]{0,1:T(1,128)} %param.20) | copy-start | bytes 12292
  60.6 6.4 %copy-start.16 = (s32[1024]{0:T(1024)S(1)}, s32[1024]{0:T(1024)}, u32[]{:S(2)}) copy-start(s32[1024]{0:T(1024)} %param.21) | copy-start | bytes 12292
  85.7 13.9 %copy-start.17 = (s32[64,8]{0,1:T(8,128)S(1)}, s32[64,8]{0,1:T(8,128)}, u32[]{:S(2)}) copy-start(s32[64,8]{0,1:T(8,128)} %param.17) | copy-start | bytes 6148
  85.7 14.1 %copy-start.2 = (f32[7,2,64,64]{3,2,1,0:T(8,128)S(1)}, f32[7,2,64,64]{3,2,1,0:T(8,128)}, u32[]{:S(2)}) copy-start(f32[7,2,64,64]{3,2,1,0:T(8,128)} %param.14) | copy-start | bytes 688132
  85.7 15.2 %copy-start.3 = (f32[7,2,64,64]{3,2,1,0:T(8,128)S(1)}, f32[7,2,64,64]{3,2,1,0:T(8,128)}, u32[]{:S(2)}) copy-start(f32[7,2,64,64]{3,2,1,0:T(8,128)} %param.15) | copy-start | bytes 688132
  85.7 66.6 %all-to-all-start = ((bf16[128,16,1024]{2,1,0:T(8,128)(2,1)}), bf16[128,16,1024]{2,1,0:T(8,128)(2,1)}, u32[]{:S(2)}, u32[]{:S(2)}) async-start(bf16[128,16,1024]{2,1,0:T(8,128)(2,1)} %bitcast.172), calls=%async_computation | async-start | bytes 8388608 | tf_op jit(solution)/shard_map/all_to_all | solution.py:117
  115.1 5.0 %copy-start.7 = (f32[1,2,64,64]{3,2,1,0:T(8,128)S(1)}, f32[1,2,64,64]{3,2,1,0:T(8,128)}, u32[]{:S(2)}) copy-start(f32[1,2,64,64]{3,2,1,0:T(8,128)} %get-tuple-element.14) | copy-start | bytes 98308
  115.1 5.1 %copy-start.13 = (f32[1,2,64,64]{3,2,1,0:T(8,128)S(1)}, f32[1,2,64,64]{3,2,1,0:T(8,128)}, u32[]{:S(2)}) copy-start(f32[1,2,64,64]{3,2,1,0:T(8,128)} %get-tuple-element.21) | copy-start | bytes 98308
  115.1 5.3 %copy-start.6 = (f32[1,2,64,64]{3,2,1,0:T(8,128)S(1)}, f32[1,2,64,64]{3,2,1,0:T(8,128)}, u32[]{:S(2)}) copy-start(f32[1,2,64,64]{3,2,1,0:T(8,128)} %get-tuple-element.13) | copy-start | bytes 98308
  115.1 5.5 %copy-start.12 = (f32[1,2,64,64]{3,2,1,0:T(8,128)S(1)}, f32[1,2,64,64]{3,2,1,0:T(8,128)}, u32[]{:S(2)}) copy-start(f32[1,2,64,64]{3,2,1,0:T(8,128)} %get-tuple-element.22) | copy-start | bytes 98308
  115.1 5.6 %copy-start.5 = (f32[1,2,64,64]{3,2,1,0:T(8,128)S(1)}, f32[1,2,64,64]{3,2,1,0:T(8,128)}, u32[]{:S(2)}) copy-start(f32[1,2,64,64]{3,2,1,0:T(8,128)} %get-tuple-element.12) | copy-start | bytes 98308
  115.1 5.8 %copy-start.11 = (f32[1,2,64,64]{3,2,1,0:T(8,128)S(1)}, f32[1,2,64,64]{3,2,1,0:T(8,128)}, u32[]{:S(2)}) copy-start(f32[1,2,64,64]{3,2,1,0:T(8,128)} %get-tuple-element.17) | copy-start | bytes 98308
  115.1 5.9 %copy-start.4 = (f32[1,2,64,64]{3,2,1,0:T(8,128)S(1)}, f32[1,2,64,64]{3,2,1,0:T(8,128)}, u32[]{:S(2)}) copy-start(f32[1,2,64,64]{3,2,1,0:T(8,128)} %get-tuple-element.11) | copy-start | bytes 98308
  115.2 6.1 %copy-start.10 = (f32[1,2,64,64]{3,2,1,0:T(8,128)S(1)}, f32[1,2,64,64]{3,2,1,0:T(8,128)}, u32[]{:S(2)}) copy-start(f32[1,2,64,64]{3,2,1,0:T(8,128)} %get-tuple-element.18) | copy-start | bytes 98308
  115.2 6.4 %copy-start.9 = (f32[1,2,64,64]{3,2,1,0:T(8,128)S(1)}, f32[1,2,64,64]{3,2,1,0:T(8,128)}, u32[]{:S(2)}) copy-start(f32[1,2,64,64]{3,2,1,0:T(8,128)} %get-tuple-element.19) | copy-start | bytes 98308
  115.2 6.7 %copy-start.8 = (f32[1,2,64,64]{3,2,1,0:T(8,128)S(1)}, f32[1,2,64,64]{3,2,1,0:T(8,128)}, u32[]{:S(2)}) copy-start(f32[1,2,64,64]{3,2,1,0:T(8,128)} %get-tuple-element.16) | copy-start | bytes 98308
  121.7 38.9 %copy-start.1 = (bf16[64,64,128]{2,1,0:T(8,128)(2,1)S(1)}, bf16[64,64,128]{2,1,0:T(8,128)(2,1)}, u32[]{:S(2)}) copy-start(bf16[64,64,128]{2,1,0:T(8,128)(2,1)} %param.12) | copy-start | bytes 3145732
Sparse Core Ops, SparseCore 0:
  17.1 71.1 all-gather.2

commit v4 on v3

--- a/solution.py
+++ b/solution.py
@@ -27,7 +27,7 @@
 
 def scatter_rows(boxes, values, count):
     slots, width = values.shape
-    step = 256
+    step = 512
     return pl.pallas_call(
         scatter_kernel,
         grid=(width // step,),
@@ -82,20 +82,10 @@
         jnp.arange(devices * rows, dtype=jnp.int32)[:, None] == slot_flat[None, :]
     ).astype(jnp.bfloat16)
     box_plus = (coup_box + 1).astype(jnp.bfloat16)
-    box_slots = jnp.dot(
-        slot_table.reshape(devices, rows, entries)[:, :capacity, :],
-        box_plus,
-        preferred_element_type=jnp.float32,
+    box_slots = jnp.dot(slot_table, box_plus, preferred_element_type=jnp.float32)
+    box_slots = jnp.where(
+        jnp.arange(rows, dtype=jnp.int32)[None, :] < capacity, box_slots.reshape(devices, rows), 0.0
     )
-    lanes = -(-capacity // 128) * 128
-    box_table = jnp.where(
-        jnp.arange(rows, dtype=jnp.int32)[None, :, None] == capacity,
-        jnp.pad(box_slots, ((0, 0), (0, lanes - capacity)))[:, None, :],
-        0.0,
-    ).astype(jnp.bfloat16).reshape(devices * rows, lanes)
-    lane_place = (
-        jnp.arange(lanes, dtype=jnp.int32)[:, None] == jnp.arange(flat_width, dtype=jnp.int32)[None, :]
-    ).astype(jnp.bfloat16)
 
     skeleton = jnp.einsum("bkp,brp->brk", leaf_basis, charges, preferred_element_type=jnp.float32)
     skeleton_low = skeleton.astype(jnp.bfloat16)
@@ -112,18 +102,25 @@
     ).astype(jnp.bfloat16)
     send_values = jnp.dot(
         slot_table, products.reshape(entries, flat_width), preferred_element_type=jnp.float32
-    ) + jnp.dot(box_table, lane_place, preferred_element_type=jnp.float32)
-    send_values = send_values.astype(jnp.bfloat16).reshape(devices, rows, flat_width)
-    received = lax.all_to_all(send_values, "leaf", split_axis=0, concat_axis=0, tiled=True)
-    recv_boxes = jnp.where(
-        jnp.arange(rows, dtype=jnp.int32)[None, :] < capacity,
-        jnp.pad(received[:, capacity, :capacity], ((0, 0), (0, rows - capacity))).astype(jnp.int32),
-        0,
-    ) - 1
+    ).astype(jnp.bfloat16)
+    received = lax.all_to_all(
+        send_values.reshape(devices, rows, flat_width),
+        "leaf",
+        split_axis=0,
+        concat_axis=0,
+        tiled=True,
+    )
 
-    boxes_all = lax.all_gather(
-        jnp.concatenate([own_box, jnp.zeros_like(own_box)], axis=0), "leaf", axis=0, tiled=False
-    )[:, :sides_rhs]
+    gathered = lax.all_gather(
+        jnp.concatenate([own_box, box_slots.reshape(-1, ranks)], axis=0), "leaf", axis=0, tiled=False
+    )
+    boxes_all = gathered[:, :sides_rhs]
+    recv_boxes = (
+        lax.dynamic_index_in_dim(
+            gathered[:, sides_rhs:].reshape(devices, devices, rows), device_pos, 1, keepdims=False
+        ).astype(jnp.int32)
+        - 1
+    )
     upward = boxes_all
     ups = []
     for level in range(levels):

time: 171 us -> 161 us (0.942)
  waiting for transfers between devices: 24.4 us -> 0.03 us
  local copies, waits for them, and re-layouts: 46.8 us -> 54.7 us
  matrix products: 54.6 us -> 62.3 us
    all_to_all x1, waiting for transfers between devices: 24.3 us -> 0.01 us  [body_inner(): lax.all_to_all(send_values.reshape(devices, rows, flat_width), 'leaf', sp...]
    convert_element_type x2 -> x0, local copies, waits for them, and re-layouts: 6.48 us -> none  [the longest x1 6.19 us: body_inner(): picked = jnp.einsum('es,srj->erj', source_table, skeleton_low, preferred_...]
    dot_general x1, local copies, waits for them, and re-layouts: 0.14 us -> 6.18 us  [body_inner(): jnp.einsum('es,srj->erj', source_table, skeleton_low, preferred_element_t...]
    slice x2 -> x3, local copies, waits for them, and re-layouts: 2.48 us -> 8.1 us  [the longest x2 6.79 us: body_inner(): gathered[:, sides_rhs:].reshape(devices, devices, rows)]
    dot_general x6, matrix products: 3.32 us -> 8.35 us  [body_inner(): jnp.einsum('nsrj,sjk->nrk', paired, top_up[level], precision=highest)]
    dot_general x2, matrix products: 8.42 us -> 3.62 us  [the longest x1 2.17 us: body_inner(): jnp.einsum('es,srj->erj', source_table, skeleton_low, preferred_element_t...]
    dot_general x7, matrix products: 1.13 us -> 5.71 us  [body_inner(): jnp.dot(sibling, lax.dynamic_index_in_dim(top_coupling[level], node_side,...]
    dot_general x7, matrix products: 1.02 us -> 5.59 us  [body_inner(): jnp.dot(local_exp, lax.dynamic_index_in_dim(top_up[level], node_side, 0,...]
  transfers between devices with their start and end apart: 4 -> 4, of which waited for: 1 -> 0; matrix products, arithmetic and copies ran while one was open for 59% -> 73% of each run, Pallas kernels for 0% -> 0%
where the time goes in v4:
time: 161 us; the launch traced here: 159 us
  matrix products  62.3 us (39%)
  local copies, waits for them, and re-layouts  54.7 us (34%)
  starting transfers between devices  20.7 us (13%)
  between operations  13.7 us (9%)
  other arithmetic  3.82 us (2%)
  Pallas kernels  3.48 us (2%)
    unnamed x19, local copies, waits for them, and re-layouts  24.8 us
    all_to_all x1, starting transfers between devices, body_inner(): lax.all_to_all(send_values.reshape(devices, rows, flat_width), 'leaf', sp...  14.1 us
    dot_general x1, matrix products, body_inner(): jnp.einsum('crj,cjk->crk', picked, coupling_blocks, preferred_element_typ...  10.7 us
    dot_general x1, matrix products, body_inner(): jnp.einsum('brm,bmp->brp', gathered, near_blocks.reshape(leaf_count, near...  9.51 us
    dot_general x6, matrix products, body_inner(): jnp.einsum('nsrj,sjk->nrk', paired, top_up[level], precision=highest)  8.35 us
    dot_general x1, matrix products, body_inner(): jnp.dot(slot_table, products.reshape(entries, flat_width), preferred_elem...  7.68 us
    slice x2, local copies, waits for them, and re-layouts, body_inner(): gathered[:, sides_rhs:].reshape(devices, devices, rows)  6.79 us
    dot_general x1, local copies, waits for them, and re-layouts, body_inner(): jnp.einsum('es,srj->erj', source_table, skeleton_low, preferred_element_t...  6.18 us
  transfers between devices with their start and end apart: 4, of which 0 were waited for; matrix products, arithmetic and copies ran while one was open for 73% of the time, Pallas kernels for 0%

profile of v4, /device:TPU:1, one launch (start us, length us, event | category | flops | bytes accessed | tf_op | source)
XLA Modules:
  0.0 158.8 jit_solution(16292302262393424738)
XLA Ops:
  6.5 3.4 %collective-permute-start.1 = (bf16[64,16,128]{2,1,0:T(8,128)(2,1)}, bf16[64,16,128]{2,1,0:T(8,128)(2,1)}, u32[]{:S(2)}, u32[]{:S(2)}) collective-permute-start(bf16[64,16,128]{2,1,0:T(8,128)(2,1)} %param.11), channel_id=1, source_target_pairs={{1,0},{2,1},{3,2},{4,3},{5,4},{6,5},{7,6},{8,7},{9,8},{10,9},{11,1... | collective-permute-start | bytes 786440 | tf_op jit(solution)/shard_map/ppermute | solution.py:16
  10.0 3.2 %collective-permute-start = (bf16[64,16,128]{2,1,0:T(8,128)(2,1)}, bf16[64,16,128]{2,1,0:T(8,128)(2,1)}, u32[]{:S(2)}, u32[]{:S(2)}) collective-permute-start(bf16[64,16,128]{2,1,0:T(8,128)(2,1)} %param.11), channel_id=1, source_target_pairs={{0,1},{1,2},{2,3},{3,4},{4,5},{5,6},{6,7},{7,8},{8,9},{9,10},{10,1... | collective-permute-start | bytes 786440 | tf_op jit(solution)/shard_map/ppermute | solution.py:15
  15.6 1.5 fusion.1
  17.1 1.6 %fusion.107 = (bf16[64,16,64]{2,1,0:T(8,128)(2,1)S(1)}, f32[64,16,64]{2,1,0:T(8,128)S(1)}) fusion(bf16[64,16,128]{2,1,0:T(8,128)(2,1)} %param.11, bf16[64,64,128]{2,1,0:T(8,128)(2,1)S(1)} %copy-done.1), kind=kOutput, calls=%fused_computation.135 | convolution fusion | flops 16842752 | bytes 1703936 | tf_op jit(solution)/shard_map/bkp,brp->brk/dot_general | solution.py:90
  18.8 1.2 convolution_bitcast_fusion.2
  20.6 2.2 %fusion.23 = bf16[1024,16,64]{0,2,1:T(8,128)(2,1)} fusion(bf16[64,16,64]{2,1,0:T(8,128)(2,1)S(1)} %get-tuple-element.23, s32[1024]{0:T(1024)S(1)} %copy-done.7), kind=kOutput, calls=%fused_computation.40 | convolution fusion | flops 134283264 | bytes 2232320 | tf_op jit(solution)/shard_map/es,srj->erj/dot_general | solution.py:97
  22.8 6.2 %copy.35 = bf16[1024,16,64]{2,1,0:T(8,128)(2,1)} copy(bf16[1024,16,64]{0,2,1:T(8,128)(2,1)} %fusion.23) | data formatting | bytes 4194304 | tf_op jit(solution)/shard_map/es,srj->erj/dot_general | solution.py:97
  29.0 24.0 %copy.26 = bf16[1024,64,64]{2,1,0:T(8,128)(2,1)} copy(bf16[1024,64,64]{0,2,1:T(8,128)(2,1)} %param.18) | data formatting | bytes 16777216 | tf_op args[7]
  52.9 10.7 %fusion.7 = bf16[1024,16,64]{2,1,0:T(8,128)(2,1)} fusion(bf16[1024,64,64]{2,1,0:T(8,128)(2,1)} %copy.26, bf16[1024,16,64]{2,1,0:T(8,128)(2,1)} %copy.35), kind=kOutput, calls=%fused_computation.9 | convolution fusion | flops 135266304 | bytes 12582912 | tf_op jit(solution)/shard_map/crj,cjk->crk/dot_general | solution.py:100
  63.6 5.5 %copy.27 = bf16[1024,16,64]{0,2,1:T(8,128)(2,1)} copy(bf16[1024,16,64]{2,1,0:T(8,128)(2,1)} %fusion.7) | data formatting | bytes 4194304 | tf_op jit(solution)/shard_map/convert_element_type | solution.py:102
  69.1 7.7 %fusion.6 = bf16[2048,1024]{1,0:T(8,128)(2,1)} fusion(bf16[1024,1024]{0,1:T(8,128)(2,1)} %bitcast.175, s32[1024]{0:T(1024)S(1)} %multiply_add_fusion), kind=kOutput, calls=%fused_computation.8 | convolution fusion | flops 4299161600 | bytes 6295552 | tf_op jit(solution)/shard_map/dot_general | solution.py:103
  76.8 14.1 %all-to-all-start = ((bf16[128,16,1024]{2,1,0:T(8,128)(2,1)}), bf16[128,16,1024]{2,1,0:T(8,128)(2,1)}, u32[]{:S(2)}, u32[]{:S(2)}) async-start(bf16[128,16,1024]{2,1,0:T(8,128)(2,1)} %bitcast.170), calls=%async_computation | async-start | bytes 8388608 | tf_op jit(solution)/shard_map/all_to_all | solution.py:106
  92.1 1.8 %fusion.105 = (f32[1,2,64,64]{3,2,1,0:T(8,128)S(1)}, f32[1,2,64,64]{3,2,1,0:T(8,128)}, f32[1,2,64,64]{3,2,1,0:T(8,128)}, f32[1,2,64,64]{3,2,1,0:T(8,128)}, f32[1...) fusion(f32[7,2,64,64]{3,2,1,0:T(8,128)} %param.15), kind=kLoop, calls=%fused_computation.133 | loop fusion | bytes 458752 | tf_op jit(solution)/shard_map/slice | solution.py:139
  94.0 1.1 pad_maximum_fusion
  95.1 2.8 %gather_fusion = bf16[512,16,128]{2,1,0:T(8,128)(2,1)} fusion(bf16[192,16,128]{2,1,0:T(8,128)(2,1)S(1)} %pad_maximum_fusion, s32[1024]{0:T(1024)S(1)} %pad_clamp_fusion), kind=kCustom, calls=%fused_computation | custom fusion | bytes 4196352 | tf_op jit(solution)/shard_map/gather | solution.py:153
  97.8 9.5 %fusion.10 = f32[64,16,128]{2,1,0:T(8,128)} fusion(bf16[64,1024,128]{2,1,0:T(8,128)(2,1)} %bitcast.167, bf16[64,8,2,8,128]{4,3,2,1,0:T(8,128)(2,1)} %bitcast.168), kind=kOutput, calls=%fused_computation.10 | convolution fusion | flops 268435456 | bytes 19398656 | tf_op jit(solution)/shard_map/brm,bmp->brp/dot_general | solution.py:157
  107.4 1.3 slice.82
  108.7 3.1 %slice.83 = f32[128,32,64]{2,1,0:T(8,128)} slice(f32[128,48,64]{2,1,0:T(8,128)} %bitcast.172), slice={[0:128], [16:48], [0:64]} | slice | bytes 2097152 | tf_op jit(solution)/shard_map/slice | solution.py:120
  111.8 3.7 %copy.24 = f32[128,32,64]{0,2,1:T(8,128)} copy(f32[128,32,64]{2,1,0:T(8,128)} %slice.83) | data formatting | bytes 2097152 | tf_op jit(solution)/shard_map/slice | solution.py:120
  115.5 2.4 %fusion.14 = f32[64,16,64,1]{2,0,3,1:T(8,128)S(1)} fusion(f32[64,2,16,64]{3,2,1,0:T(8,128)S(1)} %bitcast.169, f32[7,2,64,64]{3,2,1,0:T(8,128)} %param.14), kind=kOutput, calls=%fused_computation.25 | convolution fusion | flops 100663296 | bytes 851968 | tf_op jit(solution)/shard_map/nsrj,sjk->nrk/dot_general | solution.py:131
  118.7 1.4 fusion.18
  122.5 1.3 fusion.26
  123.8 1.1 fusion.33
  124.9 1.1 fusion.31
  126.0 1.1 convolution_bitcast_fusion.1
  128.9 0.9 convolution_add_fusion.6
  130.7 0.9 convolution_add_fusion.5
  134.4 0.9 convolution_add_fusion.3
  138.2 5.8 %convolution_bitcast_fusion = f32[64,16,64]{2,1,0:T(8,128)} fusion(f32[16,64,1]{1,0,2:T(8,128)S(1)} %fusion.13, f32[64,64,64]{2,1,0:T(8,128)S(1)} %copy-done), kind=kOutput, calls=%fused_computation.14 | convolution fusion | flops 50331648 | bytes 1314816 | tf_op jit(solution)/shard_map/rk,bjk->brj/dot_general | solution.py:163
  144.1 3.5 %shard_map.109 = f32[64,1024]{1,0:T(8,128)} custom-call(s32[1,2048]{1,0:T(1,128)} %sub.23.boxes_ref, bf16[2048,1024]{1,0:T(8,128)(2,1)} %bitcast.68.values_ref), custom_call_target="tpu_custom_call" | custom-call | flops 268435456 | bytes 4464640 | tf_op jit(solution)/shard_map/pallas_call | solution.py:31
  147.6 1.9 %reshape.134 = f32[64,16,64]{2,1,0:T(8,128)} reshape(f32[64,1024]{1,0:T(8,128)} %shard_map.109) | data formatting | bytes 524288 | tf_op jit(solution)/shard_map/reshape | solution.py:171
  149.4 2.5 %convolution_add_fusion = f32[64,16,128]{2,1,0:T(8,128)} fusion(f32[64,16,128]{2,1,0:T(8,128)} %fusion.10, bf16[64,64,128]{2,1,0:T(8,128)(2,1)S(1)} %copy-done.2, f32[64,16,64]{2,1,0:T(8,128)} %convolution_bitcast_fusion, f32[64,16,64]{2,1,0:T(8,128)} %reshape.134), kind=kOutput, calls=%fused_computation.13 | convolution fusion | flops 17039360 | bytes 2621440 | tf_op jit(solution)/shard_map/brk,bkp->brp/dot_general | solution.py:173
  (62 shorter events, 15.8 us)
Async XLA Ops:
  6.5 12.2 %copy-start = (f32[64,64,64]{2,1,0:T(8,128)S(1)}, f32[64,64,64]{2,1,0:T(8,128)}, u32[]{:S(2)}) copy-start(f32[64,64,64]{2,1,0:T(8,128)} %param.13) | copy-start | bytes 3145732
  6.5 8.7 %copy-start.6 = (s32[1024,1]{0,1:T(1,128)S(1)}, s32[1024,1]{0,1:T(1,128)}, u32[]{:S(2)}) copy-start(s32[1024,1]{0,1:T(1,128)} %param.20) | copy-start | bytes 12292
  6.5 100.8 %all-gather.3.cloned.1.call-start = ((), (), s32[]{:S(2)}) async-start(), calls=%async_computation.1 | async-start | bytes 3170304 | tf_op jit(solution)/shard_map/all_gather | solution.py:114
  6.5 87.4 %collective-permute-start.1 = (bf16[64,16,128]{2,1,0:T(8,128)(2,1)}, bf16[64,16,128]{2,1,0:T(8,128)(2,1)}, u32[]{:S(2)}, u32[]{:S(2)}) collective-permute-start(bf16[64,16,128]{2,1,0:T(8,128)(2,1)} %param.11), channel_id=1, source_target_pairs={{1,0},{2,1},{3,2},{4,3},{5,4},{6,5},{7,6},{8,7},{9,8},{10,9},{11,1... | collective-permute-start | bytes 786440 | tf_op jit(solution)/shard_map/ppermute | solution.py:16
  10.0 84.0 %collective-permute-start = (bf16[64,16,128]{2,1,0:T(8,128)(2,1)}, bf16[64,16,128]{2,1,0:T(8,128)(2,1)}, u32[]{:S(2)}, u32[]{:S(2)}) collective-permute-start(bf16[64,16,128]{2,1,0:T(8,128)(2,1)} %param.11), channel_id=1, source_target_pairs={{0,1},{1,2},{2,3},{3,4},{4,5},{5,6},{6,7},{7,8},{8,9},{9,10},{10,1... | collective-permute-start | bytes 786440 | tf_op jit(solution)/shard_map/ppermute | solution.py:15
  15.2 1.9 %copy-start.1 = (bf16[64,64,128]{2,1,0:T(8,128)(2,1)S(1)}, bf16[64,64,128]{2,1,0:T(8,128)(2,1)}, u32[]{:S(2)}) copy-start(bf16[64,64,128]{2,1,0:T(8,128)(2,1)} %param.12) | copy-start | bytes 3145732
  17.1 3.5 %copy-start.7 = (s32[1024]{0:T(1024)S(1)}, s32[1024]{0:T(1024)}, u32[]{:S(2)}) copy-start(s32[1024]{0:T(1024)} %param.19) | copy-start | bytes 12292
  76.8 14.1 %copy-start.8 = (s32[64,8]{0,1:T(8,128)S(1)}, s32[64,8]{0,1:T(8,128)}, u32[]{:S(2)}) copy-start(s32[64,8]{0,1:T(8,128)} %param.17) | copy-start | bytes 6148
  76.8 14.3 %copy-start.4 = (f32[7,2,64,64]{3,2,1,0:T(8,128)S(1)}, f32[7,2,64,64]{3,2,1,0:T(8,128)}, u32[]{:S(2)}) copy-start(f32[7,2,64,64]{3,2,1,0:T(8,128)} %param.14) | copy-start | bytes 688132
  76.8 67.3 %all-to-all-start = ((bf16[128,16,1024]{2,1,0:T(8,128)(2,1)}), bf16[128,16,1024]{2,1,0:T(8,128)(2,1)}, u32[]{:S(2)}, u32[]{:S(2)}) async-start(bf16[128,16,1024]{2,1,0:T(8,128)(2,1)} %bitcast.170), calls=%async_computation | async-start | bytes 8388608 | tf_op jit(solution)/shard_map/all_to_all | solution.py:106
  90.9 3.0 %copy-start.5 = (bf16[64,16,128]{2,1,0:T(8,128)(2,1)S(1)}, bf16[64,16,128]{2,1,0:T(8,128)(2,1)}, u32[]{:S(2)}) copy-start(bf16[64,16,128]{2,1,0:T(8,128)(2,1)} %param.11) | copy-start | bytes 786436
  117.9 0.8 copy-start.3
  144.1 5.4 %copy-start.2 = (bf16[64,64,128]{2,1,0:T(8,128)(2,1)S(1)}, bf16[64,64,128]{2,1,0:T(8,128)(2,1)}, u32[]{:S(2)}) copy-start(bf16[64,64,128]{2,1,0:T(8,128)(2,1)} %param.12) | copy-start | bytes 3145732
Sparse Core Ops, SparseCore 0:
  20.7 71.5 all-gather.2

commit v5 on v4

--- a/solution.py
+++ b/solution.py
@@ -20,29 +20,29 @@
 
 def scatter_kernel(boxes_ref, values_ref, out_ref):
     table = (
-        boxes_ref[...] == lax.broadcasted_iota(jnp.int32, (out_ref.shape[0], boxes_ref.shape[1]), 0)
+        boxes_ref[0] == lax.broadcasted_iota(jnp.int32, (out_ref.shape[0], boxes_ref.shape[2]), 0)
     ).astype(values_ref.dtype)
     out_ref[...] = jnp.dot(table, values_ref[...], preferred_element_type=jnp.float32)
 
 
 def scatter_rows(boxes, values, count):
-    slots, width = values.shape
-    step = 512
+    parts, slots = boxes.shape
+    width = values.shape[1]
     return pl.pallas_call(
         scatter_kernel,
-        grid=(width // step,),
+        grid=(parts,),
         in_specs=[
-            pl.BlockSpec((1, slots), lambda i: (0, 0)),
-            pl.BlockSpec((slots, step), lambda i: (0, i)),
+            pl.BlockSpec((1, 1, slots), lambda i: (i, 0, 0)),
+            pl.BlockSpec((slots, width), lambda i: (0, 0)),
         ],
-        out_specs=pl.BlockSpec((count, step), lambda i: (0, i)),
-        out_shape=jax.ShapeDtypeStruct((count, width), jnp.float32),
+        out_specs=pl.BlockSpec((count, width), lambda i: (0, i)),
+        out_shape=jax.ShapeDtypeStruct((count, parts * width), jnp.float32),
         cost_estimate=pl.CostEstimate(
-            flops=2 * count * slots * width,
-            bytes_accessed=slots * width * 2 + count * width * 4 + slots * 4,
+            flops=2 * count * slots * width * parts,
+            bytes_accessed=slots * width * 2 + count * width * parts * 4 + parts * slots * 4,
             transcendentals=0,
         ),
-    )(boxes, values)
+    )(boxes.reshape(parts, 1, slots), values)
 
 
 def body_inner(
@@ -100,11 +100,21 @@
     products = jnp.einsum(
         "crj,cjk->crk", picked, coupling_blocks, preferred_element_type=jnp.float32
     ).astype(jnp.bfloat16)
+    halves = 2
+    slot_half = (
+        (target_dev * capacity + slot_pos)[:, None] * halves
+        + jnp.arange(halves, dtype=jnp.int32)[None, :]
+    ).reshape(1, entries * halves)
+    half_table = (
+        jnp.arange(devices * capacity * halves, dtype=jnp.int32)[:, None] == slot_half
+    ).astype(jnp.bfloat16)
     send_values = jnp.dot(
-        slot_table, products.reshape(entries, flat_width), preferred_element_type=jnp.float32
+        half_table,
+        products.reshape(entries * halves, flat_width // halves),
+        preferred_element_type=jnp.float32,
     ).astype(jnp.bfloat16)
     received = lax.all_to_all(
-        send_values.reshape(devices, rows, flat_width),
+        send_values.reshape(devices, capacity * halves, flat_width // halves),
         "leaf",
         split_axis=0,
         concat_axis=0,
@@ -163,9 +173,16 @@
     tree_part = jnp.einsum("rk,bjk->brj", local_exp, leaf_up, precision=highest)
     nearfield, tree_part = lax.optimization_barrier((nearfield, tree_part))
 
+    slot_boxes = recv_boxes[:, :capacity].reshape(devices * capacity, 1)
+    half_boxes = jnp.where(
+        jnp.arange(halves, dtype=jnp.int32)[:, None, None]
+        == jnp.arange(halves, dtype=jnp.int32)[None, None, :],
+        slot_boxes[None, :, :],
+        -1,
+    ).reshape(halves, devices * capacity * halves)
     far = scatter_rows(
-        recv_boxes.reshape(1, devices * rows),
-        received.reshape(devices * rows, flat_width),
+        half_boxes,
+        received.reshape(devices * capacity * halves, flat_width // halves),
         leaf_count,
     )
     far = far.reshape(leaf_count, sides_rhs, ranks)

time: 161 us -> 157 us (0.975)
  matrix products: 62.3 us -> 52.5 us
  local copies, waits for them, and re-layouts: 54.7 us -> 58 us
  other arithmetic: 3.82 us -> 6.64 us
    reshape x0 -> x1, local copies, waits for them, and re-layouts: none -> 6.48 us  [body_inner(): products.reshape(entries * halves, flat_width // halves)]
    convert_element_type x1 -> x0, local copies, waits for them, and re-layouts: 5.51 us -> none  [body_inner(): products = jnp.einsum('crj,cjk->crk', picked, coupling_blocks, preferred_...]
    dot_general x6, matrix products: 8.35 us -> 3.34 us  [body_inner(): jnp.einsum('nsrj,sjk->nrk', paired, top_up[level], precision=highest)]
    broadcast_in_dim x0 -> x5, local copies, waits for them, and re-layouts: none -> 4.61 us  [body_inner(): jnp.where(jnp.arange(halves, dtype=jnp.int32)[:, None, None] == jnp.arang...]
    dot_general x7, matrix products: 5.71 us -> 1.11 us  [body_inner(): jnp.dot(sibling, lax.dynamic_index_in_dim(top_coupling[level], node_side,...]
    dot_general x7, matrix products: 5.59 us -> 1.02 us  [body_inner(): jnp.dot(local_exp, lax.dynamic_index_in_dim(top_up[level], node_side, 0,...]
    dot_general x1, matrix products: 7.68 us -> 12.1 us  [body_inner(): jnp.dot(half_table, products.reshape(entries * halves, flat_width // halv...]
    unnamed x19 -> x41, local copies, waits for them, and re-layouts: 24.8 us -> 25 us
  transfers between devices with their start and end apart: 4 -> 4, of which waited for: 0 -> 1; matrix products, arithmetic and copies ran while one was open for 73% -> 72% of each run, Pallas kernels for 0% -> 0%
where the time goes in v5:
time: 157 us; the launch traced here: 156 us
  local copies, waits for them, and re-layouts  58 us (37%)
  matrix products  52.5 us (33%)
  starting transfers between devices  20.7 us (13%)
  between operations  13.9 us (9%)
  other arithmetic  6.64 us (4%)
  Pallas kernels  3.88 us (2%)
    unnamed x41, local copies, waits for them, and re-layouts  25 us
    all_to_all x1, starting transfers between devices, body_inner(): lax.all_to_all(send_values.reshape(devices, capacity * halves, flat_width...  14 us
    dot_general x1, matrix products, body_inner(): jnp.dot(half_table, products.reshape(entries * halves, flat_width // halv...  12.1 us
    dot_general x1, matrix products, body_inner(): jnp.einsum('crj,cjk->crk', picked, coupling_blocks, preferred_element_typ...  10.7 us
    dot_general x1, matrix products, body_inner(): jnp.einsum('brm,bmp->brp', gathered, near_blocks.reshape(leaf_count, near...  9.51 us
    reshape x1, local copies, waits for them, and re-layouts, body_inner(): products.reshape(entries * halves, flat_width // halves)  6.48 us
    dot_general x1, local copies, waits for them, and re-layouts, body_inner(): jnp.einsum('es,srj->erj', source_table, skeleton_low, preferred_element_t...  6.18 us
    dot_general x1, matrix products, body_inner(): tree_part = jnp.einsum('rk,bjk->brj', local_exp, leaf_up, precision=highest)  5.77 us
  transfers between devices with their start and end apart: 4, of which 1 were waited for; matrix products, arithmetic and copies ran while one was open for 72% of the time, Pallas kernels for 0%

profile of v5, /device:TPU:1, one launch (start us, length us, event | category | flops | bytes accessed | tf_op | source)
XLA Modules:
  0.0 156.0 jit_solution(16579299380001811788)
XLA Ops:
  6.5 3.4 %collective-permute-start.1 = (bf16[64,16,128]{2,1,0:T(8,128)(2,1)}, bf16[64,16,128]{2,1,0:T(8,128)(2,1)}, u32[]{:S(2)}, u32[]{:S(2)}) collective-permute-start(bf16[64,16,128]{2,1,0:T(8,128)(2,1)} %param.11), channel_id=1, source_target_pairs={{1,0},{2,1},{3,2},{4,3},{5,4},{6,5},{7,6},{8,7},{9,8},{10,9},{11,1... | collective-permute-start | bytes 786440 | tf_op jit(solution)/shard_map/ppermute | solution.py:16
  10.0 3.2 %collective-permute-start = (bf16[64,16,128]{2,1,0:T(8,128)(2,1)}, bf16[64,16,128]{2,1,0:T(8,128)(2,1)}, u32[]{:S(2)}, u32[]{:S(2)}) collective-permute-start(bf16[64,16,128]{2,1,0:T(8,128)(2,1)} %param.11), channel_id=1, source_target_pairs={{0,1},{1,2},{2,3},{3,4},{4,5},{5,6},{6,7},{7,8},{8,9},{9,10},{10,1... | collective-permute-start | bytes 786440 | tf_op jit(solution)/shard_map/ppermute | solution.py:15
  13.9 0.8 copy.19
  15.7 1.2 broadcast_add_fusion
  17.0 1.0 fusion.17
  18.1 1.5 fusion.2
  19.7 1.6 %fusion.107 = (bf16[64,16,64]{2,1,0:T(8,128)(2,1)S(1)}, f32[64,16,64]{2,1,0:T(8,128)S(1)}) fusion(bf16[64,16,128]{2,1,0:T(8,128)(2,1)} %param.11, bf16[64,64,128]{2,1,0:T(8,128)(2,1)S(1)} %copy-done.1), kind=kOutput, calls=%fused_computation.140 | convolution fusion | flops 16842752 | bytes 1703936 | tf_op jit(solution)/shard_map/bkp,brp->brk/dot_general | solution.py:90
  21.3 1.2 convolution_bitcast_fusion.2
  23.2 24.1 %copy.27 = bf16[1024,64,64]{2,1,0:T(8,128)(2,1)} copy(bf16[1024,64,64]{0,2,1:T(8,128)(2,1)} %param.18) | data formatting | bytes 16777216 | tf_op args[7]
  47.3 2.2 %fusion.23 = bf16[1024,16,64]{0,2,1:T(8,128)(2,1)} fusion(bf16[64,16,64]{2,1,0:T(8,128)(2,1)S(1)} %get-tuple-element.23, s32[1024]{0:T(1024)S(1)} %copy-done.18), kind=kOutput, calls=%fused_computation.42 | convolution fusion | flops 134283264 | bytes 2232320 | tf_op jit(solution)/shard_map/es,srj->erj/dot_general | solution.py:97
  49.5 6.2 %copy.35 = bf16[1024,16,64]{2,1,0:T(8,128)(2,1)} copy(bf16[1024,16,64]{0,2,1:T(8,128)(2,1)} %fusion.23) | data formatting | bytes 4194304 | tf_op jit(solution)/shard_map/es,srj->erj/dot_general | solution.py:97
  55.7 10.7 %fusion.7 = bf16[1024,16,64]{2,1,0:T(8,128)(2,1)} fusion(bf16[1024,64,64]{2,1,0:T(8,128)(2,1)} %copy.27, bf16[1024,16,64]{2,1,0:T(8,128)(2,1)} %copy.35), kind=kOutput, calls=%fused_computation.10 | convolution fusion | flops 135266304 | bytes 12582912 | tf_op jit(solution)/shard_map/crj,cjk->crk/dot_general | solution.py:100
  66.4 6.5 %reshape.183 = bf16[2048,512]{1,0:T(8,128)(2,1)} reshape(bf16[1024,16,64]{2,1,0:T(8,128)(2,1)} %fusion.7) | data formatting | bytes 4194304 | tf_op jit(solution)/shard_map/reshape | solution.py:113
  73.4 12.1 %fusion.3 = bf16[3072,512]{1,0:T(8,128)(2,1)} fusion(bf16[2048,512]{1,0:T(8,128)(2,1)} %reshape.183, s32[2048]{0:T(1024)S(1)} %add.168), kind=kOutput, calls=%fused_computation.6 | convolution fusion | flops 6450315264 | bytes 5251072 | tf_op jit(solution)/shard_map/dot_general | solution.py:111
  85.5 14.0 %all-to-all-start = ((bf16[128,24,512]{2,1,0:T(8,128)(2,1)}), bf16[128,24,512]{2,1,0:T(8,128)(2,1)}, u32[]{:S(2)}, u32[]{:S(2)}) async-start(bf16[128,24,512]{2,1,0:T(8,128)(2,1)} %bitcast.172), calls=%async_computation | async-start | bytes 6291456 | tf_op jit(solution)/shard_map/all_to_all | solution.py:116
  99.7 0.8 fusion.106
  100.9 1.7 %broadcast_in_dim.74 = pred[2,1,3072]{2,1,0:T(4,128)(4,1)} reshape(pred[2,1536,2]{2,1,0:T(8,128)(4,1)S(1)} %broadcast_in_dim.67) | data formatting | bytes 12288 | tf_op jit(solution)/shard_map/jit(_where)/broadcast_in_dim | solution.py:177
  102.6 1.8 %fusion.105 = (f32[1,2,64,64]{3,2,1,0:T(8,128)S(1)}, f32[1,2,64,64]{3,2,1,0:T(8,128)S(1)}, f32[1,2,64,64]{3,2,1,0:T(8,128)}, f32[1,2,64,64]{3,2,1,0:T(8,128)}, f...) fusion(f32[7,2,64,64]{3,2,1,0:T(8,128)} %param.15), kind=kLoop, calls=%fused_computation.138 | loop fusion | bytes 458752 | tf_op jit(solution)/shard_map/slice | solution.py:149
  104.4 1.2 pad_maximum_fusion
  105.6 2.8 %gather_fusion = bf16[512,16,128]{2,1,0:T(8,128)(2,1)} fusion(bf16[192,16,128]{2,1,0:T(8,128)(2,1)S(1)} %pad_maximum_fusion, s32[1024]{0:T(1024)S(1)} %pad_clamp_fusion), kind=kCustom, calls=%fused_computation | custom fusion | bytes 4196352 | tf_op jit(solution)/shard_map/gather | solution.py:163
  108.4 9.5 %fusion.10 = f32[64,16,128]{2,1,0:T(8,128)} fusion(bf16[64,1024,128]{2,1,0:T(8,128)(2,1)} %bitcast.169, bf16[64,8,2,8,128]{4,3,2,1,0:T(8,128)(2,1)} %bitcast.170), kind=kOutput, calls=%fused_computation.11 | convolution fusion | flops 268435456 | bytes 19398656 | tf_op jit(solution)/shard_map/brm,bmp->brp/dot_general | solution.py:167
  117.9 1.5 slice.86
  119.4 1.6 %fusion.14 = f32[64,16,64,1]{2,0,3,1:T(8,128)S(1)} fusion(f32[64,2,16,64]{3,2,1,0:T(8,128)S(1)} %bitcast.171, f32[7,2,64,64]{3,2,1,0:T(8,128)S(1)} %copy-done.5), kind=kOutput, calls=%fused_computation.26 | convolution fusion | flops 100663296 | bytes 1376256 | tf_op jit(solution)/shard_map/nsrj,sjk->nrk/dot_general | solution.py:141
  123.5 1.6 %slice.87 = f32[128,32,64]{2,1,0:T(8,128)} slice(f32[128,48,64]{2,1,0:T(8,128)S(1)} %bitcast.174), slice={[0:128], [16:48], [0:64]} | slice | bytes 2097152 | tf_op jit(solution)/shard_map/slice | solution.py:130
  126.7 5.8 %convolution_bitcast_fusion = f32[64,16,64]{2,1,0:T(8,128)} fusion(f32[16,64,1]{1,0,2:T(8,128)S(1)} %fusion.13, f32[64,64,64]{2,1,0:T(8,128)S(1)} %copy-done), kind=kOutput, calls=%fused_computation.15 | convolution fusion | flops 50331648 | bytes 1314816 | tf_op jit(solution)/shard_map/rk,bjk->brj/dot_general | solution.py:173
  132.5 3.7 %copy.24 = f32[128,32,64]{0,2,1:T(8,128)} copy(f32[128,32,64]{2,1,0:T(8,128)} %slice.87) | data formatting | bytes 2097152 | tf_op jit(solution)/shard_map/slice | solution.py:130
  136.2 0.8 add_bitcast_fusion
  137.2 1.2 broadcast_in_dim.70
  138.4 1.5 broadcast_in_dim.71
  140.9 3.9 %shard_map.109 = f32[64,1024]{1,0:T(8,128)} custom-call(s32[2,1,3072]{2,1,0:T(1,128)} %broadcast_select_fusion.boxes_ref, bf16[3072,512]{1,0:T(8,128)(2,1)} %bitcast.70.values_ref), custom_call_target="tpu_custom_call" | custom-call | flops 402653184 | bytes 3432448 | tf_op jit(solution)/shard_map/pallas_call | solution.py:31
  144.7 1.9 %reshape.186 = f32[64,16,64]{2,1,0:T(8,128)} reshape(f32[64,1024]{1,0:T(8,128)} %shard_map.109) | data formatting | bytes 524288 | tf_op jit(solution)/shard_map/reshape | solution.py:188
  146.6 2.5 %convolution_add_fusion = f32[64,16,128]{2,1,0:T(8,128)} fusion(f32[64,16,128]{2,1,0:T(8,128)} %fusion.10, bf16[64,64,128]{2,1,0:T(8,128)(2,1)S(1)} %copy-done.2, f32[64,16,64]{2,1,0:T(8,128)} %convolution_bitcast_fusion, f32[64,16,64]{2,1,0:T(8,128)} %reshape.186), kind=kOutput, calls=%fused_computation.14 | convolution fusion | flops 17039360 | bytes 2621440 | tf_op jit(solution)/shard_map/brk,bkp->brp/dot_general | solution.py:190
  (93 shorter events, 8.7 us)
Async XLA Ops:
  6.5 14.8 %copy-start = (f32[64,64,64]{2,1,0:T(8,128)S(1)}, f32[64,64,64]{2,1,0:T(8,128)}, u32[]{:S(2)}) copy-start(f32[64,64,64]{2,1,0:T(8,128)} %param.13) | copy-start | bytes 3145732
  6.5 11.5 %copy-start.17 = (s32[1024,1]{0,1:T(1,128)S(1)}, s32[1024,1]{0,1:T(1,128)}, u32[]{:S(2)}) copy-start(s32[1024,1]{0,1:T(1,128)} %param.20) | copy-start | bytes 12292
  6.5 111.4 %all-gather.3.cloned.1.call-start = ((), (), s32[]{:S(2)}) async-start(), calls=%async_computation.1 | async-start | bytes 3170304 | tf_op jit(solution)/shard_map/all_gather | solution.py:124
  6.5 97.8 %collective-permute-start.1 = (bf16[64,16,128]{2,1,0:T(8,128)(2,1)}, bf16[64,16,128]{2,1,0:T(8,128)(2,1)}, u32[]{:S(2)}, u32[]{:S(2)}) collective-permute-start(bf16[64,16,128]{2,1,0:T(8,128)(2,1)} %param.11), channel_id=1, source_target_pairs={{1,0},{2,1},{3,2},{4,3},{5,4},{6,5},{7,6},{8,7},{9,8},{10,9},{11,1... | collective-permute-start | bytes 786440 | tf_op jit(solution)/shard_map/ppermute | solution.py:16
  10.0 94.4 %collective-permute-start = (bf16[64,16,128]{2,1,0:T(8,128)(2,1)}, bf16[64,16,128]{2,1,0:T(8,128)(2,1)}, u32[]{:S(2)}, u32[]{:S(2)}) collective-permute-start(bf16[64,16,128]{2,1,0:T(8,128)(2,1)} %param.11), channel_id=1, source_target_pairs={{0,1},{1,2},{2,3},{3,4},{4,5},{5,6},{6,7},{7,8},{8,9},{9,10},{10,1... | collective-permute-start | bytes 786440 | tf_op jit(solution)/shard_map/ppermute | solution.py:15
  14.9 0.8 copy-start.4
  15.7 4.0 %copy-start.1 = (bf16[64,64,128]{2,1,0:T(8,128)(2,1)S(1)}, bf16[64,64,128]{2,1,0:T(8,128)(2,1)}, u32[]{:S(2)}) copy-start(bf16[64,64,128]{2,1,0:T(8,128)(2,1)} %param.12) | copy-start | bytes 3145732
  23.2 24.1 %copy-start.18 = (s32[1024]{0:T(1024)S(1)}, s32[1024]{0:T(1024)}, u32[]{:S(2)}) copy-start(s32[1024]{0:T(1024)} %param.19) | copy-start | bytes 12292
  85.5 14.1 %copy-start.19 = (s32[64,8]{0,1:T(8,128)S(1)}, s32[64,8]{0,1:T(8,128)}, u32[]{:S(2)}) copy-start(s32[64,8]{0,1:T(8,128)} %param.17) | copy-start | bytes 6148
  85.5 14.3 %copy-start.5 = (f32[7,2,64,64]{3,2,1,0:T(8,128)S(1)}, f32[7,2,64,64]{3,2,1,0:T(8,128)}, u32[]{:S(2)}) copy-start(f32[7,2,64,64]{3,2,1,0:T(8,128)} %param.14) | copy-start | bytes 688132
  85.5 55.4 %all-to-all-start = ((bf16[128,24,512]{2,1,0:T(8,128)(2,1)}), bf16[128,24,512]{2,1,0:T(8,128)(2,1)}, u32[]{:S(2)}, u32[]{:S(2)}) async-start(bf16[128,24,512]{2,1,0:T(8,128)(2,1)} %bitcast.172), calls=%async_computation | async-start | bytes 6291456 | tf_op jit(solution)/shard_map/all_to_all | solution.py:116
  117.9 5.0 %copy-start.9 = (f32[1,2,64,64]{3,2,1,0:T(8,128)S(1)}, f32[1,2,64,64]{3,2,1,0:T(8,128)}, u32[]{:S(2)}) copy-start(f32[1,2,64,64]{3,2,1,0:T(8,128)} %get-tuple-element.14) | copy-start | bytes 98308
  117.9 5.1 %copy-start.15 = (f32[1,2,64,64]{3,2,1,0:T(8,128)S(1)}, f32[1,2,64,64]{3,2,1,0:T(8,128)}, u32[]{:S(2)}) copy-start(f32[1,2,64,64]{3,2,1,0:T(8,128)} %get-tuple-element.21) | copy-start | bytes 98308
  117.9 5.3 %copy-start.8 = (f32[1,2,64,64]{3,2,1,0:T(8,128)S(1)}, f32[1,2,64,64]{3,2,1,0:T(8,128)}, u32[]{:S(2)}) copy-start(f32[1,2,64,64]{3,2,1,0:T(8,128)} %get-tuple-element.13) | copy-start | bytes 98308
  117.9 5.4 %copy-start.14 = (f32[1,2,64,64]{3,2,1,0:T(8,128)S(1)}, f32[1,2,64,64]{3,2,1,0:T(8,128)}, u32[]{:S(2)}) copy-start(f32[1,2,64,64]{3,2,1,0:T(8,128)} %get-tuple-element.22) | copy-start | bytes 98308
  117.9 5.6 %copy-start.3 = (f32[6144,64]{1,0:T(8,128)S(1)}, f32[6144,64]{1,0:T(8,128)}, u32[]{:S(2)}) copy-start(f32[6144,64]{1,0:T(8,128)} %all-gather.3.cloned.1.call-done) | copy-start | bytes 4718596
  121.0 4.2 %copy-start.7 = (f32[1,2,64,64]{3,2,1,0:T(8,128)S(1)}, f32[1,2,64,64]{3,2,1,0:T(8,128)}, u32[]{:S(2)}) copy-start(f32[1,2,64,64]{3,2,1,0:T(8,128)} %get-tuple-element.12) | copy-start | bytes 98308
  121.0 4.4 %copy-start.13 = (f32[1,2,64,64]{3,2,1,0:T(8,128)S(1)}, f32[1,2,64,64]{3,2,1,0:T(8,128)}, u32[]{:S(2)}) copy-start(f32[1,2,64,64]{3,2,1,0:T(8,128)} %get-tuple-element.17) | copy-start | bytes 98308
  121.0 4.5 %copy-start.6 = (f32[1,2,64,64]{3,2,1,0:T(8,128)S(1)}, f32[1,2,64,64]{3,2,1,0:T(8,128)}, u32[]{:S(2)}) copy-start(f32[1,2,64,64]{3,2,1,0:T(8,128)} %get-tuple-element.11) | copy-start | bytes 98308
  121.0 4.7 %copy-start.12 = (f32[1,2,64,64]{3,2,1,0:T(8,128)S(1)}, f32[1,2,64,64]{3,2,1,0:T(8,128)}, u32[]{:S(2)}) copy-start(f32[1,2,64,64]{3,2,1,0:T(8,128)} %get-tuple-element.18) | copy-start | bytes 98308
  121.0 5.0 %copy-start.11 = (f32[1,2,64,64]{3,2,1,0:T(8,128)S(1)}, f32[1,2,64,64]{3,2,1,0:T(8,128)}, u32[]{:S(2)}) copy-start(f32[1,2,64,64]{3,2,1,0:T(8,128)} %get-tuple-element.19) | copy-start | bytes 98308
  121.6 4.7 %copy-start.10 = (f32[1,2,64,64]{3,2,1,0:T(8,128)S(1)}, f32[1,2,64,64]{3,2,1,0:T(8,128)}, u32[]{:S(2)}) copy-start(f32[1,2,64,64]{3,2,1,0:T(8,128)} %get-tuple-element.16) | copy-start | bytes 98308
  126.7 13.2 %copy-start.16 = (pred[2,1,3072]{2,1,0:T(4,128)(4,1)S(1)}, pred[2,1,3072]{2,1,0:T(4,128)(4,1)}, u32[]{:S(2)}) copy-start(pred[2,1,3072]{2,1,0:T(4,128)(4,1)} %broadcast_in_dim.74) | copy-start | bytes 18436
  136.2 10.5 %copy-start.2 = (bf16[64,64,128]{2,1,0:T(8,128)(2,1)S(1)}, bf16[64,64,128]{2,1,0:T(8,128)(2,1)}, u32[]{:S(2)}) copy-start(bf16[64,64,128]{2,1,0:T(8,128)(2,1)} %param.12) | copy-start | bytes 3145732
Sparse Core Ops, SparseCore 0:
  23.3 71.6 all-gather.2

commit v6 on v4

--- a/solution.py
+++ b/solution.py
@@ -2,6 +2,7 @@
 import jax.numpy as jnp
 from jax import lax
 from jax.experimental import pallas as pl
+from jax.experimental.pallas import tpu as pltpu
 from jax.sharding import PartitionSpec as P
 
 
@@ -43,6 +44,28 @@
             transcendentals=0,
         ),
     )(boxes, values)
+
+
+def pick_kernel(source_ref, table_ref, out_ref):
+    def row(e, carry):
+        out_ref[e] = table_ref[source_ref[e]]
+        return carry
+
+    lax.fori_loop(0, out_ref.shape[0], row, 0, unroll=8)
+
+
+def pick_rows(table, source):
+    entries = source.shape[0]
+    return pl.pallas_call(
+        pick_kernel,
+        grid_spec=pltpu.PrefetchScalarGridSpec(
+            num_scalar_prefetch=1,
+            grid=(1,),
+            in_specs=[pl.BlockSpec(table.shape, lambda i, src: (0, 0, 0))],
+            out_specs=pl.BlockSpec((entries,) + table.shape[1:], lambda i, src: (0, 0, 0)),
+        ),
+        out_shape=jax.ShapeDtypeStruct((entries,) + table.shape[1:], table.dtype),
+    )(source, table)
 
 
 def body_inner(
@@ -91,12 +114,7 @@
     skeleton_low = skeleton.astype(jnp.bfloat16)
     own_box = jnp.einsum("brj,bjk->rk", skeleton, leaf_up, precision=highest)
 
-    source_table = (
-        coup_source[:, None] == jnp.arange(leaf_count, dtype=jnp.int32)[None, :]
-    ).astype(jnp.bfloat16)
-    picked = jnp.einsum(
-        "es,srj->erj", source_table, skeleton_low, preferred_element_type=jnp.float32
-    ).astype(jnp.bfloat16)
+    picked = pick_rows(skeleton_low, coup_source)
     products = jnp.einsum(
         "crj,cjk->crk", picked, coupling_blocks, preferred_element_type=jnp.float32
     ).astype(jnp.bfloat16)

time: 161 us -> 160 us (level)
  local copies, waits for them, and re-layouts: 54.7 us -> 48.2 us
  Pallas kernels: 3.48 us -> 8.98 us
  matrix products: 62.3 us -> 59.9 us
  other arithmetic: 3.82 us -> 5.65 us
    dot_general x1 -> x0, local copies, waits for them, and re-layouts: 6.18 us -> none  [body_inner(): jnp.einsum('es,srj->erj', source_table, skeleton_low, preferred_element_t...]
    pallas_call x0 -> x1, Pallas kernels: none -> 5.57 us  [pick_rows(): pl.pallas_call(pick_kernel, grid_spec=pltpu.PrefetchScalarGridSpec(num_sc...]
    dot_general x1 -> x0, matrix products: 2.17 us -> none  [body_inner(): jnp.einsum('es,srj->erj', source_table, skeleton_low, preferred_element_t...]
    unnamed x19 -> x21, local copies, waits for them, and re-layouts: 24.8 us -> 25.6 us
  transfers between devices with their start and end apart: 4 -> 4, of which waited for: 0 -> 1; matrix products, arithmetic and copies ran while one was open for 73% -> 68% of each run, Pallas kernels for 0% -> 4%
where the time goes in v6:
time: 160 us; the launch traced here: 158 us
  matrix products  59.9 us (37%)
  local copies, waits for them, and re-layouts  48.2 us (30%)
  starting transfers between devices  20.8 us (13%)
  between operations  13.7 us (9%)
  Pallas kernels  8.98 us (6%)
  other arithmetic  5.65 us (4%)
    unnamed x21, local copies, waits for them, and re-layouts  25.6 us
    all_to_all x1, starting transfers between devices, body_inner(): lax.all_to_all(send_values.reshape(devices, rows, flat_width), 'leaf', sp...  14.1 us
    dot_general x1, matrix products, body_inner(): jnp.einsum('crj,cjk->crk', picked, coupling_blocks, preferred_element_typ...  10.6 us
    dot_general x1, matrix products, body_inner(): jnp.einsum('brm,bmp->brp', gathered, near_blocks.reshape(leaf_count, near...  9.51 us
    dot_general x6, matrix products, body_inner(): jnp.einsum('nsrj,sjk->nrk', paired, top_up[level], precision=highest)  8.35 us
    dot_general x1, matrix products, body_inner(): jnp.dot(slot_table, products.reshape(entries, flat_width), preferred_elem...  7.67 us
    slice x2, local copies, waits for them, and re-layouts, body_inner(): gathered[:, sides_rhs:].reshape(devices, devices, rows)  6.8 us
    dot_general x1, matrix products, body_inner(): tree_part = jnp.einsum('rk,bjk->brj', local_exp, leaf_up, precision=highest)  5.81 us
  transfers between devices with their start and end apart: 4, of which 1 were waited for; matrix products, arithmetic and copies ran while one was open for 68% of the time, Pallas kernels for 4%

profile of v6, /device:TPU:1, one launch (start us, length us, event | category | flops | bytes accessed | tf_op | source)
XLA Modules:
  0.0 157.8 jit_solution(7007917669353720471)
XLA Ops:
  6.5 3.4 %collective-permute-start.1 = (bf16[64,16,128]{2,1,0:T(8,128)(2,1)}, bf16[64,16,128]{2,1,0:T(8,128)(2,1)}, u32[]{:S(2)}, u32[]{:S(2)}) collective-permute-start(bf16[64,16,128]{2,1,0:T(8,128)(2,1)} %param.11), channel_id=1, source_target_pairs={{1,0},{2,1},{3,2},{4,3},{5,4},{6,5},{7,6},{8,7},{9,8},{10,9},{11,1... | collective-permute-start | bytes 786440 | tf_op jit(solution)/shard_map/ppermute | solution.py:17
  10.0 3.2 %collective-permute-start = (bf16[64,16,128]{2,1,0:T(8,128)(2,1)}, bf16[64,16,128]{2,1,0:T(8,128)(2,1)}, u32[]{:S(2)}, u32[]{:S(2)}) collective-permute-start(bf16[64,16,128]{2,1,0:T(8,128)(2,1)} %param.11), channel_id=1, source_target_pairs={{0,1},{1,2},{2,3},{3,4},{4,5},{5,6},{6,7},{7,8},{8,9},{9,10},{10,1... | collective-permute-start | bytes 786440 | tf_op jit(solution)/shard_map/ppermute | solution.py:16
  15.8 1.2 broadcast_add_fusion
  17.1 1.0 fusion.12
  18.2 1.5 fusion.1
  19.7 1.4 fusion.97
  21.1 1.2 convolution_bitcast_fusion.2
  23.0 24.0 %copy.26 = bf16[1024,64,64]{2,1,0:T(8,128)(2,1)} copy(bf16[1024,64,64]{0,2,1:T(8,128)(2,1)} %param.18) | data formatting | bytes 16777216 | tf_op args[7]
  46.9 5.6 %shard_map.109 = bf16[1024,16,64]{2,1,0:T(8,128)(2,1)} custom-call(s32[1024]{0:T(1024)} %source_ref.1, bf16[64,16,64]{2,1,0:T(8,128)(2,1)} %get-tuple-element.23.table_ref), custom_call_target="tpu_custom_call" | custom-call | tf_op jit(solution)/shard_map/pallas_call | solution.py:59
  52.5 10.6 %convolution_convert_fusion = bf16[1024,16,64]{2,1,0:T(8,128)(2,1)} fusion(bf16[1024,16,64]{2,1,0:T(8,128)(2,1)} %shard_map.109, bf16[1024,64,64]{2,1,0:T(8,128)(2,1)} %copy.26), kind=kOutput, calls=%fused_computation.7 | convolution fusion | flops 135266304 | bytes 12582912 | tf_op jit(solution)/shard_map/crj,cjk->crk/dot_general | solution.py:118
  63.1 5.5 %copy.27 = bf16[1024,16,64]{0,2,1:T(8,128)(2,1)} copy(bf16[1024,16,64]{2,1,0:T(8,128)(2,1)} %convolution_convert_fusion) | data formatting | bytes 4194304 | tf_op jit(solution)/shard_map/convert_element_type | solution.py:120
  68.6 7.7 %fusion.4 = bf16[2048,1024]{1,0:T(8,128)(2,1)} fusion(bf16[1024,1024]{0,1:T(8,128)(2,1)} %bitcast.172, s32[1024]{0:T(1024)S(1)} %multiply_add_fusion), kind=kOutput, calls=%fused_computation.6 | convolution fusion | flops 4299161600 | bytes 6295552 | tf_op jit(solution)/shard_map/dot_general | solution.py:121
  76.3 14.1 %all-to-all-start = ((bf16[128,16,1024]{2,1,0:T(8,128)(2,1)}), bf16[128,16,1024]{2,1,0:T(8,128)(2,1)}, u32[]{:S(2)}, u32[]{:S(2)}) async-start(bf16[128,16,1024]{2,1,0:T(8,128)(2,1)} %bitcast.167), calls=%async_computation | async-start | bytes 8388608 | tf_op jit(solution)/shard_map/all_to_all | solution.py:124
  92.4 1.1 pad_maximum_fusion
  93.5 2.8 %gather_fusion = bf16[512,16,128]{2,1,0:T(8,128)(2,1)} fusion(bf16[192,16,128]{2,1,0:T(8,128)(2,1)S(1)} %pad_maximum_fusion, s32[1024]{0:T(1024)S(1)} %pad_clamp_fusion), kind=kCustom, calls=%fused_computation | custom fusion | bytes 4196352 | tf_op jit(solution)/shard_map/gather | solution.py:171
  96.3 9.5 %fusion.5 = f32[64,16,128]{2,1,0:T(8,128)} fusion(bf16[64,1024,128]{2,1,0:T(8,128)(2,1)} %bitcast.164, bf16[64,8,2,8,128]{4,3,2,1,0:T(8,128)(2,1)} %bitcast.165), kind=kOutput, calls=%fused_computation.8 | convolution fusion | flops 268435456 | bytes 19398656 | tf_op jit(solution)/shard_map/brm,bmp->brp/dot_general | solution.py:175
  105.8 1.3 slice.82
  107.1 3.2 %slice.83 = f32[128,32,64]{2,1,0:T(8,128)} slice(f32[128,48,64]{2,1,0:T(8,128)} %bitcast.169), slice={[0:128], [16:48], [0:64]} | slice | bytes 2097152 | tf_op jit(solution)/shard_map/slice | solution.py:138
  110.3 3.6 %copy.24 = f32[128,32,64]{0,2,1:T(8,128)} copy(f32[128,32,64]{2,1,0:T(8,128)} %slice.83) | data formatting | bytes 2097152 | tf_op jit(solution)/shard_map/slice | solution.py:138
  113.9 2.4 %fusion.9 = f32[64,16,64,1]{2,0,3,1:T(8,128)S(1)} fusion(f32[64,2,16,64]{3,2,1,0:T(8,128)S(1)} %bitcast.166, f32[7,2,64,64]{3,2,1,0:T(8,128)} %param.14), kind=kOutput, calls=%fused_computation.23 | convolution fusion | flops 100663296 | bytes 851968 | tf_op jit(solution)/shard_map/nsrj,sjk->nrk/dot_general | solution.py:149
  117.2 1.4 fusion.13
  121.0 1.3 fusion.17
  122.2 1.1 fusion.23
  123.4 1.1 fusion.21
  124.5 1.1 convolution_bitcast_fusion.1
  127.3 0.9 convolution_add_fusion.6
  132.8 0.9 convolution_add_fusion.3
  134.7 0.9 convolution_add_fusion.2
  136.7 5.8 %convolution_bitcast_fusion = f32[64,16,64]{2,1,0:T(8,128)} fusion(f32[16,64,1]{1,0,2:T(8,128)S(1)} %fusion.8, f32[64,64,64]{2,1,0:T(8,128)S(1)} %copy-done), kind=kOutput, calls=%fused_computation.12 | convolution fusion | flops 50331648 | bytes 1314816 | tf_op jit(solution)/shard_map/rk,bjk->brj/dot_general | solution.py:181
  143.2 3.4 %shard_map.110 = f32[64,1024]{1,0:T(8,128)} custom-call(s32[1,2048]{1,0:T(1,128)} %sub.23.boxes_ref, bf16[2048,1024]{1,0:T(8,128)(2,1)} %bitcast.67.values_ref), custom_call_target="tpu_custom_call" | custom-call | flops 268435456 | bytes 4464640 | tf_op jit(solution)/shard_map/pallas_call | solution.py:32
  146.6 1.9 %reshape.133 = f32[64,16,64]{2,1,0:T(8,128)} reshape(f32[64,1024]{1,0:T(8,128)} %shard_map.110) | data formatting | bytes 524288 | tf_op jit(solution)/shard_map/reshape | solution.py:189
  148.5 2.5 %convolution_add_fusion = f32[64,16,128]{2,1,0:T(8,128)} fusion(f32[64,16,128]{2,1,0:T(8,128)} %fusion.5, bf16[64,64,128]{2,1,0:T(8,128)(2,1)S(1)} %copy-done.2, f32[64,16,64]{2,1,0:T(8,128)} %convolution_bitcast_fusion, f32[64,16,64]{2,1,0:T(8,128)} %reshape.133), kind=kOutput, calls=%fused_computation.11 | convolution fusion | flops 17039360 | bytes 2621440 | tf_op jit(solution)/shard_map/brk,bkp->brp/dot_general | solution.py:191
  (63 shorter events, 17.5 us)
Async XLA Ops:
  6.5 14.6 %copy-start = (f32[64,64,64]{2,1,0:T(8,128)S(1)}, f32[64,64,64]{2,1,0:T(8,128)}, u32[]{:S(2)}) copy-start(f32[64,64,64]{2,1,0:T(8,128)} %param.13) | copy-start | bytes 3145732
  6.5 11.7 %copy-start.8 = (s32[1024,1]{0,1:T(1,128)S(1)}, s32[1024,1]{0,1:T(1,128)}, u32[]{:S(2)}) copy-start(s32[1024,1]{0,1:T(1,128)} %param.20) | copy-start | bytes 12292
  6.5 99.3 %all-gather.3.cloned.1.call-start = ((), (), s32[]{:S(2)}) async-start(), calls=%async_computation.1 | async-start | bytes 3170304 | tf_op jit(solution)/shard_map/all_gather | solution.py:132
  6.5 85.9 %collective-permute-start.1 = (bf16[64,16,128]{2,1,0:T(8,128)(2,1)}, bf16[64,16,128]{2,1,0:T(8,128)(2,1)}, u32[]{:S(2)}, u32[]{:S(2)}) collective-permute-start(bf16[64,16,128]{2,1,0:T(8,128)(2,1)} %param.11), channel_id=1, source_target_pairs={{1,0},{2,1},{3,2},{4,3},{5,4},{6,5},{7,6},{8,7},{9,8},{10,9},{11,1... | collective-permute-start | bytes 786440 | tf_op jit(solution)/shard_map/ppermute | solution.py:17
  10.0 82.5 %collective-permute-start = (bf16[64,16,128]{2,1,0:T(8,128)(2,1)}, bf16[64,16,128]{2,1,0:T(8,128)(2,1)}, u32[]{:S(2)}, u32[]{:S(2)}) collective-permute-start(bf16[64,16,128]{2,1,0:T(8,128)(2,1)} %param.11), channel_id=1, source_target_pairs={{0,1},{1,2},{2,3},{3,4},{4,5},{5,6},{6,7},{7,8},{8,9},{9,10},{10,1... | collective-permute-start | bytes 786440 | tf_op jit(solution)/shard_map/ppermute | solution.py:16
  15.0 0.8 copy-start.4
  15.8 3.9 %copy-start.1 = (bf16[64,64,128]{2,1,0:T(8,128)(2,1)S(1)}, bf16[64,64,128]{2,1,0:T(8,128)(2,1)}, u32[]{:S(2)}) copy-start(bf16[64,64,128]{2,1,0:T(8,128)(2,1)} %param.12) | copy-start | bytes 3145732
  15.8 3.9 %copy-start.6 = (bf16[64,16,128]{2,1,0:T(8,128)(2,1)S(1)}, bf16[64,16,128]{2,1,0:T(8,128)(2,1)}, u32[]{:S(2)}) copy-start(bf16[64,16,128]{2,1,0:T(8,128)(2,1)} %param.11) | copy-start | bytes 786436
  76.3 14.2 %copy-start.9 = (s32[64,8]{0,1:T(8,128)S(1)}, s32[64,8]{0,1:T(8,128)}, u32[]{:S(2)}) copy-start(s32[64,8]{0,1:T(8,128)} %param.17) | copy-start | bytes 6148
  76.3 14.4 %copy-start.5 = (f32[7,2,64,64]{3,2,1,0:T(8,128)S(1)}, f32[7,2,64,64]{3,2,1,0:T(8,128)}, u32[]{:S(2)}) copy-start(f32[7,2,64,64]{3,2,1,0:T(8,128)} %param.14) | copy-start | bytes 688132
  76.3 15.3 %copy-start.7 = (f32[7,2,64,64]{3,2,1,0:T(8,128)S(1)}, f32[7,2,64,64]{3,2,1,0:T(8,128)}, u32[]{:S(2)}) copy-start(f32[7,2,64,64]{3,2,1,0:T(8,128)} %param.15) | copy-start | bytes 688132
  76.3 66.8 %all-to-all-start = ((bf16[128,16,1024]{2,1,0:T(8,128)(2,1)}), bf16[128,16,1024]{2,1,0:T(8,128)(2,1)}, u32[]{:S(2)}, u32[]{:S(2)}) async-start(bf16[128,16,1024]{2,1,0:T(8,128)(2,1)} %bitcast.167), calls=%async_computation | async-start | bytes 8388608 | tf_op jit(solution)/shard_map/all_to_all | solution.py:124
  116.3 0.8 copy-start.3
  142.5 5.9 %copy-start.2 = (bf16[64,64,128]{2,1,0:T(8,128)(2,1)S(1)}, bf16[64,64,128]{2,1,0:T(8,128)(2,1)}, u32[]{:S(2)}) copy-start(bf16[64,64,128]{2,1,0:T(8,128)(2,1)} %param.12) | copy-start | bytes 3145732
Sparse Core Ops, SparseCore 0:
  23.1 71.5 all-gather.2

commit v7 on v6

--- a/solution.py
+++ b/solution.py
@@ -97,9 +97,13 @@
 
     target_dev = coup_device[:, 0]
     onehot_dev = (target_dev[:, None] == jnp.arange(devices, dtype=jnp.int32)[None, :]).astype(
-        jnp.int32
-    )
-    slot_pos = jnp.sum((jnp.cumsum(onehot_dev, axis=0) - onehot_dev) * onehot_dev, axis=1)
+        jnp.bfloat16
+    )
+    earlier = (
+        jnp.arange(entries, dtype=jnp.int32)[:, None] > jnp.arange(entries, dtype=jnp.int32)[None, :]
+    ).astype(jnp.bfloat16)
+    prefix = jnp.dot(earlier, onehot_dev, preferred_element_type=jnp.float32)
+    slot_pos = jnp.sum(prefix * onehot_dev.astype(jnp.float32), axis=1).astype(jnp.int32)
     slot_flat = target_dev * rows + slot_pos
     slot_table = (
         jnp.arange(devices * rows, dtype=jnp.int32)[:, None] == slot_flat[None, :]

time: 160 us -> 157 us (0.981)
  local copies, waits for them, and re-layouts: 48.2 us -> 45.8 us
  other arithmetic: 5.65 us -> 3.88 us
    unnamed x21 -> x15, local copies, waits for them, and re-layouts: 25.6 us -> 24.8 us
where the time goes in v7:
time: 157 us; the launch traced here: 155 us
  matrix products  60.4 us (38%)
  local copies, waits for them, and re-layouts  45.8 us (29%)
  starting transfers between devices  20.9 us (13%)
  between operations  13.6 us (9%)
  Pallas kernels  8.95 us (6%)
  other arithmetic  3.88 us (2%)
    unnamed x15, local copies, waits for them, and re-layouts  24.8 us
    all_to_all x1, starting transfers between devices, body_inner(): lax.all_to_all(send_values.reshape(devices, rows, flat_width), 'leaf', sp...  14.1 us
    dot_general x1, matrix products, body_inner(): jnp.einsum('crj,cjk->crk', picked, coupling_blocks, preferred_element_typ...  10.7 us
    dot_general x1, matrix products, body_inner(): jnp.einsum('brm,bmp->brp', gathered, near_blocks.reshape(leaf_count, near...  9.51 us
    dot_general x6, matrix products, body_inner(): jnp.einsum('nsrj,sjk->nrk', paired, top_up[level], precision=highest)  8.35 us
    dot_general x1, matrix products, body_inner(): jnp.dot(slot_table, products.reshape(entries, flat_width), preferred_elem...  7.67 us
    slice x2, local copies, waits for them, and re-layouts, body_inner(): gathered[:, sides_rhs:].reshape(devices, devices, rows)  6.81 us
    dot_general x7, matrix products, body_inner(): jnp.dot(sibling, lax.dynamic_index_in_dim(top_coupling[level], node_side,...  5.71 us
  transfers between devices with their start and end apart: 4, of which 1 were waited for; matrix products, arithmetic and copies ran while one was open for 68% of the time, Pallas kernels for 4%

profile of v7, /device:TPU:1, one launch (start us, length us, event | category | flops | bytes accessed | tf_op | source)
XLA Modules:
  0.0 155.1 jit_solution(12627680134686981780)
XLA Ops:
  6.5 3.6 %collective-permute-start.1 = (bf16[64,16,128]{2,1,0:T(8,128)(2,1)}, bf16[64,16,128]{2,1,0:T(8,128)(2,1)}, u32[]{:S(2)}, u32[]{:S(2)}) collective-permute-start(bf16[64,16,128]{2,1,0:T(8,128)(2,1)} %param.11), channel_id=1, source_target_pairs={{1,0},{2,1},{3,2},{4,3},{5,4},{6,5},{7,6},{8,7},{9,8},{10,9},{11,1... | collective-permute-start | bytes 786440 | tf_op jit(solution)/shard_map/ppermute | solution.py:17
  10.1 3.2 %collective-permute-start = (bf16[64,16,128]{2,1,0:T(8,128)(2,1)}, bf16[64,16,128]{2,1,0:T(8,128)(2,1)}, u32[]{:S(2)}, u32[]{:S(2)}) collective-permute-start(bf16[64,16,128]{2,1,0:T(8,128)(2,1)} %param.11), channel_id=1, source_target_pairs={{0,1},{1,2},{2,3},{3,4},{4,5},{5,6},{6,7},{7,8},{8,9},{9,10},{10,1... | collective-permute-start | bytes 786440 | tf_op jit(solution)/shard_map/ppermute | solution.py:16
  14.1 1.4 fusion.10
  16.2 1.5 fusion.1
  17.8 1.4 fusion.97
  19.1 1.2 convolution_bitcast_fusion.2
  21.0 24.0 %copy.23 = bf16[1024,64,64]{2,1,0:T(8,128)(2,1)} copy(bf16[1024,64,64]{0,2,1:T(8,128)(2,1)} %param.18) | data formatting | bytes 16777216 | tf_op args[7]
  45.0 5.6 %shard_map.109 = bf16[1024,16,64]{2,1,0:T(8,128)(2,1)} custom-call(s32[1024]{0:T(1024)} %source_ref.1, bf16[64,16,64]{2,1,0:T(8,128)(2,1)} %get-tuple-element.23.table_ref), custom_call_target="tpu_custom_call" | custom-call | tf_op jit(solution)/shard_map/pallas_call | solution.py:59
  50.5 10.7 %convolution_convert_fusion = bf16[1024,16,64]{2,1,0:T(8,128)(2,1)} fusion(bf16[1024,16,64]{2,1,0:T(8,128)(2,1)} %shard_map.109, bf16[1024,64,64]{2,1,0:T(8,128)(2,1)} %copy.23), kind=kOutput, calls=%fused_computation.9 | convolution fusion | flops 135266304 | bytes 12582912 | tf_op jit(solution)/shard_map/crj,cjk->crk/dot_general | solution.py:122
  61.2 5.5 %copy.24 = bf16[1024,16,64]{0,2,1:T(8,128)(2,1)} copy(bf16[1024,16,64]{2,1,0:T(8,128)(2,1)} %convolution_convert_fusion) | data formatting | bytes 4194304 | tf_op jit(solution)/shard_map/convert_element_type | solution.py:124
  66.7 7.7 %fusion.5 = bf16[2048,1024]{1,0:T(8,128)(2,1)} fusion(bf16[1024,1024]{0,1:T(8,128)(2,1)} %bitcast.161, s32[1024]{0:T(1024)S(1)} %convert_add_fusion.1), kind=kOutput, calls=%fused_computation.8 | convolution fusion | flops 4299161600 | bytes 6295552 | tf_op jit(solution)/shard_map/dot_general | solution.py:125
  74.4 14.1 %all-to-all-start = ((bf16[128,16,1024]{2,1,0:T(8,128)(2,1)}), bf16[128,16,1024]{2,1,0:T(8,128)(2,1)}, u32[]{:S(2)}, u32[]{:S(2)}) async-start(bf16[128,16,1024]{2,1,0:T(8,128)(2,1)} %bitcast.156), calls=%async_computation | async-start | bytes 8388608 | tf_op jit(solution)/shard_map/all_to_all | solution.py:128
  90.5 1.1 pad_maximum_fusion
  91.6 2.8 %gather_fusion = bf16[512,16,128]{2,1,0:T(8,128)(2,1)} fusion(bf16[192,16,128]{2,1,0:T(8,128)(2,1)S(1)} %pad_maximum_fusion, s32[1024]{0:T(1024)S(1)} %pad_clamp_fusion), kind=kCustom, calls=%fused_computation | custom fusion | bytes 4196352 | tf_op jit(solution)/shard_map/gather | solution.py:175
  94.4 9.5 %fusion.6 = f32[64,16,128]{2,1,0:T(8,128)} fusion(bf16[64,1024,128]{2,1,0:T(8,128)(2,1)} %bitcast.153, bf16[64,8,2,8,128]{4,3,2,1,0:T(8,128)(2,1)} %bitcast.154), kind=kOutput, calls=%fused_computation.10 | convolution fusion | flops 268435456 | bytes 19398656 | tf_op jit(solution)/shard_map/brm,bmp->brp/dot_general | solution.py:179
  103.9 1.3 slice.72
  105.2 3.2 %slice.73 = f32[128,32,64]{2,1,0:T(8,128)} slice(f32[128,48,64]{2,1,0:T(8,128)} %bitcast.158), slice={[0:128], [16:48], [0:64]} | slice | bytes 2097152 | tf_op jit(solution)/shard_map/slice | solution.py:142
  108.3 3.7 %copy.21 = f32[128,32,64]{0,2,1:T(8,128)} copy(f32[128,32,64]{2,1,0:T(8,128)} %slice.73) | data formatting | bytes 2097152 | tf_op jit(solution)/shard_map/slice | solution.py:142
  112.0 2.4 %fusion.12 = f32[64,16,64,1]{2,0,3,1:T(8,128)S(1)} fusion(f32[64,2,16,64]{3,2,1,0:T(8,128)S(1)} %bitcast.155, f32[7,2,64,64]{3,2,1,0:T(8,128)} %param.14), kind=kOutput, calls=%fused_computation.27 | convolution fusion | flops 100663296 | bytes 851968 | tf_op jit(solution)/shard_map/nsrj,sjk->nrk/dot_general | solution.py:153
  115.2 1.4 fusion.14
  119.0 1.3 fusion.17
  120.3 1.1 fusion.23
  121.4 1.1 fusion.21
  122.5 1.1 convolution_bitcast_fusion.1
  125.4 0.9 convolution_add_fusion.6
  129.1 0.9 convolution_add_fusion.4
  130.9 0.9 convolution_add_fusion.3
  134.8 5.0 %convolution_bitcast_fusion = f32[64,16,64]{2,1,0:T(8,128)S(1)} fusion(f32[16,64,1]{1,0,2:T(8,128)S(1)} %fusion.11, f32[64,64,64]{2,1,0:T(8,128)S(1)} %copy-done), kind=kOutput, calls=%fused_computation.14 | convolution fusion | flops 50331648 | bytes 1314816 | tf_op jit(solution)/shard_map/rk,bjk->brj/dot_general | solution.py:185
  139.7 1.5 all-to-all-done
  141.2 3.4 %shard_map.110 = f32[64,1024]{1,0:T(8,128)} custom-call(s32[1,2048]{1,0:T(1,128)} %sub.19.boxes_ref, bf16[2048,1024]{1,0:T(8,128)(2,1)} %bitcast.63.values_ref), custom_call_target="tpu_custom_call" | custom-call | flops 268435456 | bytes 4464640 | tf_op jit(solution)/shard_map/pallas_call | solution.py:32
  144.6 1.1 reshape.117
  145.7 2.6 %convolution_add_fusion = f32[64,16,128]{2,1,0:T(8,128)} fusion(f32[64,16,128]{2,1,0:T(8,128)} %fusion.6, bf16[64,64,128]{2,1,0:T(8,128)(2,1)} %param.12, f32[64,16,64]{2,1,0:T(8,128)S(1)} %convolution_bitcast_fusion, f32[64,16,64]{2,1,0:T(8,128)S(1)} %reshape.117), kind=kOutput, calls=%fused_computation.13 | convolution fusion | flops 17039360 | bytes 2621440 | tf_op jit(solution)/shard_map/brk,bkp->brp/dot_general | solution.py:195
  (50 shorter events, 15.6 us)
Async XLA Ops:
  6.5 12.6 %copy-start = (f32[64,64,64]{2,1,0:T(8,128)S(1)}, f32[64,64,64]{2,1,0:T(8,128)}, u32[]{:S(2)}) copy-start(f32[64,64,64]{2,1,0:T(8,128)} %param.13) | copy-start | bytes 3145732
  6.5 11.2 %copy-start.4 = (bf16[64,16,128]{2,1,0:T(8,128)(2,1)S(1)}, bf16[64,16,128]{2,1,0:T(8,128)(2,1)}, u32[]{:S(2)}) copy-start(bf16[64,16,128]{2,1,0:T(8,128)(2,1)} %param.11) | copy-start | bytes 786436
  6.5 11.2 %copy-start.1 = (bf16[64,64,128]{2,1,0:T(8,128)(2,1)S(1)}, bf16[64,64,128]{2,1,0:T(8,128)(2,1)}, u32[]{:S(2)}) copy-start(bf16[64,64,128]{2,1,0:T(8,128)(2,1)} %param.12) | copy-start | bytes 3145732
  6.5 97.3 %all-gather.3.cloned.1.call-start = ((), (), s32[]{:S(2)}) async-start(), calls=%async_computation.1 | async-start | bytes 3170304 | tf_op jit(solution)/shard_map/all_gather | solution.py:136
  6.5 83.9 %collective-permute-start.1 = (bf16[64,16,128]{2,1,0:T(8,128)(2,1)}, bf16[64,16,128]{2,1,0:T(8,128)(2,1)}, u32[]{:S(2)}, u32[]{:S(2)}) collective-permute-start(bf16[64,16,128]{2,1,0:T(8,128)(2,1)} %param.11), channel_id=1, source_target_pairs={{1,0},{2,1},{3,2},{4,3},{5,4},{6,5},{7,6},{8,7},{9,8},{10,9},{11,1... | collective-permute-start | bytes 786440 | tf_op jit(solution)/shard_map/ppermute | solution.py:17
  10.1 80.4 %collective-permute-start = (bf16[64,16,128]{2,1,0:T(8,128)(2,1)}, bf16[64,16,128]{2,1,0:T(8,128)(2,1)}, u32[]{:S(2)}, u32[]{:S(2)}) collective-permute-start(bf16[64,16,128]{2,1,0:T(8,128)(2,1)} %param.11), channel_id=1, source_target_pairs={{0,1},{1,2},{2,3},{3,4},{4,5},{5,6},{6,7},{7,8},{8,9},{9,10},{10,1... | collective-permute-start | bytes 786440 | tf_op jit(solution)/shard_map/ppermute | solution.py:16
  74.4 14.2 %copy-start.6 = (s32[64,8]{0,1:T(8,128)S(1)}, s32[64,8]{0,1:T(8,128)}, u32[]{:S(2)}) copy-start(s32[64,8]{0,1:T(8,128)} %param.17) | copy-start | bytes 6148
  74.4 14.4 %copy-start.3 = (f32[7,2,64,64]{3,2,1,0:T(8,128)S(1)}, f32[7,2,64,64]{3,2,1,0:T(8,128)}, u32[]{:S(2)}) copy-start(f32[7,2,64,64]{3,2,1,0:T(8,128)} %param.14) | copy-start | bytes 688132
  74.4 15.3 %copy-start.5 = (f32[7,2,64,64]{3,2,1,0:T(8,128)S(1)}, f32[7,2,64,64]{3,2,1,0:T(8,128)}, u32[]{:S(2)}) copy-start(f32[7,2,64,64]{3,2,1,0:T(8,128)} %param.15) | copy-start | bytes 688132
  74.4 66.8 %all-to-all-start = ((bf16[128,16,1024]{2,1,0:T(8,128)(2,1)}), bf16[128,16,1024]{2,1,0:T(8,128)(2,1)}, u32[]{:S(2)}, u32[]{:S(2)}) async-start(bf16[128,16,1024]{2,1,0:T(8,128)(2,1)} %bitcast.156), calls=%async_computation | async-start | bytes 8388608 | tf_op jit(solution)/shard_map/all_to_all | solution.py:128
  114.4 0.8 copy-start.2
Sparse Core Ops, SparseCore 0:
  21.1 71.5 all-gather.2

commit v8 on v7

--- a/solution.py
+++ b/solution.py
@@ -19,15 +19,17 @@
     return value
 
 
-def scatter_kernel(boxes_ref, values_ref, out_ref):
+def scatter_kernel(boxes_ref, values_ref, base_ref, out_ref):
     table = (
         boxes_ref[...] == lax.broadcasted_iota(jnp.int32, (out_ref.shape[0], boxes_ref.shape[1]), 0)
     ).astype(values_ref.dtype)
-    out_ref[...] = jnp.dot(table, values_ref[...], preferred_element_type=jnp.float32)
-
-
-def scatter_rows(boxes, values, count):
+    total = base_ref[...] + jnp.dot(table, values_ref[...], preferred_element_type=jnp.float32)
+    out_ref[...] = total.astype(out_ref.dtype)
+
+
+def scatter_rows(boxes, values, base):
     slots, width = values.shape
+    count = base.shape[0]
     step = 512
     return pl.pallas_call(
         scatter_kernel,
@@ -35,15 +37,16 @@
         in_specs=[
             pl.BlockSpec((1, slots), lambda i: (0, 0)),
             pl.BlockSpec((slots, step), lambda i: (0, i)),
+            pl.BlockSpec((count, step), lambda i: (0, i)),
         ],
         out_specs=pl.BlockSpec((count, step), lambda i: (0, i)),
-        out_shape=jax.ShapeDtypeStruct((count, width), jnp.float32),
+        out_shape=jax.ShapeDtypeStruct((count, width), jnp.bfloat16),
         cost_estimate=pl.CostEstimate(
             flops=2 * count * slots * width,
-            bytes_accessed=slots * width * 2 + count * width * 4 + slots * 4,
+            bytes_accessed=slots * width * 2 + count * width * 6 + slots * 4,
             transcendentals=0,
         ),
-    )(boxes, values)
+    )(boxes, values, base)
 
 
 def pick_kernel(source_ref, table_ref, out_ref):
@@ -183,15 +186,14 @@
         preferred_element_type=jnp.float32,
     )
     tree_part = jnp.einsum("rk,bjk->brj", local_exp, leaf_up, precision=highest)
+    tree_part = tree_part.reshape(leaf_count, flat_width)
     nearfield, tree_part = lax.optimization_barrier((nearfield, tree_part))
 
-    far = scatter_rows(
+    leaf_local = scatter_rows(
         recv_boxes.reshape(1, devices * rows),
         received.reshape(devices * rows, flat_width),
-        leaf_count,
-    )
-    far = far.reshape(leaf_count, sides_rhs, ranks)
-    leaf_local = (tree_part + far).astype(jnp.bfloat16)
+        tree_part.reshape(leaf_count, flat_width),
+    ).reshape(leaf_count, sides_rhs, ranks)
     farfield = jnp.einsum(
         "brk,bkp->brp", leaf_local, leaf_basis, preferred_element_type=jnp.float32
     )

time: 157 us -> 161 us (1.025)
  local copies, waits for them, and re-layouts: 45.8 us -> 57.3 us
  matrix products: 60.4 us -> 56.7 us
  starting transfers between devices: 20.9 us -> 17.8 us
    reshape x1 -> x3, local copies, waits for them, and re-layouts: 1.08 us -> 8.58 us  [the longest x1 5.55 us: body_inner(): paired = upward.reshape(count // 2, 2, sides_rhs, ranks)]
    dot_general x7, matrix products: 5.71 us -> 1.92 us  [body_inner(): jnp.dot(sibling, lax.dynamic_index_in_dim(top_coupling[level], node_side,...]
    unnamed x15 -> x24, local copies, waits for them, and re-layouts: 24.8 us -> 28.6 us
    all_to_all x1, starting transfers between devices: 14.1 us -> 11 us  [body_inner(): lax.all_to_all(send_values.reshape(devices, rows, flat_width), 'leaf', sp...]
    ppermute x1, starting transfers between devices: 3.21 us -> 4.85 us  [padded_2(): before = lax.ppermute(last, axis, up)]
    ppermute x1, starting transfers between devices: 3.55 us -> 1.92 us  [padded_2(): after = lax.ppermute(initial, axis, down)]
  transfers between devices with their start and end apart: 4 -> 4, of which waited for: 1 -> 0; matrix products, arithmetic and copies ran while one was open for 68% -> 72% of each run, Pallas kernels for 4% -> 4%
where the time goes in v8:
time: 161 us; the launch traced here: 159 us
  local copies, waits for them, and re-layouts  57.3 us (36%)
  matrix products  56.7 us (35%)
  starting transfers between devices  17.8 us (11%)
  between operations  13.7 us (9%)
  Pallas kernels  9.21 us (6%)
  other arithmetic  3.89 us (2%)
    unnamed x24, local copies, waits for them, and re-layouts  28.6 us
    all_to_all x1, starting transfers between devices, body_inner(): lax.all_to_all(send_values.reshape(devices, rows, flat_width), 'leaf', sp...  11 us
    dot_general x1, matrix products, body_inner(): jnp.einsum('crj,cjk->crk', picked, coupling_blocks, preferred_element_typ...  10.7 us
    dot_general x1, matrix products, body_inner(): jnp.einsum('brm,bmp->brp', gathered, near_blocks.reshape(leaf_count, near...  9.51 us
    dot_general x6, matrix products, body_inner(): jnp.einsum('nsrj,sjk->nrk', paired, top_up[level], precision=highest)  7.8 us
    dot_general x1, matrix products, body_inner(): jnp.dot(slot_table, products.reshape(entries, flat_width), preferred_elem...  7.69 us
    slice x2, local copies, waits for them, and re-layouts, body_inner(): gathered[:, sides_rhs:].reshape(devices, devices, rows)  6.87 us
    dot_general x1, matrix products, body_inner(): tree_part = jnp.einsum('rk,bjk->brj', local_exp, leaf_up, precision=highest)  5.84 us
  transfers between devices with their start and end apart: 4, of which 0 were waited for; matrix products, arithmetic and copies ran while one was open for 72% of the time, Pallas kernels for 4%

profile of v8, /device:TPU:1, one launch (start us, length us, event | category | flops | bytes accessed | tf_op | source)
XLA Modules:
  0.0 158.6 jit_solution(17021647925301818220)
XLA Ops:
  6.5 4.8 %collective-permute-start = (bf16[64,16,128]{2,1,0:T(8,128)(2,1)}, bf16[64,16,128]{2,1,0:T(8,128)(2,1)}, u32[]{:S(2)}, u32[]{:S(2)}) collective-permute-start(bf16[64,16,128]{2,1,0:T(8,128)(2,1)} %param.11), channel_id=1, source_target_pairs={{0,1},{1,2},{2,3},{3,4},{4,5},{5,6},{6,7},{7,8},{8,9},{9,10},{10,1... | collective-permute-start | bytes 786440 | tf_op jit(solution)/shard_map/ppermute | solution.py:16
  11.4 1.9 %collective-permute-start.1 = (bf16[64,16,128]{2,1,0:T(8,128)(2,1)}, bf16[64,16,128]{2,1,0:T(8,128)(2,1)}, u32[]{:S(2)}, u32[]{:S(2)}) collective-permute-start(bf16[64,16,128]{2,1,0:T(8,128)(2,1)} %param.11), channel_id=1, source_target_pairs={{1,0},{2,1},{3,2},{4,3},{5,4},{6,5},{7,6},{8,7},{9,8},{10,9},{11,1... | collective-permute-start | bytes 786440 | tf_op jit(solution)/shard_map/ppermute | solution.py:17
  14.1 1.4 fusion.10
  16.2 1.5 fusion.1
  17.8 1.4 fusion.94
  19.1 1.2 convolution_bitcast_fusion.2
  21.0 24.0 %copy.40 = bf16[1024,64,64]{2,1,0:T(8,128)(2,1)} copy(bf16[1024,64,64]{0,2,1:T(8,128)(2,1)} %param.18) | data formatting | bytes 16777216 | tf_op args[7]
  45.0 5.6 %shard_map.109 = bf16[1024,16,64]{2,1,0:T(8,128)(2,1)} custom-call(s32[1024]{0:T(1024)} %source_ref.1, bf16[64,16,64]{2,1,0:T(8,128)(2,1)} %get-tuple-element.23.table_ref), custom_call_target="tpu_custom_call" | custom-call | tf_op jit(solution)/shard_map/pallas_call | solution.py:62
  50.5 10.7 %convolution_convert_fusion = bf16[1024,16,64]{2,1,0:T(8,128)(2,1)} fusion(bf16[1024,16,64]{2,1,0:T(8,128)(2,1)} %shard_map.109, bf16[1024,64,64]{2,1,0:T(8,128)(2,1)} %copy.40), kind=kOutput, calls=%fused_computation.9 | convolution fusion | flops 135266304 | bytes 12582912 | tf_op jit(solution)/shard_map/crj,cjk->crk/dot_general | solution.py:125
  61.2 5.5 %copy.41 = bf16[1024,16,64]{0,2,1:T(8,128)(2,1)} copy(bf16[1024,16,64]{2,1,0:T(8,128)(2,1)} %convolution_convert_fusion) | data formatting | bytes 4194304 | tf_op jit(solution)/shard_map/convert_element_type | solution.py:127
  66.7 7.7 %fusion.5 = bf16[2048,1024]{1,0:T(8,128)(2,1)} fusion(bf16[1024,1024]{0,1:T(8,128)(2,1)} %bitcast.163, s32[1024]{0:T(1024)S(1)} %convert_add_fusion.1), kind=kOutput, calls=%fused_computation.8 | convolution fusion | flops 4299161600 | bytes 6295552 | tf_op jit(solution)/shard_map/dot_general | solution.py:128
  74.4 11.0 %all-to-all-start = ((bf16[128,16,1024]{2,1,0:T(8,128)(2,1)}), bf16[128,16,1024]{2,1,0:T(8,128)(2,1)}, u32[]{:S(2)}, u32[]{:S(2)}) async-start(bf16[128,16,1024]{2,1,0:T(8,128)(2,1)} %bitcast.158), calls=%async_computation | async-start | bytes 8388608 | tf_op jit(solution)/shard_map/all_to_all | solution.py:131
  87.5 1.1 pad_maximum_fusion
  88.6 2.8 %gather_fusion = bf16[512,16,128]{2,1,0:T(8,128)(2,1)} fusion(bf16[192,16,128]{2,1,0:T(8,128)(2,1)S(1)} %pad_maximum_fusion, s32[1024]{0:T(1024)S(1)} %pad_clamp_fusion), kind=kCustom, calls=%fused_computation | custom fusion | bytes 4196352 | tf_op jit(solution)/shard_map/gather | solution.py:178
  91.4 9.5 %fusion.6 = f32[64,16,128]{2,1,0:T(8,128)} fusion(bf16[64,1024,128]{2,1,0:T(8,128)(2,1)} %bitcast.155, bf16[64,8,2,8,128]{4,3,2,1,0:T(8,128)(2,1)} %bitcast.157), kind=kOutput, calls=%fused_computation.10 | convolution fusion | flops 268435456 | bytes 19398656 | tf_op jit(solution)/shard_map/brm,bmp->brp/dot_general | solution.py:182
  100.9 1.3 slice.73
  102.3 3.2 %slice.72 = f32[128,32,64]{2,1,0:T(8,128)} slice(f32[128,48,64]{2,1,0:T(8,128)} %bitcast.160), slice={[0:128], [16:48], [0:64]} | slice | bytes 2097152 | tf_op jit(solution)/shard_map/slice | solution.py:145
  105.4 3.7 %copy.38 = f32[128,32,64]{0,2,1:T(8,128)} copy(f32[128,32,64]{2,1,0:T(8,128)} %slice.72) | data formatting | bytes 2097152 | tf_op jit(solution)/shard_map/slice | solution.py:145
  109.1 4.5 %copy.59 = f32[128,16,64]{1,0,2:T(8,128)} copy(f32[128,16,64]{2,1,0:T(8,128)S(1)} %slice.73) | data formatting | bytes 1048576
  113.6 5.6 %copy.45 = f32[64,2,16,64]{3,0,1,2:T(8,128)S(1)} copy(f32[64,2,16,64]{2,1,0,3:T(2,128)} %bitcast.156) | data formatting | bytes 1048576 | tf_op jit(solution)/shard_map/reshape | solution.py:155
  119.2 1.8 %fusion.25 = f32[64,16,64,1]{2,0,3,1:T(8,128)S(1)} fusion(f32[64,2,16,64]{3,0,1,2:T(8,128)S(1)} %copy.45, f32[7,2,64,64]{3,2,1,0:T(8,128)} %param.14), kind=kOutput, calls=%fused_computation.42 | convolution fusion | flops 100663296 | bytes 851968 | tf_op jit(solution)/shard_map/nsrj,sjk->nrk/dot_general | solution.py:156
  121.0 1.4 fusion.12
  125.0 1.3 fusion.15
  126.3 1.1 fusion.21
  127.4 1.1 fusion.19
  128.5 1.1 convolution_bitcast_fusion.1
  136.1 1.0 fusion.11
  137.1 5.8 %convolution_bitcast_fusion = f32[64,16,64]{2,1,0:T(8,128)} fusion(f32[16,64,1]{1,0,2:T(8,128)S(1)} %fusion.11, f32[64,64,64]{2,1,0:T(8,128)S(1)} %copy-done), kind=kOutput, calls=%fused_computation.14 | convolution fusion | flops 50331648 | bytes 1314816 | tf_op jit(solution)/shard_map/rk,bjk->brj/dot_general | solution.py:188
  142.9 1.9 %reshape.120.base_ref = f32[64,1024]{1,0:T(8,128)} reshape(f32[64,16,64]{2,1,0:T(8,128)} %convolution_bitcast_fusion) | data formatting | bytes 524288 | tf_op jit(solution)/shard_map/reshape | solution.py:189
  144.8 3.6 %shard_map.110 = bf16[64,1024]{1,0:T(8,128)(2,1)} custom-call(s32[1,2048]{1,0:T(1,128)} %sub.16.boxes_ref, bf16[2048,1024]{1,0:T(8,128)(2,1)} %bitcast.7.values_ref, f32[64,1024]{1,0:T(8,128)} %reshape.120.base_ref), custom_call_target="tpu_custom_call" | custom-call | flops 268435456 | bytes 4595712 | tf_op jit(solution)/shard_map/pallas_call | solution.py:34
  148.4 1.1 reshape.121
  149.6 2.2 %convolution_add_fusion = f32[64,16,128]{2,1,0:T(8,128)} fusion(f32[64,16,128]{2,1,0:T(8,128)} %fusion.6, bf16[64,16,64]{2,1,0:T(8,128)(2,1)S(1)} %reshape.121, bf16[64,64,128]{2,1,0:T(8,128)(2,1)S(1)} %copy-done.2), kind=kOutput, calls=%fused_computation.13 | convolution fusion | flops 16908288 | bytes 2228224 | tf_op jit(solution)/shard_map/brk,bkp->brp/dot_general | solution.py:197
  (62 shorter events, 13.1 us)
Async XLA Ops:
  6.5 12.6 %copy-start = (f32[64,64,64]{2,1,0:T(8,128)S(1)}, f32[64,64,64]{2,1,0:T(8,128)}, u32[]{:S(2)}) copy-start(f32[64,64,64]{2,1,0:T(8,128)} %param.13) | copy-start | bytes 3145732
  6.5 11.2 %copy-start.4 = (bf16[64,16,128]{2,1,0:T(8,128)(2,1)S(1)}, bf16[64,16,128]{2,1,0:T(8,128)(2,1)}, u32[]{:S(2)}) copy-start(bf16[64,16,128]{2,1,0:T(8,128)(2,1)} %param.11) | copy-start | bytes 786436
  6.5 11.2 %copy-start.1 = (bf16[64,64,128]{2,1,0:T(8,128)(2,1)S(1)}, bf16[64,64,128]{2,1,0:T(8,128)(2,1)}, u32[]{:S(2)}) copy-start(bf16[64,64,128]{2,1,0:T(8,128)(2,1)} %param.12) | copy-start | bytes 3145732
  6.5 94.4 %all-gather.3.cloned.1.call-start = ((), (), s32[]{:S(2)}) async-start(), calls=%async_computation.1 | async-start | bytes 3170304 | tf_op jit(solution)/shard_map/all_gather | solution.py:139
  6.5 81.0 %collective-permute-start = (bf16[64,16,128]{2,1,0:T(8,128)(2,1)}, bf16[64,16,128]{2,1,0:T(8,128)(2,1)}, u32[]{:S(2)}, u32[]{:S(2)}) collective-permute-start(bf16[64,16,128]{2,1,0:T(8,128)(2,1)} %param.11), channel_id=1, source_target_pairs={{0,1},{1,2},{2,3},{3,4},{4,5},{5,6},{6,7},{7,8},{8,9},{9,10},{10,1... | collective-permute-start | bytes 786440 | tf_op jit(solution)/shard_map/ppermute | solution.py:16
  11.4 76.1 %collective-permute-start.1 = (bf16[64,16,128]{2,1,0:T(8,128)(2,1)}, bf16[64,16,128]{2,1,0:T(8,128)(2,1)}, u32[]{:S(2)}, u32[]{:S(2)}) collective-permute-start(bf16[64,16,128]{2,1,0:T(8,128)(2,1)} %param.11), channel_id=1, source_target_pairs={{1,0},{2,1},{3,2},{4,3},{5,4},{6,5},{7,6},{8,7},{9,8},{10,9},{11,1... | collective-permute-start | bytes 786440 | tf_op jit(solution)/shard_map/ppermute | solution.py:17
  74.4 11.1 %copy-start.10 = (s32[64,8]{0,1:T(8,128)S(1)}, s32[64,8]{0,1:T(8,128)}, u32[]{:S(2)}) copy-start(s32[64,8]{0,1:T(8,128)} %param.17) | copy-start | bytes 6148
  74.4 11.3 %copy-start.3 = (f32[7,2,64,64]{3,2,1,0:T(8,128)S(1)}, f32[7,2,64,64]{3,2,1,0:T(8,128)}, u32[]{:S(2)}) copy-start(f32[7,2,64,64]{3,2,1,0:T(8,128)} %param.14) | copy-start | bytes 688132
  74.4 12.3 %copy-start.5 = (f32[7,2,64,64]{3,2,1,0:T(8,128)S(1)}, f32[7,2,64,64]{3,2,1,0:T(8,128)}, u32[]{:S(2)}) copy-start(f32[7,2,64,64]{3,2,1,0:T(8,128)} %param.15) | copy-start | bytes 688132
  74.4 70.4 %all-to-all-start = ((bf16[128,16,1024]{2,1,0:T(8,128)(2,1)}), bf16[128,16,1024]{2,1,0:T(8,128)(2,1)}, u32[]{:S(2)}, u32[]{:S(2)}) async-start(bf16[128,16,1024]{2,1,0:T(8,128)(2,1)} %bitcast.158), calls=%async_computation | async-start | bytes 8388608 | tf_op jit(solution)/shard_map/all_to_all | solution.py:131
  113.6 16.0 %copy-start.9 = (f32[1,2,64,64]{3,2,1,0:T(8,128)S(1)}, f32[1,2,64,64]{3,2,1,0:T(8,128)}, u32[]{:S(2)}) copy-start(f32[1,2,64,64]{3,2,1,0:T(8,128)} %get-tuple-element.14) | copy-start | bytes 98308
  113.6 17.0 %copy-start.8 = (f32[1,2,64,64]{3,2,1,0:T(8,128)S(1)}, f32[1,2,64,64]{3,2,1,0:T(8,128)}, u32[]{:S(2)}) copy-start(f32[1,2,64,64]{3,2,1,0:T(8,128)} %get-tuple-element.13) | copy-start | bytes 98308
  113.6 18.1 %copy-start.7 = (f32[1,2,64,64]{3,2,1,0:T(8,128)S(1)}, f32[1,2,64,64]{3,2,1,0:T(8,128)}, u32[]{:S(2)}) copy-start(f32[1,2,64,64]{3,2,1,0:T(8,128)} %get-tuple-element.12) | copy-start | bytes 98308
  113.6 19.2 %copy-start.6 = (f32[1,2,64,64]{3,2,1,0:T(8,128)S(1)}, f32[1,2,64,64]{3,2,1,0:T(8,128)}, u32[]{:S(2)}) copy-start(f32[1,2,64,64]{3,2,1,0:T(8,128)} %get-tuple-element.11) | copy-start | bytes 98308
  137.0 12.5 %copy-start.2 = (bf16[64,64,128]{2,1,0:T(8,128)(2,1)S(1)}, bf16[64,64,128]{2,1,0:T(8,128)(2,1)}, u32[]{:S(2)}) copy-start(bf16[64,64,128]{2,1,0:T(8,128)(2,1)} %param.12) | copy-start | bytes 3145732
Sparse Core Ops, SparseCore 0:
  21.1 68.4 all-gather.2
